TPU v7x, 128 devices: a whole 4x4x4 slice. The times are simulated.
128 devices in a mesh: dp: 8 (over z, core), ts: 16 (over y, x).
Axes of the slice: x: 4, y: 4, z: 4, core: 2. Of those that a mesh axis runs over, the one named last changes fastest.
Arguments:
- text_embed: bfloat16 [8, 1024, 4096], P('dp', None, 'ts'), may hold values from -6 to 6
- bridge: bfloat16 [128, 32, 4096], P('dp', None, 'ts'), may hold values from -6 to 6
- crystal_slot: int32 [128], P('dp'), may hold values from 0 to 8159, as said below
- segments: int32 [8, 1024], P('dp'), may hold values from 0 to 15, as said below
- attn_gain: float32 [4096], replicated, may hold values from 0.1 to 1.9
- w_query: bfloat16 [4096, 4096], P(None, 'ts'), as said below
- w_key: bfloat16 [4096, 1024], P(None, 'ts'), may hold values from -0.09375 to 0.09375
- w_value: bfloat16 [4096, 1024], P(None, 'ts'), may hold values from -0.09375 to 0.09375
- w_out: bfloat16 [4096, 4096], P('ts'), may hold values from -0.09375 to 0.09375
- mlp_gain: float32 [4096], replicated, may hold values from 0.1 to 1.9
- w_gate: bfloat16 [4096, 12288], P(None, 'ts'), may hold values from -0.09375 to 0.09375
- w_up: bfloat16 [4096, 12288], P(None, 'ts'), may hold values from -0.09375 to 0.09375
- w_down: bfloat16 [12288, 4096], P('ts'), may hold values from -0.0546875 to 0.0546875
Outputs:
- layer_out: bfloat16 [8, 1024, 4096], P('dp', 'ts')
Inputs may be any that keep to these rules, and one draw needn't show every extreme that they name: `segments`: each row starts at 0, never falls and names every document number of 0 to 15; every document holds at least 33 positions. `crystal_slot`: each crystal's 32 rows take the first 32 positions of one document, given as sequence * 1024 + that document's first position; every document takes exactly one crystal, and each sequence takes exactly 2 of the 16 crystals held by each index of dp. `w_query`: entries lie within plus or minus 104 / sqrt(4096).
All inputs are finite; a program needn't handle non-finite values.
Results may differ from a plain program's by a relative error of at most 0.025.
The roundings to bfloat16 on the way count: a program that leaves them out, or rounds other values in their place, can miss the bound.
Values may be sent and summed in bfloat16 or wider, within the bound.
No kernel may reach another device: no remote copies, remote signals or barrier semaphores. Data moves between devices by JAX's collectives and lax.ppermute only.
A program may use at most 128 MiB of HBM per device.

v0:
```python
import jax
import jax.numpy as jnp
from jax import lax
from jax.sharding import PartitionSpec as P

HD = 128
DOC_LEN = 64


norm_epsilon = 1e-05
rope_base = 500000.0
masked_score = -1e30


def partner_2(block, axis, apart):
    count = lax.axis_size(axis)
    route = []
    for low in range(count):
        high = low | 1 << apart
        if high != low and high < count:
            route += [(low, high), (high, low)]
    return lax.ppermute(block, axis, route)


def norm_rows(rows, gain):
    widened = rows.astype(jnp.float32)
    inverse_rms = lax.rsqrt(jnp.mean(widened * widened, axis=-1, keepdims=True) + norm_epsilon)
    return (widened * inverse_rms * gain).astype(jnp.bfloat16)


def rotate_pairs(values, positions, first_pair):
    pair_count = values.shape[-1] // 2
    exponent = 2.0 * (first_pair + jnp.arange(pair_count, dtype=jnp.int32)).astype(jnp.float32) / HD
    frequency = rope_base ** (-exponent)
    angles = positions.astype(jnp.float32)[:, None] * frequency[None, :]
    cosine = jnp.cos(angles)[:, None, :]
    sine_part = jnp.sin(angles)[:, None, :]
    paired = values.reshape(values.shape[0], values.shape[1], pair_count, 2)
    even_part = paired[..., 0]
    odd_part = paired[..., 1]
    new_even = even_part * cosine - odd_part * sine_part
    new_odd = even_part * sine_part + odd_part * cosine
    return jnp.stack([new_even, new_odd], axis=-1).reshape(values.shape)


def attend_block(query_block, query_segments, query_index, keys_full, values_full, segment_ids):
    scores = jnp.einsum(
        "qhd,kd->hqk", query_block, keys_full, preferred_element_type=jnp.float32
    ) * HD ** (-0.5)
    key_index = jnp.arange(keys_full.shape[0], dtype=jnp.int32)
    allowed = (query_segments[:, None] == segment_ids[None, :]) & (
        key_index[None, :] <= query_index[:, None]
    )
    scores = jnp.where(allowed[None], scores, masked_score)
    row_top = jnp.max(scores, axis=-1, keepdims=True)
    weights = jnp.exp(scores - row_top)
    probabilities = (weights / jnp.sum(weights, axis=-1, keepdims=True)).astype(jnp.bfloat16)
    mixed_rows = jnp.einsum(
        "hqk,kd->qhd", probabilities, values_full, preferred_element_type=jnp.float32
    )
    return mixed_rows.astype(jnp.bfloat16).reshape(query_block.shape[0], -1)


def shards(
    text_embed,
    bridge,
    crystal_slot,
    segments,
    attn_gain,
    w_query,
    w_key,
    w_value,
    w_out,
    mlp_gain,
    w_gate,
    w_up,
    w_down,
):
    seq_len = text_embed.shape[1]
    part_width = text_embed.shape[2]
    doc_count = seq_len // DOC_LEN
    bridge_len = bridge.shape[1]
    tok_rows = seq_len // lax.axis_size("ts")
    group_index = lax.axis_index("dp")
    ts_index = lax.axis_index("ts")
    segment_ids = segments[0]
    doc_numbers = jnp.arange(doc_count, dtype=jnp.int32)
    starts = jnp.sum((segment_ids[None, :] < doc_numbers[:, None]).astype(jnp.int32), axis=1)
    doc_match = segment_ids[:, None] == doc_numbers[None, :]
    positions = jnp.arange(seq_len, dtype=jnp.int32) - jnp.sum(
        jnp.where(doc_match, starts[None, :], 0), axis=1
    )
    flat_bridge = bridge.reshape(bridge.shape[0], bridge_len * part_width)
    arrived, arrived_slots = (
        lax.all_gather(flat_bridge, "dp", axis=0, tiled=True),
        lax.all_gather(crystal_slot, "dp", axis=0, tiled=True),
    )
    wanted = group_index * seq_len + starts
    picking = wanted[:, None] == arrived_slots[None, :]
    by_doc = jnp.dot(
        picking.astype(jnp.bfloat16), arrived, preferred_element_type=jnp.float32
    ).astype(jnp.bfloat16)
    by_doc = by_doc.reshape(doc_count * bridge_len, part_width)
    in_bridge = positions < bridge_len
    row_pick = (segment_ids * bridge_len + positions)[:, None] == jnp.arange(
        doc_count * bridge_len, dtype=jnp.int32
    )[None, :]
    row_pick = row_pick & in_bridge[:, None]
    filled = jnp.dot(
        row_pick.astype(jnp.bfloat16), by_doc, preferred_element_type=jnp.float32
    ).astype(jnp.bfloat16)
    own_part = jnp.where(in_bridge[:, None], filled, text_embed[0])
    packed = lax.all_gather(own_part, "ts", axis=1, tiled=True)
    normed = norm_rows(packed, attn_gain)
    heads_here = w_query.shape[1] // HD
    queries = jnp.dot(normed, w_query, preferred_element_type=jnp.float32).reshape(
        seq_len, heads_here, HD
    )
    queries = rotate_pairs(queries, positions, 0).astype(jnp.bfloat16)
    kv_cols = w_key.shape[1]
    upper_half = ts_index % 2 == 1
    key_half = jnp.dot(normed, w_key, preferred_element_type=jnp.float32).reshape(
        seq_len, 1, kv_cols
    )
    key_half = rotate_pairs(key_half, positions, ts_index % 2 * (kv_cols // 2))
    key_half = key_half.astype(jnp.bfloat16).reshape(seq_len, kv_cols)
    value_half = jnp.dot(normed, w_value, preferred_element_type=jnp.float32).astype(jnp.bfloat16)
    own_pair = jnp.concatenate([key_half, value_half], axis=1)
    partner = partner_2(own_pair, "ts", 0)
    lower_half = jnp.where(upper_half, partner, own_pair)
    higher = jnp.where(upper_half, own_pair, partner)
    keys_full = jnp.concatenate([lower_half[:, :kv_cols], higher[:, :kv_cols]], axis=1)
    values_full = jnp.concatenate([lower_half[:, kv_cols:], higher[:, kv_cols:]], axis=1)
    block_rows = min(512, seq_len)
    outputs = []
    for block_index in range(seq_len // block_rows):
        first_row = block_index * block_rows
        query_index = jnp.arange(first_row, first_row + block_rows, dtype=jnp.int32)
        outputs.append(
            attend_block(
                queries[first_row : first_row + block_rows],
                segment_ids[first_row : first_row + block_rows],
                query_index,
                keys_full,
                values_full,
                segment_ids,
            )
        )
    attended = jnp.concatenate(outputs, axis=0)
    mine_offset = ts_index * tok_rows
    partial_rows = jnp.dot(attended, w_out, preferred_element_type=jnp.float32)
    attn_sum = lax.psum(partial_rows.astype(jnp.bfloat16), "ts").astype(jnp.float32)
    after_all = (packed.astype(jnp.float32) + attn_sum).astype(jnp.bfloat16)
    after_mine = lax.dynamic_slice_in_dim(after_all, mine_offset, tok_rows, 0)
    normed_mlp = norm_rows(after_all, mlp_gain)
    gate_proj = jnp.dot(normed_mlp, w_gate, preferred_element_type=jnp.float32)
    up_proj = jnp.dot(normed_mlp, w_up, preferred_element_type=jnp.float32)
    hidden = (jax.nn.silu(gate_proj) * up_proj).astype(jnp.bfloat16)
    mlp_mine = lax.psum_scatter(
        jnp.dot(hidden, w_down, preferred_element_type=jnp.float32).astype(jnp.bfloat16),
        "ts",
        scatter_dimension=0,
        tiled=True,
    ).astype(jnp.float32)
    layer_rows = (after_mine.astype(jnp.float32) + mlp_mine).astype(jnp.bfloat16)
    return layer_rows.reshape(1, tok_rows, layer_rows.shape[1])


def solution(mesh):
    return jax.shard_map(
        shards,
        mesh=mesh,
        in_specs=(
            P("dp", None, "ts"),
            P("dp", None, "ts"),
            P("dp"),
            P("dp", None),
            P(),
            P(None, "ts"),
            P(None, "ts"),
            P(None, "ts"),
            P("ts", None),
            P(),
            P(None, "ts"),
            P(None, "ts"),
            P("ts", None),
        ),
        out_specs=P("dp", "ts", None),
        check_vma=False,
    )
```

profile of v0, /device:TPU:0, one launch (start us, length us, event | category | flops | bytes accessed | tf_op | source)
XLA Modules:
  0.0 462.7 jit_solution(8637387790045024165)
XLA Ops:
  6.5 2.0 copy.65
  8.5 0.0 all-gather.3.cloned.1.call-update
  8.5 0.0 all-gather.5.cloned.1.call-start
  8.6 1.3 dynamic-slice
  10.6 0.9 dynamic-update-slice
  11.4 10.6 %all-reduce = s32[128]{0:T(128)S(1)} all-reduce(s32[128]{0:T(128)S(1)} %dynamic-update-slice), channel_id=1, replica_groups=mesh['dp'=8,'ts'=16] {'dp'}, use_global_device_ids=true, to_apply=%add | all-reduce | flops 128 | bytes 1024
  22.0 0.8 convert_reduce_fusion
  22.8 0.8 select_reduce_fusion
  23.6 0.7 fusion.77
  24.3 12.6 %all-gather.3.cloned.1.call-done = bf16[128,8192]{1,0:T(8,128)(2,1)} async-done(((bf16[16,8192]{1,0:T(8,128)(2,1)}), bf16[128,8192]{1,0:T(8,128)(2,1)}) %all-gather.3.cloned.1.call-update) | async-done | bytes 2097168 | tf_op jit(solution)/shard_map/all_gather | solution.py:95
  37.0 2.0 convolution_convert_fusion
  39.0 0.1 reshape.345
  39.1 2.7 fusion.36
  41.9 0.0 all-reduce.3.cloned.1.call-start
  42.0 2.3 multiply_cosine_fusion
  44.3 1.6 fusion.22
  45.9 74.7 %all-gather.5.cloned.1.call-done = bf16[1024,4096]{1,0:T(8,128)(2,1)} async-done(((bf16[1024,256]{1,0:T(8,128)(2,1)}), bf16[1024,4096]{1,0:T(8,128)(2,1)}) %all-gather.5.cloned.1.call-update) | async-done | bytes 8388624 | tf_op jit(solution)/shard_map/all_gather | solution.py:113
  120.6 5.1 %fusion.5 = f32[1024]{0:T(1024)S(1)} fusion(bf16[1024,4096]{1,0:T(8,128)(2,1)} %all-gather.5.cloned.1.call-done), kind=kLoop, calls=%fused_computation.10 | loop fusion | flops 12581888 | bytes 8392704 | tf_op jit(solution)/shard_map/reduce_sum | solution.py:27
  125.7 10.4 %fusion.7 = bf16[1024,4096]{1,0:T(8,128)(2,1)} fusion(bf16[1024,4096]{1,0:T(8,128)(2,1)} %all-gather.5.cloned.1.call-done, f32[4096]{0:T(1024)S(1)} %copy-done.8, f32[1024]{0:T(1024)S(1)} %add_rsqrt_fusion.1), kind=kLoop, calls=%fused_computation.12 | loop fusion | flops 16777216 | bytes 16797696 | tf_op jit(solution)/shard_map/convert_element_type | solution.py:28
  136.1 6.2 %convolution_convert_fusion.3 = bf16[1024,64]{0,1:T(8,128)(2,1)S(1)} fusion(bf16[1024,4096]{1,0:T(8,128)(2,1)} %fusion.7, bf16[4096,64]{0,1:T(8,128)(2,1)S(1)} %copy-done.4), kind=kOutput, calls=%fused_computation.48 | convolution fusion | flops 536936448 | bytes 9043968 | tf_op jit(solution)/shard_map/dot_general | solution.py:127
  142.4 2.7 fusion.103
  145.0 3.6 fusion.104
  148.7 1.8 reshape_reshape.7
  150.5 0.9 reshape_reshape.6
  151.4 1.3 fusion.91
  152.6 0.6 fusion.71
  153.2 0.1 copy.46
  153.4 0.1 convert_element_type.107
  153.4 0.8 fusion.88
  154.3 1.3 collective-permute-start
  155.5 2.1 subtract_convert_fusion
  157.6 1.2 fusion.51
  158.9 2.7 collective-permute-done
  161.5 0.1 broadcast_select_fusion.1
  161.7 4.8 %fusion.98 = (f32[2,512]{1,0:T(2,128)S(1)}, f32[2,512,1024]{1,2,0:T(8,128)}) fusion(pred[512,1024]{0,1:T(8,128)(4,1)} %get-tuple-element.25, bf16[512,2,128]{0,1,2:T(2,128)(2,1)} %bitcast.86, bf16[1024,64]{0,1:T(8,128)(2,1)S(1)} %get-tuple-element.35, bf16[1024,64]{0,1:T(8,128)(2,1)S(1)} %get-tuple-element.18), kind=kOutput, calls=%fused_computation.119 | convolution fusion | flops 273155072 | bytes 5246976 | tf_op jit(solution)/shard_map/sub | solution.py:56
  166.5 3.7 fusion.93
  170.2 2.8 fusion.40
  173.0 0.7 copy-done.11
  173.7 0.5 fusion.39
  174.2 5.6 %convolution_convert_fusion.2 = bf16[1024,4096]{1,0:T(8,128)(2,1)} fusion(bf16[256,4096]{1,0:T(8,128)(2,1)S(1)} %copy-done, bf16[512,256]{0,1:T(8,128)(2,1)S(1)} %bitcast.83, bf16[512,256]{0,1:T(8,128)(2,1)S(1)} %bitcast.82), kind=kOutput, calls=%fused_computation.16 | convolution fusion | flops 2152726528 | bytes 11010048 | tf_op jit(solution)/shard_map/dot_general | solution.py:151
  179.8 0.0 reduce-scatter.2.cloned.1.call-start
  179.8 140.8 %all-reduce.3.cloned.1.call-done = bf16[1024,4096]{1,0:T(8,128)(2,1)} async-done(((bf16[1024,4096]{1,0:T(8,128)(2,1)}), bf16[1024,4096]{1,0:T(8,128)(2,1)}) %all-reduce.3.cloned.1.call-update) | async-done | bytes 8388624 | tf_op jit(solution)/shard_map/psum | solution.py:152
  320.6 8.0 %fusion.2 = (f32[1024]{0:T(1024)S(1)}, bf16[1024,4096]{1,0:T(8,128)(2,1)S(1)}) fusion(bf16[1024,4096]{1,0:T(8,128)(2,1)} %all-reduce.3.cloned.1.call-done, bf16[1024,4096]{1,0:T(8,128)(2,1)} %all-gather.5.cloned.1.call-done), kind=kLoop, calls=%fused_computation.7 | loop fusion | flops 29359104 | bytes 25169920 | tf_op jit(solution)/shard_map/reduce_sum | solution.py:27
  328.7 3.2 copy-done.3
  331.9 11.3 %fusion.11 = f32[1024,768]{1,0:T(8,128)} fusion(bf16[4096,768]{1,0:T(8,128)(2,1)} %param.24, bf16[1024,4096]{1,0:T(8,128)(2,1)S(1)} %get-tuple-element.6, f32[4096]{0:T(1024)S(1)} %copy-done.10, f32[1024]{0:T(1024)S(1)} %add_rsqrt_fusion), kind=kOutput, calls=%fused_computation.26 | convolution fusion | flops 6459228160 | bytes 17846272 | tf_op jit(solution)/shard_map/dot_general | solution.py:157
  343.2 26.4 %convolution_convert_fusion.1 = bf16[1024,4096]{1,0:T(8,128)(2,1)} fusion(bf16[768,4096]{1,0:T(8,128)(2,1)} %param.25, f32[1024,768]{1,0:T(8,128)} %fusion.11, bf16[4096,768]{1,0:T(8,128)(2,1)} %param.23, bf16[1024,4096]{1,0:T(8,128)(2,1)} %copy-done.3, f32[4096]{0:T(1024)S(1)} %copy-done.10, f32[1024]{0:T(1024)S(1)} %add_rsqrt_fusion), kind=kOutput, calls=%fused_computation.15 | convolution fusion | flops 12910592000 | bytes 32526336 | tf_op jit(solution)/shard_map/dot_general | solution.py:160
  369.6 84.2 %reduce-scatter.2.cloned.1.call-done = bf16[64,4096]{1,0:T(8,128)(2,1)} async-done(((bf16[1024,4096]{1,0:T(8,128)(2,1)}), bf16[64,4096]{1,0:T(8,128)(2,1)}) %reduce-scatter.2.cloned.1.call-update) | async-done | bytes 524304 | tf_op jit(solution)/shard_map/reduce_scatter | solution.py:159
  453.8 2.1 fusion.43
  (38 shorter events, 0.2 us)
Async XLA Ops:
  6.5 167.6 %copy-start = (bf16[256,4096]{1,0:T(8,128)(2,1)S(1)}, bf16[256,4096]{1,0:T(8,128)(2,1)}, u32[]{:S(2)}) copy-start(bf16[256,4096]{1,0:T(8,128)(2,1)} %param.21) | copy-start | bytes 6291460
  6.5 35.4 %copy-start.7 = (s32[1,1024]{1,0:T(1,128)S(1)}, s32[1,1024]{1,0:T(1,128)}, u32[]{:S(2)}) copy-start(s32[1,1024]{1,0:T(1,128)} %param.16) | copy-start | bytes 12292
  6.5 30.4 %all-gather.3.cloned.1.call-start = ((), (), s32[]{:S(2)}) async-start(), calls=%async_computation.1 | async-start | bytes 2359296 | tf_op jit(solution)/shard_map/all_gather | solution.py:95
  8.5 112.1 %all-gather.5.cloned.1.call-start = ((), (), s32[]{:S(2)}) async-start(), calls=%async_computation.2 | async-start | bytes 8912896 | tf_op jit(solution)/shard_map/all_gather | solution.py:113
  39.1 86.6 %copy-start.8 = (f32[4096]{0:T(1024)S(1)}, f32[4096]{0:T(1024)}, u32[]{:S(2)}) copy-start(f32[4096]{0:T(1024)} %param.17) | copy-start | bytes 49156
  41.9 278.8 %all-reduce.3.cloned.1.call-start = ((), (), s32[]{:S(2)}) async-start(), calls=%async_computation.3 | async-start | bytes 16777216 | tf_op jit(solution)/shard_map/psum | solution.py:152
  125.7 10.4 %copy-start.4 = (bf16[4096,64]{0,1:T(8,128)(2,1)S(1)}, bf16[4096,64]{0,1:T(8,128)(2,1)}, u32[]{:S(2)}) copy-start(bf16[4096,64]{0,1:T(8,128)(2,1)} %param.20) | copy-start | bytes 1572868
  136.1 6.2 %copy-start.2 = (bf16[1024,4096]{1,0:T(8,128)(2,1)S(1)}, bf16[1024,4096]{1,0:T(8,128)(2,1)}, u32[]{:S(2)}) copy-start(bf16[1024,4096]{1,0:T(8,128)(2,1)} %fusion.7) | copy-start | bytes 25165828
  136.1 6.2 %copy-start.5 = (bf16[4096,64]{0,1:T(8,128)(2,1)S(1)}, bf16[4096,64]{0,1:T(8,128)(2,1)}, u32[]{:S(2)}) copy-start(bf16[4096,64]{0,1:T(8,128)(2,1)} %param.19) | copy-start | bytes 1572868
  142.3 2.7 copy-start.9
  154.3 7.3 %collective-permute-start = (bf16[1024,128]{0,1:T(8,128)(2,1)S(1)}, bf16[1024,128]{0,1:T(8,128)(2,1)S(1)}, u32[]{:S(2)}, u32[]{:S(2)}) collective-permute-start(bf16[1024,128]{0,1:T(8,128)(2,1)S(1)} %pad_maximum_fusion.1), channel_id=1, source_target_pairs={{0,1},{1,0},{2,3},{3,2},{4,5},{5,4},{6,7},{7,6},{8,9},{9,8},{10,11... | collective-permute-start | bytes 786440 | tf_op jit(solution)/shard_map/ppermute | solution.py:22
  157.6 8.9 %copy-start.6 = (pred[512,1024]{0,1:T(8,128)(4,1)S(1)}, pred[512,1024]{0,1:T(8,128)(4,1)}, u32[]{:S(2)}) copy-start(pred[512,1024]{0,1:T(8,128)(4,1)} %get-tuple-element.26) | copy-start | bytes 1572868
  170.2 3.4 copy-start.11
  179.8 152.1 %copy-start.10 = (f32[4096]{0:T(1024)S(1)}, f32[4096]{0:T(1024)}, u32[]{:S(2)}) copy-start(f32[4096]{0:T(1024)} %param.22) | copy-start | bytes 49156
  179.8 274.0 %reduce-scatter.2.cloned.1.call-start = ((), (), s32[]{:S(2)}) async-start(), calls=%async_computation.4 | async-start | bytes 8912896 | tf_op jit(solution)/shard_map/reduce_scatter | solution.py:159
  328.7 3.2 copy-start.3
  343.2 112.7 %copy-start.1 = (bf16[256,4096]{1,0:T(8,128)(2,1)S(1)}, bf16[256,4096]{1,0:T(8,128)(2,1)}, u32[]{:S(2)}) copy-start(bf16[256,4096]{1,0:T(8,128)(2,1)} %param.21) | copy-start | bytes 6291460
Sparse Core Ops, SparseCore 0:
  9.1 27.8 all-gather.2
  42.0 78.5 all-gather.4
  179.9 140.6 all-reduce.2
  369.7 84.0 reduce-scatter.1
where the time goes:
time: 466 us; the launch traced here: 463 us
  waiting for transfers between devices  315 us (68%)
  matrix products  72.3 us (16%)
  other arithmetic  35.9 us (8%)
  between operations  14.3 us (3%)
  local copies, waits for them, and re-layouts  13.2 us (3%)
  blocking collectives  10.6 us (2%)
    psum x1, waiting for transfers between devices, shards(): lax.psum(partial_rows.astype(jnp.bfloat16), 'ts').astype(jnp.float32)  141 us
    reduce_scatter x1, waiting for transfers between devices, shards(): lax.psum_scatter(jnp.dot(hidden, w_down, preferred_element_type=jnp.float...  84.2 us
    all_gather x1, waiting for transfers between devices, shards(): packed = lax.all_gather(own_part, 'ts', axis=1, tiled=True)  74.7 us
    dot_general x1, matrix products, shards(): jnp.dot(hidden, w_down, preferred_element_type=jnp.float32)  26.4 us
    reduce_sum x2, other arithmetic, norm_rows(): jnp.mean(widened * widened, axis=-1, keepdims=True) + norm_epsilon  13.1 us
    all_gather x1, waiting for transfers between devices, shards(): lax.all_gather(flat_bridge, 'dp', axis=0, tiled=True)  12.6 us
    dot_general x1, matrix products, shards(): up_proj = jnp.dot(normed_mlp, w_up, preferred_element_type=jnp.float32)  11.3 us
    unnamed x1, blocking collectives  10.6 us
  transfers between devices with their start and end apart: 5, of which 5 were waited for; matrix products, arithmetic and copies ran while one was open for 3% of the time, Pallas kernels for 0%

commit v1 on v0

--- a/solution.py
+++ b/solution.py
@@ -5,6 +5,8 @@
 
 HD = 128
 DOC_LEN = 64
+ROW_CHUNKS = 2
+COL_CHUNKS = 2
 
 
 norm_epsilon = 1e-05
@@ -59,6 +61,10 @@
         "hqk,kd->qhd", probabilities, values_full, preferred_element_type=jnp.float32
     )
     return mixed_rows.astype(jnp.bfloat16).reshape(query_block.shape[0], -1)
+
+
+def after(ready, value):
+    return lax.optimization_barrier((ready, value))[1]
 
 
 def shards(
@@ -91,9 +97,16 @@
         jnp.where(doc_match, starts[None, :], 0), axis=1
     )
     flat_bridge = bridge.reshape(bridge.shape[0], bridge_len * part_width)
-    arrived, arrived_slots = (
-        lax.all_gather(flat_bridge, "dp", axis=0, tiled=True),
-        lax.all_gather(crystal_slot, "dp", axis=0, tiled=True),
+    slot_high = (crystal_slot // 128).astype(jnp.bfloat16)
+    slot_low = (crystal_slot % 128).astype(jnp.bfloat16)
+    slot_cols = jnp.zeros((bridge.shape[0], 128), jnp.bfloat16)
+    slot_cols = slot_cols.at[:, 0].set(slot_high).at[:, 1].set(slot_low)
+    arrived_all = lax.all_gather(
+        jnp.concatenate([flat_bridge, slot_cols], axis=1), "dp", axis=0, tiled=True
+    )
+    arrived = arrived_all[:, : bridge_len * part_width]
+    arrived_slots = (
+        arrived_all[:, -128].astype(jnp.int32) * 128 + arrived_all[:, -127].astype(jnp.int32)
     )
     wanted = group_index * seq_len + starts
     picking = wanted[:, None] == arrived_slots[None, :]
@@ -110,58 +123,91 @@
         row_pick.astype(jnp.bfloat16), by_doc, preferred_element_type=jnp.float32
     ).astype(jnp.bfloat16)
     own_part = jnp.where(in_bridge[:, None], filled, text_embed[0])
-    packed = lax.all_gather(own_part, "ts", axis=1, tiled=True)
-    normed = norm_rows(packed, attn_gain)
+
+    chunk_rows = seq_len // ROW_CHUNKS
     heads_here = w_query.shape[1] // HD
-    queries = jnp.dot(normed, w_query, preferred_element_type=jnp.float32).reshape(
-        seq_len, heads_here, HD
-    )
-    queries = rotate_pairs(queries, positions, 0).astype(jnp.bfloat16)
     kv_cols = w_key.shape[1]
     upper_half = ts_index % 2 == 1
-    key_half = jnp.dot(normed, w_key, preferred_element_type=jnp.float32).reshape(
-        seq_len, 1, kv_cols
-    )
-    key_half = rotate_pairs(key_half, positions, ts_index % 2 * (kv_cols // 2))
-    key_half = key_half.astype(jnp.bfloat16).reshape(seq_len, kv_cols)
-    value_half = jnp.dot(normed, w_value, preferred_element_type=jnp.float32).astype(jnp.bfloat16)
-    own_pair = jnp.concatenate([key_half, value_half], axis=1)
-    partner = partner_2(own_pair, "ts", 0)
-    lower_half = jnp.where(upper_half, partner, own_pair)
-    higher = jnp.where(upper_half, own_pair, partner)
-    keys_full = jnp.concatenate([lower_half[:, :kv_cols], higher[:, :kv_cols]], axis=1)
-    values_full = jnp.concatenate([lower_half[:, kv_cols:], higher[:, kv_cols:]], axis=1)
-    block_rows = min(512, seq_len)
-    outputs = []
-    for block_index in range(seq_len // block_rows):
-        first_row = block_index * block_rows
-        query_index = jnp.arange(first_row, first_row + block_rows, dtype=jnp.int32)
-        outputs.append(
-            attend_block(
-                queries[first_row : first_row + block_rows],
-                segment_ids[first_row : first_row + block_rows],
-                query_index,
-                keys_full,
-                values_full,
-                segment_ids,
-            )
-        )
-    attended = jnp.concatenate(outputs, axis=0)
-    mine_offset = ts_index * tok_rows
-    partial_rows = jnp.dot(attended, w_out, preferred_element_type=jnp.float32)
-    attn_sum = lax.psum(partial_rows.astype(jnp.bfloat16), "ts").astype(jnp.float32)
-    after_all = (packed.astype(jnp.float32) + attn_sum).astype(jnp.bfloat16)
-    after_mine = lax.dynamic_slice_in_dim(after_all, mine_offset, tok_rows, 0)
-    normed_mlp = norm_rows(after_all, mlp_gain)
-    gate_proj = jnp.dot(normed_mlp, w_gate, preferred_element_type=jnp.float32)
-    up_proj = jnp.dot(normed_mlp, w_up, preferred_element_type=jnp.float32)
-    hidden = (jax.nn.silu(gate_proj) * up_proj).astype(jnp.bfloat16)
-    mlp_mine = lax.psum_scatter(
-        jnp.dot(hidden, w_down, preferred_element_type=jnp.float32).astype(jnp.bfloat16),
-        "ts",
-        scatter_dimension=0,
-        tiled=True,
-    ).astype(jnp.float32)
+
+    packed_chunks = []
+    keys_chunks = []
+    values_chunks = []
+    after_chunks = []
+    hidden_chunks = []
+    previous = None
+    previous_sum = None
+    gate = None
+    for chunk in range(ROW_CHUNKS):
+        rows = slice(chunk * chunk_rows, (chunk + 1) * chunk_rows)
+        local_rows = own_part[rows]
+        if previous is not None:
+            local_rows = after(previous, local_rows)
+        packed = lax.all_gather(local_rows, "ts", axis=1, tiled=True)
+        previous = packed
+        if gate is not None:
+            packed = after(gate, packed)
+        packed_chunks.append(packed)
+        chunk_positions = positions[rows]
+        normed = norm_rows(packed, attn_gain)
+        queries = jnp.dot(normed, w_query, preferred_element_type=jnp.float32).reshape(
+            chunk_rows, heads_here, HD
+        )
+        queries = rotate_pairs(queries, chunk_positions, 0).astype(jnp.bfloat16)
+        key_half = jnp.dot(normed, w_key, preferred_element_type=jnp.float32).reshape(
+            chunk_rows, 1, kv_cols
+        )
+        key_half = rotate_pairs(key_half, chunk_positions, ts_index % 2 * (kv_cols // 2))
+        key_half = key_half.astype(jnp.bfloat16).reshape(chunk_rows, kv_cols)
+        value_half = jnp.dot(normed, w_value, preferred_element_type=jnp.float32).astype(jnp.bfloat16)
+        own_pair = jnp.concatenate([key_half, value_half], axis=1)
+        partner = partner_2(own_pair, "ts", 0)
+        lower_half = jnp.where(upper_half, partner, own_pair)
+        higher = jnp.where(upper_half, own_pair, partner)
+        keys_chunks.append(jnp.concatenate([lower_half[:, :kv_cols], higher[:, :kv_cols]], axis=1))
+        values_chunks.append(jnp.concatenate([lower_half[:, kv_cols:], higher[:, kv_cols:]], axis=1))
+        keys_seen = jnp.concatenate(keys_chunks, axis=0)
+        values_seen = jnp.concatenate(values_chunks, axis=0)
+        end_row = (chunk + 1) * chunk_rows
+        query_index = jnp.arange(chunk * chunk_rows, end_row, dtype=jnp.int32)
+        attended = attend_block(
+            queries,
+            segment_ids[rows],
+            query_index,
+            keys_seen,
+            values_seen,
+            segment_ids[:end_row],
+        )
+        gate = attended
+        partial_rows = jnp.dot(attended, w_out, preferred_element_type=jnp.float32).astype(
+            jnp.bfloat16
+        )
+        if previous_sum is not None:
+            partial_rows = after(previous_sum, partial_rows)
+        attn_sum = lax.psum(partial_rows, "ts")
+        previous_sum = attn_sum
+        after_attn = (packed.astype(jnp.float32) + attn_sum.astype(jnp.float32)).astype(jnp.bfloat16)
+        after_chunks.append(after_attn)
+        normed_mlp = norm_rows(after_attn, mlp_gain)
+        gate_proj = jnp.dot(normed_mlp, w_gate, preferred_element_type=jnp.float32)
+        up_proj = jnp.dot(normed_mlp, w_up, preferred_element_type=jnp.float32)
+        hidden_chunks.append((jax.nn.silu(gate_proj) * up_proj).astype(jnp.bfloat16))
+
+    hidden = jnp.concatenate(hidden_chunks, axis=0)
+    after_all = jnp.concatenate(after_chunks, axis=0)
+    after_mine = lax.dynamic_slice_in_dim(after_all, ts_index * tok_rows, tok_rows, 0)
+    out_cols = w_down.shape[1] // COL_CHUNKS
+    mlp_parts = []
+    previous_part = None
+    for col in range(COL_CHUNKS):
+        down = jnp.dot(
+            hidden, w_down[:, col * out_cols : (col + 1) * out_cols], preferred_element_type=jnp.float32
+        ).astype(jnp.bfloat16)
+        if previous_part is not None:
+            down = after(previous_part, down)
+        part = lax.psum_scatter(down, "ts", scatter_dimension=0, tiled=True)
+        previous_part = part
+        mlp_parts.append(part)
+    mlp_mine = jnp.concatenate(mlp_parts, axis=1).astype(jnp.float32)
     layer_rows = (after_mine.astype(jnp.float32) + mlp_mine).astype(jnp.bfloat16)
     return layer_rows.reshape(1, tok_rows, layer_rows.shape[1])
 

time: 466 us -> 573 us (1.23)
  waiting for transfers between devices: 315 us -> 417 us
  blocking collectives: 10.6 us -> 0 us
  other arithmetic: 35.9 us -> 42.6 us
    reduce_scatter x1 -> x2, waiting for transfers between devices: 84.2 us -> 150 us  [shards(): part = lax.psum_scatter(down, 'ts', scatter_dimension=0, tiled=True)]
    psum x1 -> x2, waiting for transfers between devices: 141 us -> 163 us  [shards(): attn_sum = lax.psum(partial_rows, 'ts')]
    all_gather x2 -> x3, waiting for transfers between devices: 87.3 us -> 102 us  [the longest x2 76 us: shards(): packed = lax.all_gather(local_rows, 'ts', axis=1, tiled=True)]
    unnamed x1 -> x0, blocking collectives: 10.6 us -> none
    convert_element_type x1 -> x2, other arithmetic: 10.4 us -> 3.31 us  [norm_rows(): return (widened * inverse_rms * gain).astype(jnp.bfloat16)]
    reduce_sum x2 -> x4, other arithmetic: 13.1 us -> 17.5 us  [norm_rows(): jnp.mean(widened * widened, axis=-1, keepdims=True) + norm_epsilon]
    dot_general x2 -> x6, matrix products: 32 us -> 33.8 us  [the longest x2 14.7 us: shards(): gate_proj = jnp.dot(normed_mlp, w_gate, preferred_element_type=jnp.float32)]
  transfers between devices with their start and end apart: 5 -> 9, of which waited for: 5 -> 8; matrix products, arithmetic and copies ran while one was open for 3% -> 17% of each run, Pallas kernels for 0% -> 0%
where the time goes in v1:
time: 573 us; the launch traced here: 566 us
  waiting for transfers between devices  417 us (73%)
  matrix products  75.9 us (13%)
  other arithmetic  42.6 us (7%)
  between operations  14.6 us (3%)
  local copies, waits for them, and re-layouts  13.4 us (2%)
    psum x2, waiting for transfers between devices, shards(): attn_sum = lax.psum(partial_rows, 'ts')  163 us
    reduce_scatter x2, waiting for transfers between devices, shards(): part = lax.psum_scatter(down, 'ts', scatter_dimension=0, tiled=True)  150 us
    all_gather x2, waiting for transfers between devices, shards(): packed = lax.all_gather(local_rows, 'ts', axis=1, tiled=True)  76 us
    all_gather x1, waiting for transfers between devices, shards(): lax.all_gather(jnp.concatenate([flat_bridge, slot_cols], axis=1), 'dp', a...  25.7 us
    reduce_sum x4, other arithmetic, norm_rows(): jnp.mean(widened * widened, axis=-1, keepdims=True) + norm_epsilon  17.5 us
    dot_general x2, matrix products, shards(): gate_proj = jnp.dot(normed_mlp, w_gate, preferred_element_type=jnp.float32)  14.7 us
    dot_general x2, matrix products, shards(): jnp.dot(hidden, w_down[:, col * out_cols:(col + 1) * out_cols], preferred...  12.6 us
  transfers between devices with their start and end apart: 9, of which 8 were waited for; matrix products, arithmetic and copies ran while one was open for 17% of the time, Pallas kernels for 0%

profile of v1, /device:TPU:0, one launch (start us, length us, event | category | flops | bytes accessed | tf_op | source)
XLA Modules:
  0.0 566.0 jit_solution(9591049494155157957)
XLA Ops:
  7.8 1.9 fusion.95
  9.8 1.1 copy.107
  14.0 25.7 %all-gather.4.cloned.1.call-done = bf16[128,8320]{1,0:T(8,128)(2,1)} async-done(((bf16[16,8320]{1,0:T(8,128)(2,1)}), bf16[128,8320]{1,0:T(8,128)(2,1)}) %all-gather.4.cloned.1.call-update) | async-done | bytes 2129936 | tf_op jit(solution)/shard_map/all_gather | solution.py:104
  40.8 2.0 convolution_convert_fusion
  42.9 1.1 fusion.32
  44.9 57.9 %all-gather.6.cloned.1.call-done = bf16[512,4096]{1,0:T(8,128)(2,1)} async-done(((bf16[512,256]{1,0:T(8,128)(2,1)}), bf16[512,4096]{1,0:T(8,128)(2,1)}) %all-gather.6.cloned.1.call-update) | async-done | bytes 4194320 | tf_op jit(solution)/shard_map/all_gather | solution.py:145
  104.5 1.7 multiply_cosine_fusion
  106.3 1.3 fusion.25
  107.5 3.1 fusion.8
  110.6 1.7 fusion.10
  112.3 2.0 copy-done.6
  114.3 1.4 fusion.132
  115.9 1.0 fusion.88
  117.1 3.7 convolution_convert_fusion.7
  121.5 1.3 collective-permute-start
  122.8 3.8 fusion.133
  126.6 2.1 reshape_reshape.13
  128.7 1.7 fusion.116
  130.4 1.4 subtract_convert_fusion.1
  131.8 1.0 pad_maximum_fusion.4
  134.5 4.0 fusion.124
  138.5 2.0 convolution_convert_fusion.5
  140.5 3.2 convolution_convert_fusion.2
  143.8 18.1 %all-gather.8.cloned.1.call-done = bf16[512,4096]{1,0:T(8,128)(2,1)} async-done(((bf16[512,256]{1,0:T(8,128)(2,1)}), bf16[512,4096]{1,0:T(8,128)(2,1)}) %all-gather.8.cloned.1.call-update) | async-done | bytes 4194320 | tf_op jit(solution)/shard_map/all_gather | solution.py:145
  161.9 3.2 fusion.12
  165.3 1.7 fusion.14
  167.0 2.0 copy-done.4
  168.9 1.4 fusion.134
  171.0 4.4 convolution_convert_fusion.6
  177.1 3.7 fusion.135
  180.8 1.4 reshape_reshape.15
  183.5 1.3 collective-permute-done.1
  185.9 4.6 fusion.127
  190.5 2.7 fusion.41
  193.2 3.3 convolution_convert_fusion.1
  196.5 74.1 %all-reduce.4.cloned.1.call-done = bf16[512,4096]{1,0:T(8,128)(2,1)} async-done(((bf16[512,4096]{1,0:T(8,128)(2,1)}), bf16[512,4096]{1,0:T(8,128)(2,1)}) %all-reduce.4.cloned.1.call-update) | async-done | bytes 4194320 | tf_op jit(solution)/shard_map/psum | solution.py:186
  270.7 5.6 fusion.2
  276.3 7.5 %fusion.39 = f32[512,768]{1,0:T(8,128)S(1)} fusion(bf16[4096,768]{1,0:T(8,128)(2,1)} %param.27, bf16[512,4096]{1,0:T(8,128)(2,1)S(1)} %get-tuple-element.38, f32[4096]{0:T(1024)S(1)} %copy-done.27, f32[512]{0:T(512)S(1)} %add_rsqrt_fusion.1), kind=kOutput, calls=%fused_computation.59 | convolution fusion | flops 3229614080 | bytes 12077056 | tf_op jit(solution)/shard_map/dot_general | solution.py:191
  283.9 3.6 multiply_convert_fusion.1
  287.5 89.4 %all-reduce.6.cloned.1.call-done = bf16[512,4096]{1,0:T(8,128)(2,1)} async-done(((bf16[512,4096]{1,0:T(8,128)(2,1)}), bf16[512,4096]{1,0:T(8,128)(2,1)}) %all-reduce.6.cloned.1.call-update) | async-done | bytes 4194320 | tf_op jit(solution)/shard_map/psum | solution.py:186
  376.9 5.6 fusion.5
  382.5 7.2 %fusion.36 = f32[512,768]{1,0:T(8,128)S(1)} fusion(bf16[4096,768]{1,0:T(8,128)(2,1)} %param.27, bf16[512,4096]{1,0:T(8,128)(2,1)S(1)} %get-tuple-element.40, f32[512]{0:T(512)S(1)} %add_rsqrt_fusion, f32[4096]{0:T(1024)S(1)} %copy-done.27), kind=kOutput, calls=%fused_computation.58 | convolution fusion | flops 3229614080 | bytes 12077056 | tf_op jit(solution)/shard_map/dot_general | solution.py:191
  389.7 3.6 multiply_convert_fusion
  393.4 5.0 convolution_convert_fusion.4
  398.4 7.7 %convolution_convert_fusion.3 = bf16[1024,2048]{1,0:T(8,128)(2,1)} fusion(bf16[768,4096]{1,0:T(8,128)(2,1)} %param.29, bf16[512,768]{1,0:T(8,128)(2,1)S(1)} %multiply_convert_fusion, bf16[512,768]{1,0:T(8,128)(2,1)S(1)} %multiply_convert_fusion.1), kind=kOutput, calls=%fused_computation.34 | convolution fusion | flops 3226468352 | bytes 8912896 | tf_op jit(solution)/shard_map/dot_general | solution.py:202
  406.1 69.8 %reduce-scatter.3.cloned.1.call-done = bf16[64,2048]{1,0:T(8,128)(2,1)} async-done(((bf16[1024,2048]{1,0:T(8,128)(2,1)}), bf16[64,2048]{1,0:T(8,128)(2,1)}) %reduce-scatter.3.cloned.1.call-update) | async-done | bytes 262160 | tf_op jit(solution)/shard_map/reduce_scatter | solution.py:207
  475.9 80.6 %reduce-scatter.5.cloned.1.call-done = bf16[64,2048]{1,0:T(8,128)(2,1)} async-done(((bf16[1024,2048]{1,0:T(8,128)(2,1)}), bf16[64,2048]{1,0:T(8,128)(2,1)}) %reduce-scatter.5.cloned.1.call-update) | async-done | bytes 262160 | tf_op jit(solution)/shard_map/reduce_scatter | solution.py:207
  556.5 2.2 fusion.49
  (130 shorter events, 15.7 us)
Async XLA Ops:
  6.5 133.9 %copy-start = (bf16[256,4096]{1,0:T(8,128)(2,1)S(1)}, bf16[256,4096]{1,0:T(8,128)(2,1)}, u32[]{:S(2)}) copy-start(bf16[256,4096]{1,0:T(8,128)(2,1)} %param.25) | copy-start | bytes 6291460
  6.5 36.4 %copy-start.26 = (bf16[1,1024,256]{2,1,0:T(8,128)(2,1)S(1)}, bf16[1,1024,256]{2,1,0:T(8,128)(2,1)}, u32[]{:S(2)}) copy-start(bf16[1,1024,256]{2,1,0:T(8,128)(2,1)} %param.17) | copy-start | bytes 1572868
  6.5 33.2 %all-gather.4.cloned.1.call-start = ((), (), s32[]{:S(2)}) async-start(), calls=%async_computation.2 | async-start | bytes 2396160 | tf_op jit(solution)/shard_map/all_gather | solution.py:104
  10.9 92.6 %copy-start.16 = (s32[1,1024]{1,0:T(1,128)S(1)}, s32[1,1024]{1,0:T(1,128)}, u32[]{:S(2)}) copy-start(s32[1,1024]{1,0:T(1,128)} %param.20) | copy-start | bytes 12292
  11.7 91.2 %all-gather.6.cloned.1.call-start = ((), (), s32[]{:S(2)}) async-start(), calls=%async_computation.3 | async-start | bytes 4456448 | tf_op jit(solution)/shard_map/all_gather | solution.py:145
  44.0 66.6 %copy-start.17 = (f32[4096]{0:T(1024)S(1)}, f32[4096]{0:T(1024)}, u32[]{:S(2)}) copy-start(f32[4096]{0:T(1024)} %param.21) | copy-start | bytes 49156
  44.9 117.0 %all-gather.8.cloned.1.call-start = ((), (), s32[]{:S(2)}) async-start(), calls=%async_computation.5 | async-start | bytes 4456448 | tf_op jit(solution)/shard_map/all_gather | solution.py:145
  102.9 167.7 %all-reduce.4.cloned.1.call-start = ((), (), s32[]{:S(2)}) async-start(), calls=%async_computation.4 | async-start | bytes 8388608 | tf_op jit(solution)/shard_map/psum | solution.py:186
  102.9 7.7 %copy-start.3 = (bf16[512,4096]{1,0:T(8,128)(2,1)S(1)}, bf16[512,4096]{1,0:T(8,128)(2,1)}, u32[]{:S(2)}) copy-start(bf16[512,4096]{1,0:T(8,128)(2,1)} %all-gather.6.cloned.1.call-done) | copy-start | bytes 12582916
  103.6 7.0 %copy-start.22 = (f32[512]{0:T(512)}, f32[512]{0:T(512)S(1)}, u32[]{:S(2)}) copy-start(f32[512]{0:T(512)S(1)} %get-tuple-element.71) | copy-start | bytes 6148
  103.6 7.0 %copy-start.24 = (f32[512]{0:T(512)}, f32[512]{0:T(512)S(1)}, u32[]{:S(2)}) copy-start(f32[512]{0:T(512)S(1)} %get-tuple-element.72) | copy-start | bytes 6148
  110.6 3.7 copy-start.10
  112.3 2.0 copy-start.6
  114.3 2.7 copy-start.11
  117.1 5.8 %copy-start.7 = (bf16[512,4096]{1,0:T(8,128)(2,1)S(1)}, bf16[512,4096]{1,0:T(8,128)(2,1)}, u32[]{:S(2)}) copy-start(bf16[512,4096]{1,0:T(8,128)(2,1)} %copy-done.6) | copy-start | bytes 12582916
  121.5 8.9 %copy-start.14 = (f32[512,64]{0,1:T(8,128)S(1)}, f32[512,64]{0,1:T(8,128)}, u32[]{:S(2)}) copy-start(f32[512,64]{0,1:T(8,128)} %get-tuple-element.81) | copy-start | bytes 393220
  121.5 11.4 %collective-permute-start = (bf16[512,128]{0,1:T(8,128)(2,1)}, bf16[512,128]{0,1:T(8,128)(2,1)}, u32[]{:S(2)}, u32[]{:S(2)}) collective-permute-start(bf16[512,128]{0,1:T(8,128)(2,1)} %pad_maximum_fusion.6), channel_id=1, source_target_pairs={{0,1},{1,0},{2,3},{3,2},{4,5},{5,4},{6,7},{7,6},{8,9},{9,8},{10,11... | collective-permute-start | bytes 393224 | tf_op jit(solution)/shard_map/ppermute | solution.py:24
  134.5 4.0 copy-start.20
  134.5 4.0 copy-start.21
  143.7 233.1 %all-reduce.6.cloned.1.call-start = ((), (), s32[]{:S(2)}) async-start(), calls=%async_computation.6 | async-start | bytes 8388608 | tf_op jit(solution)/shard_map/psum | solution.py:186
  161.9 3.4 copy-start.2
  167.0 2.0 copy-start.4
  168.9 1.6 copy-start.23
  168.9 1.6 copy-start.25
  171.0 6.1 %copy-start.5 = (bf16[512,4096]{1,0:T(8,128)(2,1)S(1)}, bf16[512,4096]{1,0:T(8,128)(2,1)}, u32[]{:S(2)}) copy-start(bf16[512,4096]{1,0:T(8,128)(2,1)} %copy-done.4) | copy-start | bytes 12582916
  176.1 6.5 %copy-start.13 = (f32[512,64]{0,1:T(8,128)S(1)}, f32[512,64]{0,1:T(8,128)}, u32[]{:S(2)}) copy-start(f32[512,64]{0,1:T(8,128)} %get-tuple-element.78) | copy-start | bytes 393220
  176.1 8.7 %collective-permute-start.1 = (bf16[512,128]{0,1:T(8,128)(2,1)}, bf16[512,128]{0,1:T(8,128)(2,1)}, u32[]{:S(2)}, u32[]{:S(2)}) collective-permute-start(bf16[512,128]{0,1:T(8,128)(2,1)} %pad_maximum_fusion.7), channel_id=1, source_target_pairs={{0,1},{1,0},{2,3},{3,2},{4,5},{5,4},{6,7},{7,6},{8,9},{9,8},{10,11... | collective-permute-start | bytes 393224 | tf_op jit(solution)/shard_map/ppermute | solution.py:24
  180.8 5.1 copy-start.12
  185.9 4.6 copy-start.18
  185.9 4.6 copy-start.19
  270.6 5.7 %copy-start.27 = (f32[4096]{0:T(1024)S(1)}, f32[4096]{0:T(1024)}, u32[]{:S(2)}) copy-start(f32[4096]{0:T(1024)} %param.26) | copy-start | bytes 49156
  270.6 205.3 %reduce-scatter.3.cloned.1.call-start = ((), (), s32[]{:S(2)}) async-start(), calls=%async_computation.7 | async-start | bytes 4456448 | tf_op jit(solution)/shard_map/reduce_scatter | solution.py:207
  270.6 13.2 %slice-start = ((s8[6291456]{0:T(1024)(128)(4,1)}), s8[4194304]{0:T(1024)(128)(4,1)S(1)}, s32[]{:S(2)}) async-start(s8[6291456]{0:T(1024)(128)(4,1)} %bitcast.109), calls=%async_computation.9 | async-start | bytes 8388608
  276.2 7.6 %copy-start.8 = (bf16[512,4096]{1,0:T(8,128)(2,1)}, bf16[512,4096]{1,0:T(8,128)(2,1)S(1)}, u32[]{:S(2)}) copy-start(bf16[512,4096]{1,0:T(8,128)(2,1)S(1)} %get-tuple-element.38) | copy-start | bytes 12582916
  276.3 7.6 %slice-start.1 = ((s8[6291456]{0:T(1024)(128)(4,1)}), s8[2097152]{0:T(1024)(128)(4,1)S(1)}, s32[]{:S(2)}) async-start(s8[6291456]{0:T(1024)(128)(4,1)} %bitcast.109), calls=%async_computation.10 | async-start | bytes 4194304
  376.9 12.8 %slice-start.2 = ((s8[6291456]{0:T(1024)(128)(4,1)}), s8[4194304]{0:T(1024)(128)(4,1)S(1)}, s32[]{:S(2)}) async-start(s8[6291456]{0:T(1024)(128)(4,1)} %bitcast.111), calls=%async_computation.11 | async-start | bytes 8388608
  382.4 7.2 %copy-start.9 = (bf16[512,4096]{1,0:T(8,128)(2,1)}, bf16[512,4096]{1,0:T(8,128)(2,1)S(1)}, u32[]{:S(2)}) copy-start(bf16[512,4096]{1,0:T(8,128)(2,1)S(1)} %get-tuple-element.40) | copy-start | bytes 12582916
  382.5 7.2 %slice-start.3 = ((s8[6291456]{0:T(1024)(128)(4,1)}), s8[2097152]{0:T(1024)(128)(4,1)S(1)}, s32[]{:S(2)}) async-start(s8[6291456]{0:T(1024)(128)(4,1)} %bitcast.111), calls=%async_computation.12 | async-start | bytes 4194304
  382.5 10.9 %slice-start.4 = ((s8[6291456]{0:T(1024)(128)(4,1)}), s8[4194304]{0:T(1024)(128)(4,1)S(1)}, s32[]{:S(2)}) async-start(s8[6291456]{0:T(1024)(128)(4,1)} %bitcast.113), calls=%async_computation.13 | async-start | bytes 8388608
  389.7 3.6 slice-start.5
  398.4 158.1 %reduce-scatter.5.cloned.1.call-start = ((), (), s32[]{:S(2)}) async-start(), calls=%async_computation.8 | async-start | bytes 4456448 | tf_op jit(solution)/shard_map/reduce_scatter | solution.py:207
  475.9 80.6 %copy-start.15 = (bf16[64,2048]{1,0:T(8,128)(2,1)S(1)}, bf16[64,2048]{1,0:T(8,128)(2,1)}, u32[]{:S(2)}) copy-start(bf16[64,2048]{1,0:T(8,128)(2,1)} %reduce-scatter.3.cloned.1.call-done) | copy-start | bytes 786436
  475.9 82.8 %copy-start.1 = (bf16[256,4096]{1,0:T(8,128)(2,1)S(1)}, bf16[256,4096]{1,0:T(8,128)(2,1)}, u32[]{:S(2)}) copy-start(bf16[256,4096]{1,0:T(8,128)(2,1)} %param.25) | copy-start | bytes 6291460
Sparse Core Ops, SparseCore 0:
  11.8 27.8 all-gather.3
  45.0 57.8 all-gather.5
  105.0 56.8 all-gather.7
  165.1 105.4 all-reduce.3
  273.8 103.0 all-reduce.5
  398.5 77.3 reduce-scatter.2
  479.6 76.8 reduce-scatter.4

commit v2 on v0

--- a/solution.py
+++ b/solution.py
@@ -91,9 +91,16 @@
         jnp.where(doc_match, starts[None, :], 0), axis=1
     )
     flat_bridge = bridge.reshape(bridge.shape[0], bridge_len * part_width)
-    arrived, arrived_slots = (
-        lax.all_gather(flat_bridge, "dp", axis=0, tiled=True),
-        lax.all_gather(crystal_slot, "dp", axis=0, tiled=True),
+    slot_high = (crystal_slot // 128).astype(jnp.bfloat16)
+    slot_low = (crystal_slot % 128).astype(jnp.bfloat16)
+    slot_cols = jnp.zeros((bridge.shape[0], 128), jnp.bfloat16)
+    slot_cols = slot_cols.at[:, 0].set(slot_high).at[:, 1].set(slot_low)
+    arrived_all = lax.all_gather(
+        jnp.concatenate([flat_bridge, slot_cols], axis=1), "dp", axis=0, tiled=True
+    )
+    arrived = arrived_all[:, : bridge_len * part_width]
+    arrived_slots = (
+        arrived_all[:, -128].astype(jnp.int32) * 128 + arrived_all[:, -127].astype(jnp.int32)
     )
     wanted = group_index * seq_len + starts
     picking = wanted[:, None] == arrived_slots[None, :]

time: 466 us -> 469 us (level)
  waiting for transfers between devices: 315 us -> 328 us
  blocking collectives: 10.6 us -> 0 us
    all_gather x1, waiting for transfers between devices: 12.6 us -> 25.7 us  [shards(): lax.all_gather(jnp.concatenate([flat_bridge, slot_cols], axis=1), 'dp', a...]
    unnamed x1 -> x0, blocking collectives: 10.6 us -> none
  transfers between devices with their start and end apart: 5 -> 5, of which waited for: 5 -> 5; matrix products, arithmetic and copies ran while one was open for 3% -> 2% of each run, Pallas kernels for 0% -> 0%
where the time goes in v2:
time: 469 us; the launch traced here: 467 us
  waiting for transfers between devices  328 us (70%)
  matrix products  72.3 us (15%)
  other arithmetic  40.5 us (9%)
  between operations  13.9 us (3%)
  local copies, waits for them, and re-layouts  10.3 us (2%)
    psum x1, waiting for transfers between devices, shards(): lax.psum(partial_rows.astype(jnp.bfloat16), 'ts').astype(jnp.float32)  141 us
    reduce_scatter x1, waiting for transfers between devices, shards(): lax.psum_scatter(jnp.dot(hidden, w_down, preferred_element_type=jnp.float...  84.1 us
    all_gather x1, waiting for transfers between devices, shards(): packed = lax.all_gather(own_part, 'ts', axis=1, tiled=True)  75.1 us
    dot_general x1, matrix products, shards(): jnp.dot(hidden, w_down, preferred_element_type=jnp.float32)  26.4 us
    all_gather x1, waiting for transfers between devices, shards(): lax.all_gather(jnp.concatenate([flat_bridge, slot_cols], axis=1), 'dp', a...  25.7 us
    reduce_sum x2, other arithmetic, norm_rows(): jnp.mean(widened * widened, axis=-1, keepdims=True) + norm_epsilon  13.1 us
    dot_general x1, matrix products, shards(): up_proj = jnp.dot(normed_mlp, w_up, preferred_element_type=jnp.float32)  11.3 us
    convert_element_type x1, other arithmetic, norm_rows(): return (widened * inverse_rms * gain).astype(jnp.bfloat16)  10.4 us
  transfers between devices with their start and end apart: 5, of which 5 were waited for; matrix products, arithmetic and copies ran while one was open for 2% of the time, Pallas kernels for 0%

profile of v2, /device:TPU:0, one launch (start us, length us, event | category | flops | bytes accessed | tf_op | source)
XLA Modules:
  0.0 466.8 jit_solution(10688281546809678238)
XLA Ops:
  6.5 0.7 compare_reduce_fusion.1
  7.2 0.6 compare_reduce_fusion
  7.8 1.9 fusion.81
  9.8 0.1 copy.66
  9.9 1.1 copy.88
  11.0 0.7 pad_maximum_fusion
  11.8 0.0 all-gather.5.cloned.1.call-start
  11.8 0.8 convert_reduce_fusion
  12.6 0.8 select_reduce_fusion
  13.5 0.7 fusion.78
  14.1 25.7 %all-gather.3.cloned.1.call-done = bf16[128,8320]{1,0:T(8,128)(2,1)} async-done(((bf16[16,8320]{1,0:T(8,128)(2,1)}), bf16[128,8320]{1,0:T(8,128)(2,1)}) %all-gather.3.cloned.1.call-update) | async-done | bytes 2129936 | tf_op jit(solution)/shard_map/all_gather | solution.py:98
  39.8 1.0 add_reduce_fusion
  40.9 2.0 convolution_convert_fusion
  42.9 0.1 reshape.416
  43.0 2.7 fusion.37
  45.9 2.0 multiply_cosine_fusion
  47.9 1.6 fusion.23
  49.5 75.1 %all-gather.5.cloned.1.call-done = bf16[1024,4096]{1,0:T(8,128)(2,1)} async-done(((bf16[1024,256]{1,0:T(8,128)(2,1)}), bf16[1024,4096]{1,0:T(8,128)(2,1)}) %all-gather.5.cloned.1.call-update) | async-done | bytes 8388624 | tf_op jit(solution)/shard_map/all_gather | solution.py:120
  124.5 5.1 %fusion.5 = f32[1024]{0:T(1024)S(1)} fusion(bf16[1024,4096]{1,0:T(8,128)(2,1)} %all-gather.5.cloned.1.call-done), kind=kLoop, calls=%fused_computation.10 | loop fusion | flops 12581888 | bytes 8392704 | tf_op jit(solution)/shard_map/reduce_sum | solution.py:27
  129.7 10.4 %fusion.7 = bf16[1024,4096]{1,0:T(8,128)(2,1)} fusion(bf16[1024,4096]{1,0:T(8,128)(2,1)} %all-gather.5.cloned.1.call-done, f32[4096]{0:T(1024)S(1)} %copy-done.8, f32[1024]{0:T(1024)S(1)} %add_rsqrt_fusion.1), kind=kLoop, calls=%fused_computation.12 | loop fusion | flops 16777216 | bytes 16797696 | tf_op jit(solution)/shard_map/convert_element_type | solution.py:28
  140.0 6.2 %convolution_convert_fusion.3 = bf16[1024,64]{0,1:T(8,128)(2,1)S(1)} fusion(bf16[1024,4096]{1,0:T(8,128)(2,1)} %fusion.7, bf16[4096,64]{0,1:T(8,128)(2,1)S(1)} %copy-done.4), kind=kOutput, calls=%fused_computation.49 | convolution fusion | flops 536936448 | bytes 9043968 | tf_op jit(solution)/shard_map/dot_general | solution.py:134
  146.3 2.7 fusion.107
  148.9 3.7 fusion.108
  152.6 1.8 reshape_reshape.7
  154.4 0.9 reshape_reshape.6
  155.3 1.3 fusion.95
  156.6 0.6 fusion.72
  157.2 0.1 copy.69
  157.3 0.1 convert_element_type.133
  157.4 0.8 fusion.92
  158.2 1.3 collective-permute-start
  159.5 2.1 subtract_convert_fusion
  161.6 1.2 fusion.52
  162.8 2.7 collective-permute-done
  165.5 0.1 broadcast_select_fusion.1
  165.7 4.8 %fusion.102 = (f32[2,512]{1,0:T(2,128)S(1)}, f32[2,512,1024]{1,2,0:T(8,128)}) fusion(pred[512,1024]{0,1:T(8,128)(4,1)} %get-tuple-element.49, bf16[512,2,128]{0,1,2:T(2,128)(2,1)} %bitcast.88, bf16[1024,64]{0,1:T(8,128)(2,1)S(1)} %get-tuple-element.61, bf16[1024,64]{0,1:T(8,128)(2,1)S(1)} %get-tuple-element.42), kind=kOutput, calls=%fused_computation.135 | convolution fusion | flops 273155072 | bytes 5246976 | tf_op jit(solution)/shard_map/sub | solution.py:56
  170.5 3.7 fusion.97
  174.2 2.8 fusion.41
  177.0 0.6 copy-done.11
  177.6 0.5 fusion.40
  178.1 5.6 %convolution_convert_fusion.2 = bf16[1024,4096]{1,0:T(8,128)(2,1)} fusion(bf16[256,4096]{1,0:T(8,128)(2,1)S(1)} %copy-done, bf16[512,256]{0,1:T(8,128)(2,1)S(1)} %bitcast.85, bf16[512,256]{0,1:T(8,128)(2,1)S(1)} %bitcast.84), kind=kOutput, calls=%fused_computation.16 | convolution fusion | flops 2152726528 | bytes 11010048 | tf_op jit(solution)/shard_map/dot_general | solution.py:158
  183.8 140.8 %all-reduce.3.cloned.1.call-done = bf16[1024,4096]{1,0:T(8,128)(2,1)} async-done(((bf16[1024,4096]{1,0:T(8,128)(2,1)}), bf16[1024,4096]{1,0:T(8,128)(2,1)}) %all-reduce.3.cloned.1.call-update) | async-done | bytes 8388624 | tf_op jit(solution)/shard_map/psum | solution.py:159
  324.6 8.1 %fusion.2 = (f32[1024]{0:T(1024)S(1)}, bf16[1024,4096]{1,0:T(8,128)(2,1)S(1)}) fusion(bf16[1024,4096]{1,0:T(8,128)(2,1)} %all-reduce.3.cloned.1.call-done, bf16[1024,4096]{1,0:T(8,128)(2,1)} %all-gather.5.cloned.1.call-done), kind=kLoop, calls=%fused_computation.7 | loop fusion | flops 29359104 | bytes 25169920 | tf_op jit(solution)/shard_map/reduce_sum | solution.py:27
  332.7 3.2 copy-done.3
  335.8 11.3 %fusion.11 = f32[1024,768]{1,0:T(8,128)} fusion(bf16[4096,768]{1,0:T(8,128)(2,1)} %param.28, bf16[1024,4096]{1,0:T(8,128)(2,1)S(1)} %get-tuple-element.30, f32[4096]{0:T(1024)S(1)} %copy-done.10, f32[1024]{0:T(1024)S(1)} %add_rsqrt_fusion), kind=kOutput, calls=%fused_computation.26 | convolution fusion | flops 6459228160 | bytes 17846272 | tf_op jit(solution)/shard_map/dot_general | solution.py:164
  347.1 26.4 %convolution_convert_fusion.1 = bf16[1024,4096]{1,0:T(8,128)(2,1)} fusion(bf16[768,4096]{1,0:T(8,128)(2,1)} %param.29, f32[1024,768]{1,0:T(8,128)} %fusion.11, bf16[4096,768]{1,0:T(8,128)(2,1)} %param.27, bf16[1024,4096]{1,0:T(8,128)(2,1)} %copy-done.3, f32[4096]{0:T(1024)S(1)} %copy-done.10, f32[1024]{0:T(1024)S(1)} %add_rsqrt_fusion), kind=kOutput, calls=%fused_computation.15 | convolution fusion | flops 12910592000 | bytes 32526336 | tf_op jit(solution)/shard_map/dot_general | solution.py:167
  373.6 84.1 %reduce-scatter.2.cloned.1.call-done = bf16[64,4096]{1,0:T(8,128)(2,1)} async-done(((bf16[1024,4096]{1,0:T(8,128)(2,1)}), bf16[64,4096]{1,0:T(8,128)(2,1)}) %reduce-scatter.2.cloned.1.call-update) | async-done | bytes 524304 | tf_op jit(solution)/shard_map/reduce_scatter | solution.py:166
  457.7 2.1 fusion.44
  (42 shorter events, 0.4 us)
Async XLA Ops:
  6.5 171.6 %copy-start = (bf16[256,4096]{1,0:T(8,128)(2,1)S(1)}, bf16[256,4096]{1,0:T(8,128)(2,1)}, u32[]{:S(2)}) copy-start(bf16[256,4096]{1,0:T(8,128)(2,1)} %param.25) | copy-start | bytes 6291460
  6.5 39.3 %copy-start.7 = (s32[1,1024]{1,0:T(1,128)S(1)}, s32[1,1024]{1,0:T(1,128)}, u32[]{:S(2)}) copy-start(s32[1,1024]{1,0:T(1,128)} %param.20) | copy-start | bytes 12292
  6.5 33.3 %all-gather.3.cloned.1.call-start = ((), (), s32[]{:S(2)}) async-start(), calls=%async_computation.1 | async-start | bytes 2396160 | tf_op jit(solution)/shard_map/all_gather | solution.py:98
  11.8 112.8 %all-gather.5.cloned.1.call-start = ((), (), s32[]{:S(2)}) async-start(), calls=%async_computation.2 | async-start | bytes 8912896 | tf_op jit(solution)/shard_map/all_gather | solution.py:120
  43.0 86.6 %copy-start.8 = (f32[4096]{0:T(1024)S(1)}, f32[4096]{0:T(1024)}, u32[]{:S(2)}) copy-start(f32[4096]{0:T(1024)} %param.21) | copy-start | bytes 49156
  45.8 278.8 %all-reduce.3.cloned.1.call-start = ((), (), s32[]{:S(2)}) async-start(), calls=%async_computation.3 | async-start | bytes 16777216 | tf_op jit(solution)/shard_map/psum | solution.py:159
  129.6 10.4 %copy-start.4 = (bf16[4096,64]{0,1:T(8,128)(2,1)S(1)}, bf16[4096,64]{0,1:T(8,128)(2,1)}, u32[]{:S(2)}) copy-start(bf16[4096,64]{0,1:T(8,128)(2,1)} %param.24) | copy-start | bytes 1572868
  140.0 6.2 %copy-start.2 = (bf16[1024,4096]{1,0:T(8,128)(2,1)S(1)}, bf16[1024,4096]{1,0:T(8,128)(2,1)}, u32[]{:S(2)}) copy-start(bf16[1024,4096]{1,0:T(8,128)(2,1)} %fusion.7) | copy-start | bytes 25165828
  140.0 6.2 %copy-start.5 = (bf16[4096,64]{0,1:T(8,128)(2,1)S(1)}, bf16[4096,64]{0,1:T(8,128)(2,1)}, u32[]{:S(2)}) copy-start(bf16[4096,64]{0,1:T(8,128)(2,1)} %param.23) | copy-start | bytes 1572868
  146.3 2.7 copy-start.9
  158.2 7.3 %collective-permute-start = (bf16[1024,128]{0,1:T(8,128)(2,1)S(1)}, bf16[1024,128]{0,1:T(8,128)(2,1)S(1)}, u32[]{:S(2)}, u32[]{:S(2)}) collective-permute-start(bf16[1024,128]{0,1:T(8,128)(2,1)S(1)} %pad_maximum_fusion.2), channel_id=1, source_target_pairs={{0,1},{1,0},{2,3},{3,2},{4,5},{5,4},{6,7},{7,6},{8,9},{9,8},{10,11... | collective-permute-start | bytes 786440 | tf_op jit(solution)/shard_map/ppermute | solution.py:22
  161.6 8.9 %copy-start.6 = (pred[512,1024]{0,1:T(8,128)(4,1)S(1)}, pred[512,1024]{0,1:T(8,128)(4,1)}, u32[]{:S(2)}) copy-start(pred[512,1024]{0,1:T(8,128)(4,1)} %get-tuple-element.50) | copy-start | bytes 1572868
  174.2 3.4 copy-start.11
  183.7 152.1 %copy-start.10 = (f32[4096]{0:T(1024)S(1)}, f32[4096]{0:T(1024)}, u32[]{:S(2)}) copy-start(f32[4096]{0:T(1024)} %param.26) | copy-start | bytes 49156
  183.7 274.0 %reduce-scatter.2.cloned.1.call-start = ((), (), s32[]{:S(2)}) async-start(), calls=%async_computation.4 | async-start | bytes 8912896 | tf_op jit(solution)/shard_map/reduce_scatter | solution.py:166
  332.6 3.2 copy-start.3
  347.1 112.7 %copy-start.1 = (bf16[256,4096]{1,0:T(8,128)(2,1)S(1)}, bf16[256,4096]{1,0:T(8,128)(2,1)}, u32[]{:S(2)}) copy-start(bf16[256,4096]{1,0:T(8,128)(2,1)} %param.25) | copy-start | bytes 6291460
Sparse Core Ops, SparseCore 0:
  11.9 27.8 all-gather.2
  45.9 78.6 all-gather.4
  183.8 140.6 all-reduce.2
  373.7 83.9 reduce-scatter.1

commit v3 on v2

--- a/solution.py
+++ b/solution.py
@@ -95,9 +95,22 @@
     slot_low = (crystal_slot % 128).astype(jnp.bfloat16)
     slot_cols = jnp.zeros((bridge.shape[0], 128), jnp.bfloat16)
     slot_cols = slot_cols.at[:, 0].set(slot_high).at[:, 1].set(slot_low)
-    arrived_all = lax.all_gather(
-        jnp.concatenate([flat_bridge, slot_cols], axis=1), "dp", axis=0, tiled=True
-    )
+    payload = jnp.concatenate([flat_bridge, slot_cols], axis=1)
+    crystal_count = bridge.shape[0]
+    destination = crystal_slot // seq_len
+    crystal_numbers = jnp.arange(crystal_count, dtype=jnp.int32)
+    same_destination = destination[:, None] == destination[None, :]
+    rank = jnp.sum(
+        (same_destination & (crystal_numbers[None, :] < crystal_numbers[:, None])).astype(jnp.int32),
+        axis=1,
+    )
+    per_destination = crystal_count // lax.axis_size("dp")
+    send_row = destination * per_destination + rank
+    sending = crystal_numbers[:, None] == send_row[None, :]
+    outgoing = jnp.dot(
+        sending.astype(jnp.bfloat16), payload, preferred_element_type=jnp.float32
+    ).astype(jnp.bfloat16)
+    arrived_all = lax.all_to_all(outgoing, "dp", 0, 0, tiled=True)
     arrived = arrived_all[:, : bridge_len * part_width]
     arrived_slots = (
         arrived_all[:, -128].astype(jnp.int32) * 128 + arrived_all[:, -127].astype(jnp.int32)

time: 469 us -> 453 us (0.966)
  waiting for transfers between devices: 328 us -> 307 us
  starting transfers between devices: 1.38 us -> 6.77 us
    all_gather x1 -> x0, waiting for transfers between devices: 25.7 us -> none  [shards(): lax.all_gather(jnp.concatenate([flat_bridge, slot_cols], axis=1), 'dp', a...]
    all_to_all x0 -> x1, starting transfers between devices: none -> 5.4 us  [shards(): arrived_all = lax.all_to_all(outgoing, 'dp', 0, 0, tiled=True)]
    all_to_all x0 -> x1, waiting for transfers between devices: none -> 5.23 us  [shards(): arrived_all = lax.all_to_all(outgoing, 'dp', 0, 0, tiled=True)]
where the time goes in v3:
time: 453 us; the launch traced here: 450 us
  waiting for transfers between devices  307 us (68%)
  matrix products  70.8 us (16%)
  other arithmetic  40.6 us (9%)
  between operations  13.9 us (3%)
  local copies, waits for them, and re-layouts  11.2 us (2%)
  starting transfers between devices  6.77 us (1%)
    psum x1, waiting for transfers between devices, shards(): lax.psum(partial_rows.astype(jnp.bfloat16), 'ts').astype(jnp.float32)  141 us
    reduce_scatter x1, waiting for transfers between devices, shards(): lax.psum_scatter(jnp.dot(hidden, w_down, preferred_element_type=jnp.float...  83.9 us
    all_gather x1, waiting for transfers between devices, shards(): packed = lax.all_gather(own_part, 'ts', axis=1, tiled=True)  74.1 us
    dot_general x1, matrix products, shards(): jnp.dot(hidden, w_down, preferred_element_type=jnp.float32)  26.4 us
    reduce_sum x2, other arithmetic, norm_rows(): jnp.mean(widened * widened, axis=-1, keepdims=True) + norm_epsilon  13.1 us
    dot_general x1, matrix products, shards(): up_proj = jnp.dot(normed_mlp, w_up, preferred_element_type=jnp.float32)  11.3 us
    convert_element_type x1, other arithmetic, norm_rows(): return (widened * inverse_rms * gain).astype(jnp.bfloat16)  10.4 us
  transfers between devices with their start and end apart: 5, of which 5 were waited for; matrix products, arithmetic and copies ran while one was open for 2% of the time, Pallas kernels for 0%

profile of v3, /device:TPU:0, one launch (start us, length us, event | category | flops | bytes accessed | tf_op | source)
XLA Modules:
  0.0 450.1 jit_solution(106320310528948666)
XLA Ops:
  6.5 0.7 compare_reduce_fusion.1
  7.3 0.6 compare_reduce_fusion
  7.9 0.7 and_select_fusion.2
  8.6 0.2 convert_reduce_fusion.1
  8.7 0.7 multiply_add_fusion.1
  9.4 2.0 fusion.86
  11.5 1.1 copy.80
  12.7 0.2 convolution_convert_fusion
  12.9 0.8 all_to_all.8
  13.7 5.4 %all-to-all-start = ((bf16[8,2,8320]{2,1,0:T(2,128)(2,1)}), bf16[8,2,8320]{2,1,0:T(2,128)(2,1)S(1)}, u32[]{:S(2)}, u32[]{:S(2)}) async-start(bf16[8,2,8320]{2,1,0:T(2,128)(2,1)} %all_to_all.8), calls=%async_computation | async-start | bytes 532480 | tf_op jit(solution)/shard_map/all_to_all | solution.py:113
  19.1 0.8 convert_reduce_fusion
  19.9 0.8 select_reduce_fusion
  20.7 0.7 fusion.83
  21.4 5.2 %all-to-all-done = bf16[8,2,8320]{2,1,0:T(2,128)(2,1)S(1)} async-done(((bf16[8,2,8320]{2,1,0:T(2,128)(2,1)}), bf16[8,2,8320]{2,1,0:T(2,128)(2,1)S(1)}, u32[]{:S(2)}, u32[]{:S(2)}) %all-to-all-start) | async-done | bytes 266272 | tf_op jit(solution)/shard_map/all_to_all | solution.py:113
  26.8 0.2 add_reduce_fusion
  27.0 0.3 convolution_convert_fusion.1
  27.4 2.7 fusion.36
  30.2 2.0 multiply_cosine_fusion
  32.2 1.6 fusion.22
  33.8 74.1 %all-gather.2.cloned.1.call-done = bf16[1024,4096]{1,0:T(8,128)(2,1)} async-done(((bf16[1024,256]{1,0:T(8,128)(2,1)}), bf16[1024,4096]{1,0:T(8,128)(2,1)}) %all-gather.2.cloned.1.call-update) | async-done | bytes 8388624 | tf_op jit(solution)/shard_map/all_gather | solution.py:133
  108.0 5.1 %fusion.5 = f32[1024]{0:T(1024)S(1)} fusion(bf16[1024,4096]{1,0:T(8,128)(2,1)} %all-gather.2.cloned.1.call-done), kind=kLoop, calls=%fused_computation.10 | loop fusion | flops 12581888 | bytes 8392704 | tf_op jit(solution)/shard_map/reduce_sum | solution.py:27
  113.1 10.4 %fusion.7 = bf16[1024,4096]{1,0:T(8,128)(2,1)} fusion(bf16[1024,4096]{1,0:T(8,128)(2,1)} %all-gather.2.cloned.1.call-done, f32[4096]{0:T(1024)S(1)} %copy-done.8, f32[1024]{0:T(1024)S(1)} %add_rsqrt_fusion.1), kind=kLoop, calls=%fused_computation.12 | loop fusion | flops 16777216 | bytes 16797696 | tf_op jit(solution)/shard_map/convert_element_type | solution.py:28
  123.5 6.2 %convolution_convert_fusion.4 = bf16[1024,64]{0,1:T(8,128)(2,1)S(1)} fusion(bf16[1024,4096]{1,0:T(8,128)(2,1)} %fusion.7, bf16[4096,64]{0,1:T(8,128)(2,1)S(1)} %copy-done.4), kind=kOutput, calls=%fused_computation.49 | convolution fusion | flops 536936448 | bytes 9043968 | tf_op jit(solution)/shard_map/dot_general | solution.py:147
  129.7 2.7 fusion.113
  132.4 3.7 fusion.114
  136.1 1.8 reshape_reshape.7
  137.9 0.9 reshape_reshape.6
  138.8 1.3 fusion.101
  140.0 0.6 fusion.75
  140.6 0.1 copy.61
  140.8 0.8 fusion.98
  141.7 1.3 collective-permute-start
  142.9 2.1 subtract_convert_fusion
  145.0 1.2 fusion.54
  146.3 2.7 collective-permute-done
  149.1 4.8 %fusion.108 = (f32[2,512]{1,0:T(2,128)S(1)}, f32[2,512,1024]{1,2,0:T(8,128)}) fusion(pred[512,1024]{0,1:T(8,128)(4,1)} %get-tuple-element.49, bf16[512,2,128]{0,1,2:T(2,128)(2,1)} %bitcast.88, bf16[1024,64]{0,1:T(8,128)(2,1)S(1)} %get-tuple-element.61, bf16[1024,64]{0,1:T(8,128)(2,1)S(1)} %get-tuple-element.42), kind=kOutput, calls=%fused_computation.149 | convolution fusion | flops 273155072 | bytes 5246976 | tf_op jit(solution)/shard_map/sub | solution.py:56
  153.9 3.7 fusion.103
  157.6 2.8 fusion.40
  160.4 0.7 copy-done.11
  161.1 0.5 fusion.39
  161.6 5.6 %convolution_convert_fusion.3 = bf16[1024,4096]{1,0:T(8,128)(2,1)} fusion(bf16[256,4096]{1,0:T(8,128)(2,1)S(1)} %copy-done, bf16[512,256]{0,1:T(8,128)(2,1)S(1)} %bitcast.85, bf16[512,256]{0,1:T(8,128)(2,1)S(1)} %bitcast.84), kind=kOutput, calls=%fused_computation.17 | convolution fusion | flops 2152726528 | bytes 11010048 | tf_op jit(solution)/shard_map/dot_general | solution.py:171
  167.3 140.8 %all-reduce.3.cloned.1.call-done = bf16[1024,4096]{1,0:T(8,128)(2,1)} async-done(((bf16[1024,4096]{1,0:T(8,128)(2,1)}), bf16[1024,4096]{1,0:T(8,128)(2,1)}) %all-reduce.3.cloned.1.call-update) | async-done | bytes 8388624 | tf_op jit(solution)/shard_map/psum | solution.py:172
  308.1 8.1 %fusion.2 = (f32[1024]{0:T(1024)S(1)}, bf16[1024,4096]{1,0:T(8,128)(2,1)S(1)}) fusion(bf16[1024,4096]{1,0:T(8,128)(2,1)} %all-reduce.3.cloned.1.call-done, bf16[1024,4096]{1,0:T(8,128)(2,1)} %all-gather.2.cloned.1.call-done), kind=kLoop, calls=%fused_computation.7 | loop fusion | flops 29359104 | bytes 25169920 | tf_op jit(solution)/shard_map/reduce_sum | solution.py:27
  316.2 3.2 copy-done.3
  319.4 11.3 %fusion.11 = f32[1024,768]{1,0:T(8,128)} fusion(bf16[4096,768]{1,0:T(8,128)(2,1)} %param.28, bf16[1024,4096]{1,0:T(8,128)(2,1)S(1)} %get-tuple-element.30, f32[4096]{0:T(1024)S(1)} %copy-done.10, f32[1024]{0:T(1024)S(1)} %add_rsqrt_fusion), kind=kOutput, calls=%fused_computation.27 | convolution fusion | flops 6459228160 | bytes 17846272 | tf_op jit(solution)/shard_map/dot_general | solution.py:177
  330.6 26.4 %convolution_convert_fusion.2 = bf16[1024,4096]{1,0:T(8,128)(2,1)} fusion(bf16[768,4096]{1,0:T(8,128)(2,1)} %param.29, f32[1024,768]{1,0:T(8,128)} %fusion.11, bf16[4096,768]{1,0:T(8,128)(2,1)} %param.27, bf16[1024,4096]{1,0:T(8,128)(2,1)} %copy-done.3, f32[4096]{0:T(1024)S(1)} %copy-done.10, f32[1024]{0:T(1024)S(1)} %add_rsqrt_fusion), kind=kOutput, calls=%fused_computation.16 | convolution fusion | flops 12910592000 | bytes 32526336 | tf_op jit(solution)/shard_map/dot_general | solution.py:180
  357.1 83.9 %reduce-scatter.2.cloned.1.call-done = bf16[64,4096]{1,0:T(8,128)(2,1)} async-done(((bf16[1024,4096]{1,0:T(8,128)(2,1)}), bf16[64,4096]{1,0:T(8,128)(2,1)}) %reduce-scatter.2.cloned.1.call-update) | async-done | bytes 524304 | tf_op jit(solution)/shard_map/reduce_scatter | solution.py:179
  441.0 2.1 fusion.43
  (46 shorter events, 0.8 us)
Async XLA Ops:
  6.5 155.0 %copy-start = (bf16[256,4096]{1,0:T(8,128)(2,1)S(1)}, bf16[256,4096]{1,0:T(8,128)(2,1)}, u32[]{:S(2)}) copy-start(bf16[256,4096]{1,0:T(8,128)(2,1)} %param.25) | copy-start | bytes 6291460
  6.5 23.7 %copy-start.7 = (s32[1,1024]{1,0:T(1,128)S(1)}, s32[1,1024]{1,0:T(1,128)}, u32[]{:S(2)}) copy-start(s32[1,1024]{1,0:T(1,128)} %param.20) | copy-start | bytes 12292
  13.7 13.0 %all-to-all-start = ((bf16[8,2,8320]{2,1,0:T(2,128)(2,1)}), bf16[8,2,8320]{2,1,0:T(2,128)(2,1)S(1)}, u32[]{:S(2)}, u32[]{:S(2)}) async-start(bf16[8,2,8320]{2,1,0:T(2,128)(2,1)} %all_to_all.8), calls=%async_computation | async-start | bytes 532480 | tf_op jit(solution)/shard_map/all_to_all | solution.py:113
  19.1 88.9 %all-gather.2.cloned.1.call-start = ((), (), s32[]{:S(2)}) async-start(), calls=%async_computation.2 | async-start | bytes 8912896 | tf_op jit(solution)/shard_map/all_gather | solution.py:133
  27.4 85.7 %copy-start.8 = (f32[4096]{0:T(1024)S(1)}, f32[4096]{0:T(1024)}, u32[]{:S(2)}) copy-start(f32[4096]{0:T(1024)} %param.21) | copy-start | bytes 49156
  30.1 278.0 %all-reduce.3.cloned.1.call-start = ((), (), s32[]{:S(2)}) async-start(), calls=%async_computation.3 | async-start | bytes 16777216 | tf_op jit(solution)/shard_map/psum | solution.py:172
  113.1 10.4 %copy-start.4 = (bf16[4096,64]{0,1:T(8,128)(2,1)S(1)}, bf16[4096,64]{0,1:T(8,128)(2,1)}, u32[]{:S(2)}) copy-start(bf16[4096,64]{0,1:T(8,128)(2,1)} %param.24) | copy-start | bytes 1572868
  123.5 6.2 %copy-start.2 = (bf16[1024,4096]{1,0:T(8,128)(2,1)S(1)}, bf16[1024,4096]{1,0:T(8,128)(2,1)}, u32[]{:S(2)}) copy-start(bf16[1024,4096]{1,0:T(8,128)(2,1)} %fusion.7) | copy-start | bytes 25165828
  123.5 6.2 %copy-start.5 = (bf16[4096,64]{0,1:T(8,128)(2,1)S(1)}, bf16[4096,64]{0,1:T(8,128)(2,1)}, u32[]{:S(2)}) copy-start(bf16[4096,64]{0,1:T(8,128)(2,1)} %param.23) | copy-start | bytes 1572868
  129.7 2.7 copy-start.9
  141.7 7.3 %collective-permute-start = (bf16[1024,128]{0,1:T(8,128)(2,1)S(1)}, bf16[1024,128]{0,1:T(8,128)(2,1)S(1)}, u32[]{:S(2)}, u32[]{:S(2)}) collective-permute-start(bf16[1024,128]{0,1:T(8,128)(2,1)S(1)} %pad_maximum_fusion.1), channel_id=1, source_target_pairs={{0,1},{1,0},{2,3},{3,2},{4,5},{5,4},{6,7},{7,6},{8,9},{9,8},{10,11... | collective-permute-start | bytes 786440 | tf_op jit(solution)/shard_map/ppermute | solution.py:22
  145.0 8.9 %copy-start.6 = (pred[512,1024]{0,1:T(8,128)(4,1)S(1)}, pred[512,1024]{0,1:T(8,128)(4,1)}, u32[]{:S(2)}) copy-start(pred[512,1024]{0,1:T(8,128)(4,1)} %get-tuple-element.50) | copy-start | bytes 1572868
  157.6 3.4 copy-start.11
  167.2 152.2 %copy-start.10 = (f32[4096]{0:T(1024)S(1)}, f32[4096]{0:T(1024)}, u32[]{:S(2)}) copy-start(f32[4096]{0:T(1024)} %param.26) | copy-start | bytes 49156
  167.2 273.8 %reduce-scatter.2.cloned.1.call-start = ((), (), s32[]{:S(2)}) async-start(), calls=%async_computation.4 | async-start | bytes 8912896 | tf_op jit(solution)/shard_map/reduce_scatter | solution.py:179
  316.1 3.2 copy-start.3
  330.6 112.5 %copy-start.1 = (bf16[256,4096]{1,0:T(8,128)(2,1)S(1)}, bf16[256,4096]{1,0:T(8,128)(2,1)}, u32[]{:S(2)}) copy-start(bf16[256,4096]{1,0:T(8,128)(2,1)} %param.25) | copy-start | bytes 6291460
Sparse Core Ops, SparseCore 0:
  30.2 77.7 all-gather.1
  167.3 140.6 all-reduce.2
  357.2 83.7 reduce-scatter.1

commit v4 on v3

--- a/solution.py
+++ b/solution.py
@@ -131,6 +131,7 @@
     ).astype(jnp.bfloat16)
     own_part = jnp.where(in_bridge[:, None], filled, text_embed[0])
     packed = lax.all_gather(own_part, "ts", axis=1, tiled=True)
+    positions = lax.optimization_barrier((own_part, positions))[1]
     normed = norm_rows(packed, attn_gain)
     heads_here = w_query.shape[1] // HD
     queries = jnp.dot(normed, w_query, preferred_element_type=jnp.float32).reshape(
@@ -155,15 +156,16 @@
     outputs = []
     for block_index in range(seq_len // block_rows):
         first_row = block_index * block_rows
-        query_index = jnp.arange(first_row, first_row + block_rows, dtype=jnp.int32)
+        end_row = first_row + block_rows
+        query_index = jnp.arange(first_row, end_row, dtype=jnp.int32)
         outputs.append(
             attend_block(
-                queries[first_row : first_row + block_rows],
-                segment_ids[first_row : first_row + block_rows],
+                queries[first_row:end_row],
+                segment_ids[first_row:end_row],
                 query_index,
-                keys_full,
-                values_full,
-                segment_ids,
+                keys_full[:end_row],
+                values_full[:end_row],
+                segment_ids[:end_row],
             )
         )
     attended = jnp.concatenate(outputs, axis=0)

time: 453 us -> 452 us (level)
  no operation moved by 1% of the time
where the time goes in v4:
time: 452 us; the launch traced here: 448 us
  waiting for transfers between devices  306 us (68%)
  matrix products  68.4 us (15%)
  other arithmetic  41.1 us (9%)
  between operations  13.9 us (3%)
  local copies, waits for them, and re-layouts  11.5 us (3%)
  starting transfers between devices  6.77 us (1%)
    psum x1, waiting for transfers between devices, shards(): lax.psum(partial_rows.astype(jnp.bfloat16), 'ts').astype(jnp.float32)  141 us
    reduce_scatter x1, waiting for transfers between devices, shards(): lax.psum_scatter(jnp.dot(hidden, w_down, preferred_element_type=jnp.float...  84.1 us
    all_gather x1, waiting for transfers between devices, shards(): packed = lax.all_gather(own_part, 'ts', axis=1, tiled=True)  73.7 us
    dot_general x1, matrix products, shards(): jnp.dot(hidden, w_down, preferred_element_type=jnp.float32)  26.4 us
    reduce_sum x2, other arithmetic, norm_rows(): jnp.mean(widened * widened, axis=-1, keepdims=True) + norm_epsilon  13.1 us
    dot_general x1, matrix products, shards(): up_proj = jnp.dot(normed_mlp, w_up, preferred_element_type=jnp.float32)  11.3 us
    convert_element_type x1, other arithmetic, norm_rows(): return (widened * inverse_rms * gain).astype(jnp.bfloat16)  10.4 us
  transfers between devices with their start and end apart: 5, of which 5 were waited for; matrix products, arithmetic and copies ran while one was open for 2% of the time, Pallas kernels for 0%

profile of v4, /device:TPU:0, one launch (start us, length us, event | category | flops | bytes accessed | tf_op | source)
XLA Modules:
  0.0 448.2 jit_solution(7053417941443892095)
XLA Ops:
  6.5 0.7 compare_reduce_fusion.1
  7.3 0.6 compare_reduce_fusion
  7.9 0.7 and_select_fusion.2
  8.6 0.2 convert_reduce_fusion.1
  8.7 0.7 multiply_add_fusion.1
  9.4 2.0 fusion.98
  11.5 1.1 copy.80
  12.7 0.2 convolution_convert_fusion
  12.9 0.8 all_to_all.8
  13.7 5.4 %all-to-all-start = ((bf16[8,2,8320]{2,1,0:T(2,128)(2,1)}), bf16[8,2,8320]{2,1,0:T(2,128)(2,1)S(1)}, u32[]{:S(2)}, u32[]{:S(2)}) async-start(bf16[8,2,8320]{2,1,0:T(2,128)(2,1)} %all_to_all.8), calls=%async_computation | async-start | bytes 532480 | tf_op jit(solution)/shard_map/all_to_all | solution.py:113
  19.1 0.8 convert_reduce_fusion
  19.9 0.8 select_reduce_fusion
  20.7 0.7 iota_subtract_fusion
  21.4 5.2 %all-to-all-done = bf16[8,2,8320]{2,1,0:T(2,128)(2,1)S(1)} async-done(((bf16[8,2,8320]{2,1,0:T(2,128)(2,1)}), bf16[8,2,8320]{2,1,0:T(2,128)(2,1)S(1)}, u32[]{:S(2)}, u32[]{:S(2)}) %all-to-all-start) | async-done | bytes 266272 | tf_op jit(solution)/shard_map/all_to_all | solution.py:113
  26.8 0.2 add_reduce_fusion
  27.0 0.3 convolution_convert_fusion.1
  27.4 2.7 fusion.31
  30.2 0.9 fusion.39
  31.1 1.3 fusion.19
  32.4 1.9 multiply_cosine_fusion
  34.3 73.7 %all-gather.2.cloned.1.call-done = bf16[1024,4096]{1,0:T(8,128)(2,1)} async-done(((bf16[1024,256]{1,0:T(8,128)(2,1)}), bf16[1024,4096]{1,0:T(8,128)(2,1)}) %all-gather.2.cloned.1.call-update) | async-done | bytes 8388624 | tf_op jit(solution)/shard_map/all_gather | solution.py:133
  108.0 5.1 %fusion.5 = f32[1024]{0:T(1024)S(1)} fusion(bf16[1024,4096]{1,0:T(8,128)(2,1)} %all-gather.2.cloned.1.call-done), kind=kLoop, calls=%fused_computation.10 | loop fusion | flops 12581888 | bytes 8392704 | tf_op jit(solution)/shard_map/reduce_sum | solution.py:27
  113.1 10.4 %fusion.7 = bf16[1024,4096]{1,0:T(8,128)(2,1)} fusion(bf16[1024,4096]{1,0:T(8,128)(2,1)} %all-gather.2.cloned.1.call-done, f32[4096]{0:T(1024)S(1)} %copy-done.8, f32[1024]{0:T(1024)S(1)} %add_rsqrt_fusion.1), kind=kLoop, calls=%fused_computation.12 | loop fusion | flops 16777216 | bytes 16797696 | tf_op jit(solution)/shard_map/convert_element_type | solution.py:28
  123.5 6.2 %convolution_convert_fusion.5 = bf16[1024,64]{0,1:T(8,128)(2,1)S(1)} fusion(bf16[1024,4096]{1,0:T(8,128)(2,1)} %fusion.7, bf16[4096,64]{0,1:T(8,128)(2,1)S(1)} %copy-done.4), kind=kOutput, calls=%fused_computation.43 | convolution fusion | flops 536936448 | bytes 9043968 | tf_op jit(solution)/shard_map/dot_general | solution.py:148
  129.7 2.7 fusion.136
  132.4 3.5 fusion.137
  135.9 1.8 reshape_reshape.7
  137.7 1.1 reshape_reshape.6
  138.8 1.3 fusion.120
  140.0 0.6 fusion.77
  140.8 0.8 fusion.117
  141.7 1.3 collective-permute-start
  143.0 2.1 subtract_convert_fusion
  145.0 1.2 fusion.50
  146.3 2.7 collective-permute-done
  149.1 3.4 fusion.131
  152.5 3.7 fusion.122
  156.2 2.1 convolution_convert_fusion.4
  158.3 0.8 copy-done.11
  159.0 0.5 fusion.34
  159.5 5.6 %convolution_convert_fusion.3 = bf16[1024,4096]{1,0:T(8,128)(2,1)} fusion(bf16[256,4096]{1,0:T(8,128)(2,1)S(1)} %copy-done, bf16[512,256]{0,1:T(8,128)(2,1)S(1)} %bitcast.83, bf16[512,256]{0,1:T(8,128)(2,1)S(1)} %bitcast.82), kind=kOutput, calls=%fused_computation.17 | convolution fusion | flops 2152726528 | bytes 11010048 | tf_op jit(solution)/shard_map/dot_general | solution.py:173
  165.2 140.8 %all-reduce.3.cloned.1.call-done = bf16[1024,4096]{1,0:T(8,128)(2,1)} async-done(((bf16[1024,4096]{1,0:T(8,128)(2,1)}), bf16[1024,4096]{1,0:T(8,128)(2,1)}) %all-reduce.3.cloned.1.call-update) | async-done | bytes 8388624 | tf_op jit(solution)/shard_map/psum | solution.py:174
  306.0 8.1 %fusion.2 = (f32[1024]{0:T(1024)S(1)}, bf16[1024,4096]{1,0:T(8,128)(2,1)S(1)}) fusion(bf16[1024,4096]{1,0:T(8,128)(2,1)} %all-reduce.3.cloned.1.call-done, bf16[1024,4096]{1,0:T(8,128)(2,1)} %all-gather.2.cloned.1.call-done), kind=kLoop, calls=%fused_computation.7 | loop fusion | flops 29359104 | bytes 25169920 | tf_op jit(solution)/shard_map/reduce_sum | solution.py:27
  314.1 3.2 copy-done.3
  317.3 11.3 %fusion.10 = f32[1024,768]{1,0:T(8,128)} fusion(bf16[4096,768]{1,0:T(8,128)(2,1)} %param.28, bf16[1024,4096]{1,0:T(8,128)(2,1)S(1)} %get-tuple-element.32, f32[4096]{0:T(1024)S(1)} %copy-done.10, f32[1024]{0:T(1024)S(1)} %add_rsqrt_fusion), kind=kOutput, calls=%fused_computation.23 | convolution fusion | flops 6459228160 | bytes 17846272 | tf_op jit(solution)/shard_map/dot_general | solution.py:179
  328.6 26.4 %convolution_convert_fusion.2 = bf16[1024,4096]{1,0:T(8,128)(2,1)} fusion(bf16[768,4096]{1,0:T(8,128)(2,1)} %param.29, f32[1024,768]{1,0:T(8,128)} %fusion.10, bf16[4096,768]{1,0:T(8,128)(2,1)} %param.27, bf16[1024,4096]{1,0:T(8,128)(2,1)} %copy-done.3, f32[4096]{0:T(1024)S(1)} %copy-done.10, f32[1024]{0:T(1024)S(1)} %add_rsqrt_fusion), kind=kOutput, calls=%fused_computation.16 | convolution fusion | flops 12910592000 | bytes 32526336 | tf_op jit(solution)/shard_map/dot_general | solution.py:182
  355.0 84.1 %reduce-scatter.2.cloned.1.call-done = bf16[64,4096]{1,0:T(8,128)(2,1)} async-done(((bf16[1024,4096]{1,0:T(8,128)(2,1)}), bf16[64,4096]{1,0:T(8,128)(2,1)}) %reduce-scatter.2.cloned.1.call-update) | async-done | bytes 524304 | tf_op jit(solution)/shard_map/reduce_scatter | solution.py:181
  439.1 2.1 fusion.41
  (48 shorter events, 1.0 us)
Async XLA Ops:
  6.5 153.0 %copy-start = (bf16[256,4096]{1,0:T(8,128)(2,1)S(1)}, bf16[256,4096]{1,0:T(8,128)(2,1)}, u32[]{:S(2)}) copy-start(bf16[256,4096]{1,0:T(8,128)(2,1)} %param.25) | copy-start | bytes 6291460
  6.5 23.7 %copy-start.7 = (s32[1,1024]{1,0:T(1,128)S(1)}, s32[1,1024]{1,0:T(1,128)}, u32[]{:S(2)}) copy-start(s32[1,1024]{1,0:T(1,128)} %param.20) | copy-start | bytes 12292
  13.7 13.0 %all-to-all-start = ((bf16[8,2,8320]{2,1,0:T(2,128)(2,1)}), bf16[8,2,8320]{2,1,0:T(2,128)(2,1)S(1)}, u32[]{:S(2)}, u32[]{:S(2)}) async-start(bf16[8,2,8320]{2,1,0:T(2,128)(2,1)} %all_to_all.8), calls=%async_computation | async-start | bytes 532480 | tf_op jit(solution)/shard_map/all_to_all | solution.py:113
  19.1 88.9 %all-gather.2.cloned.1.call-start = ((), (), s32[]{:S(2)}) async-start(), calls=%async_computation.2 | async-start | bytes 8912896 | tf_op jit(solution)/shard_map/all_gather | solution.py:133
  27.4 85.7 %copy-start.8 = (f32[4096]{0:T(1024)S(1)}, f32[4096]{0:T(1024)}, u32[]{:S(2)}) copy-start(f32[4096]{0:T(1024)} %param.21) | copy-start | bytes 49156
  30.1 275.9 %all-reduce.3.cloned.1.call-start = ((), (), s32[]{:S(2)}) async-start(), calls=%async_computation.3 | async-start | bytes 16777216 | tf_op jit(solution)/shard_map/psum | solution.py:174
  113.1 10.4 %copy-start.4 = (bf16[4096,64]{0,1:T(8,128)(2,1)S(1)}, bf16[4096,64]{0,1:T(8,128)(2,1)}, u32[]{:S(2)}) copy-start(bf16[4096,64]{0,1:T(8,128)(2,1)} %param.24) | copy-start | bytes 1572868
  123.5 6.2 %copy-start.2 = (bf16[1024,4096]{1,0:T(8,128)(2,1)S(1)}, bf16[1024,4096]{1,0:T(8,128)(2,1)}, u32[]{:S(2)}) copy-start(bf16[1024,4096]{1,0:T(8,128)(2,1)} %fusion.7) | copy-start | bytes 25165828
  123.5 6.2 %copy-start.5 = (bf16[4096,64]{0,1:T(8,128)(2,1)S(1)}, bf16[4096,64]{0,1:T(8,128)(2,1)}, u32[]{:S(2)}) copy-start(bf16[4096,64]{0,1:T(8,128)(2,1)} %param.23) | copy-start | bytes 1572868
  129.7 2.7 copy-start.9
  141.7 10.8 %copy-start.6 = (pred[512,1024]{0,1:T(8,128)(4,1)S(1)}, pred[512,1024]{0,1:T(8,128)(4,1)}, u32[]{:S(2)}) copy-start(pred[512,1024]{0,1:T(8,128)(4,1)} %fusion.19) | copy-start | bytes 1572868
  141.7 7.3 %collective-permute-start = (bf16[1024,128]{0,1:T(8,128)(2,1)S(1)}, bf16[1024,128]{0,1:T(8,128)(2,1)S(1)}, u32[]{:S(2)}, u32[]{:S(2)}) collective-permute-start(bf16[1024,128]{0,1:T(8,128)(2,1)S(1)} %pad_maximum_fusion.3), channel_id=1, source_target_pairs={{0,1},{1,0},{2,3},{3,2},{4,5},{5,4},{6,7},{7,6},{8,9},{9,8},{10,11... | collective-permute-start | bytes 786440 | tf_op jit(solution)/shard_map/ppermute | solution.py:22
  156.2 2.8 copy-start.11
  165.1 152.1 %copy-start.10 = (f32[4096]{0:T(1024)S(1)}, f32[4096]{0:T(1024)}, u32[]{:S(2)}) copy-start(f32[4096]{0:T(1024)} %param.26) | copy-start | bytes 49156
  165.1 273.9 %reduce-scatter.2.cloned.1.call-start = ((), (), s32[]{:S(2)}) async-start(), calls=%async_computation.4 | async-start | bytes 8912896 | tf_op jit(solution)/shard_map/reduce_scatter | solution.py:181
  314.0 3.2 copy-start.3
  328.6 112.7 %copy-start.1 = (bf16[256,4096]{1,0:T(8,128)(2,1)S(1)}, bf16[256,4096]{1,0:T(8,128)(2,1)}, u32[]{:S(2)}) copy-start(bf16[256,4096]{1,0:T(8,128)(2,1)} %param.25) | copy-start | bytes 6291460
Sparse Core Ops, SparseCore 0:
  30.2 77.7 all-gather.1
  165.3 140.6 all-reduce.2
  355.1 83.9 reduce-scatter.1

commit v5 on v4

--- a/solution.py
+++ b/solution.py
@@ -130,22 +130,38 @@
         row_pick.astype(jnp.bfloat16), by_doc, preferred_element_type=jnp.float32
     ).astype(jnp.bfloat16)
     own_part = jnp.where(in_bridge[:, None], filled, text_embed[0])
-    packed = lax.all_gather(own_part, "ts", axis=1, tiled=True)
+    ts_count = lax.axis_size("ts")
+    stacked = lax.all_gather(own_part, "ts", axis=0, tiled=False)
     positions = lax.optimization_barrier((own_part, positions))[1]
-    normed = norm_rows(packed, attn_gain)
+    packed = lax.optimization_barrier(
+        stacked.transpose(1, 0, 2).reshape(seq_len, ts_count * part_width)
+    )
+    widened = stacked.astype(jnp.float32)
+    square_sum = jnp.sum(jnp.sum(widened * widened, axis=2), axis=0)
+    inverse_rms = lax.rsqrt(square_sum / (ts_count * part_width) + norm_epsilon)
+    normed = (
+        widened * inverse_rms[None, :, None] * attn_gain.reshape(ts_count, 1, part_width)
+    ).astype(jnp.bfloat16)
+
+    def project(weight):
+        return jnp.einsum(
+            "srk,skn->rn",
+            normed,
+            weight.reshape(ts_count, part_width, weight.shape[1]),
+            preferred_element_type=jnp.float32,
+        )
+
     heads_here = w_query.shape[1] // HD
-    queries = jnp.dot(normed, w_query, preferred_element_type=jnp.float32).reshape(
-        seq_len, heads_here, HD
-    )
+    queries = project(w_query).reshape(seq_len, heads_here, HD)
     queries = rotate_pairs(queries, positions, 0).astype(jnp.bfloat16)
     kv_cols = w_key.shape[1]
     upper_half = ts_index % 2 == 1
-    key_half = jnp.dot(normed, w_key, preferred_element_type=jnp.float32).reshape(
+    key_half = project(w_key).reshape(
         seq_len, 1, kv_cols
     )
     key_half = rotate_pairs(key_half, positions, ts_index % 2 * (kv_cols // 2))
     key_half = key_half.astype(jnp.bfloat16).reshape(seq_len, kv_cols)
-    value_half = jnp.dot(normed, w_value, preferred_element_type=jnp.float32).astype(jnp.bfloat16)
+    value_half = project(w_value).astype(jnp.bfloat16)
     own_pair = jnp.concatenate([key_half, value_half], axis=1)
     partner = partner_2(own_pair, "ts", 0)
     lower_half = jnp.where(upper_half, partner, own_pair)

time: 452 us -> 429 us (0.949)
  waiting for transfers between devices: 306 us -> 284 us
  other arithmetic: 41.1 us -> 25.9 us
  local copies, waits for them, and re-layouts: 11.5 us -> 21.8 us
  matrix products: 68.4 us -> 75.6 us
    reshape x0 -> x2, local copies, waits for them, and re-layouts: none -> 12.6 us  [the longest x1 7.93 us: shards(): stacked.transpose(1, 0, 2).reshape(seq_len, ts_count * part_width)]
    all_gather x1, waiting for transfers between devices: 73.7 us -> 62.1 us  [shards(): stacked = lax.all_gather(own_part, 'ts', axis=0, tiled=False)]
    convert_element_type x1 -> x0, other arithmetic: 10.4 us -> none  [norm_rows(): return (widened * inverse_rms * gain).astype(jnp.bfloat16)]
    psum x1, waiting for transfers between devices: 141 us -> 133 us  [shards(): lax.psum(partial_rows.astype(jnp.bfloat16), 'ts').astype(jnp.float32)]
    dot_general x3, matrix products: 12.3 us -> 18.7 us  [project(): jnp.einsum('srk,skn->rn', normed, weight.reshape(ts_count, part_width, we...]
    reduce_sum x2 -> x1, other arithmetic: 13.1 us -> 7.87 us  [norm_rows(): jnp.mean(widened * widened, axis=-1, keepdims=True) + norm_epsilon]
    reduce_sum x0 -> x1, other arithmetic: none -> 5.22 us  [shards(): square_sum = jnp.sum(jnp.sum(widened * widened, axis=2), axis=0)]
  transfers between devices with their start and end apart: 5 -> 5, of which waited for: 5 -> 4; matrix products, arithmetic and copies ran while one was open for 2% -> 6% of each run, Pallas kernels for 0% -> 0%
where the time goes in v5:
time: 429 us; the launch traced here: 428 us
  waiting for transfers between devices  284 us (66%)
  matrix products  75.6 us (18%)
  other arithmetic  25.9 us (6%)
  local copies, waits for them, and re-layouts  21.8 us (5%)
  between operations  13.4 us (3%)
  starting transfers between devices  7.24 us (2%)
    psum x1, waiting for transfers between devices, shards(): lax.psum(partial_rows.astype(jnp.bfloat16), 'ts').astype(jnp.float32)  133 us
    reduce_scatter x1, waiting for transfers between devices, shards(): lax.psum_scatter(jnp.dot(hidden, w_down, preferred_element_type=jnp.float...  84.1 us
    all_gather x1, waiting for transfers between devices, shards(): stacked = lax.all_gather(own_part, 'ts', axis=0, tiled=False)  62.1 us
    dot_general x1, matrix products, shards(): jnp.dot(hidden, w_down, preferred_element_type=jnp.float32)  26.4 us
    dot_general x3, matrix products, project(): jnp.einsum('srk,skn->rn', normed, weight.reshape(ts_count, part_width, we...  18.7 us
    dot_general x1, matrix products, shards(): up_proj = jnp.dot(normed_mlp, w_up, preferred_element_type=jnp.float32)  11.3 us
  transfers between devices with their start and end apart: 5, of which 4 were waited for; matrix products, arithmetic and copies ran while one was open for 6% of the time, Pallas kernels for 0%

profile of v5, /device:TPU:0, one launch (start us, length us, event | category | flops | bytes accessed | tf_op | source)
XLA Modules:
  0.0 428.3 jit_solution(13390936119666607840)
XLA Ops:
  6.5 0.7 compare_reduce_fusion.1
  7.3 0.6 compare_reduce_fusion
  7.9 0.7 and_select_fusion.2
  8.6 0.2 convert_reduce_fusion.1
  8.7 0.7 multiply_add_fusion.1
  9.4 2.0 fusion.114
  11.5 1.1 copy.79
  12.7 0.2 convolution_convert_fusion
  12.9 0.8 all_to_all.8
  13.7 5.4 %all-to-all-start = ((bf16[8,2,8320]{2,1,0:T(2,128)(2,1)}), bf16[8,2,8320]{2,1,0:T(2,128)(2,1)S(1)}, u32[]{:S(2)}, u32[]{:S(2)}) async-start(bf16[8,2,8320]{2,1,0:T(2,128)(2,1)} %all_to_all.8), calls=%async_computation | async-start | bytes 532480 | tf_op jit(solution)/shard_map/all_to_all | solution.py:113
  19.1 0.8 convert_reduce_fusion
  19.9 0.8 select_reduce_fusion
  20.7 0.7 iota_subtract_fusion
  21.4 5.2 %all-to-all-done = bf16[8,2,8320]{2,1,0:T(2,128)(2,1)S(1)} async-done(((bf16[8,2,8320]{2,1,0:T(2,128)(2,1)}), bf16[8,2,8320]{2,1,0:T(2,128)(2,1)S(1)}, u32[]{:S(2)}, u32[]{:S(2)}) %all-to-all-start) | async-done | bytes 266272 | tf_op jit(solution)/shard_map/all_to_all | solution.py:113
  26.8 0.2 add_reduce_fusion
  27.0 0.3 convolution_convert_fusion.1
  27.4 2.7 fusion.40
  30.2 0.9 copy.80
  31.1 4.7 %copy.75 = bf16[16,256,256]{1,0,2:T(8,128)(2,1)} copy(bf16[16,256,256]{2,1,0:T(8,128)(2,1)} %bitcast.126) | data formatting | bytes 4194304 | tf_op jit(solution)/shard_map/reshape | solution.py:150
  35.9 0.9 fusion.52
  36.8 0.5 fusion.23
  37.3 1.0 multiply_cosine_fusion
  38.2 62.1 %all-gather.3.cloned.1.call-done = bf16[16384,256]{1,0:T(8,128)(2,1)} async-done(((bf16[1024,256]{1,0:T(8,128)(2,1)}), bf16[16384,256]{1,0:T(8,128)(2,1)}) %all-gather.3.cloned.1.call-update) | async-done | bytes 8388624 | tf_op jit(solution)/shard_map/all_gather | solution.py:134
  100.4 5.2 %fusion.2 = f32[1024]{0:T(1024)S(1)} fusion(bf16[16,1024,256]{2,1,0:T(8,128)(2,1)} %bitcast.123), kind=kLoop, calls=%fused_computation.6 | loop fusion | flops 12581888 | bytes 8392704 | tf_op jit(solution)/shard_map/reduce_sum | solution.py:140
  105.6 0.5 copy-done.2
  106.2 4.0 fusion.44
  110.2 0.6 fusion.93
  111.0 6.3 %fusion.47 = bf16[1024,64]{0,1:T(8,128)(2,1)S(1)} fusion(bf16[8,16,8,256]{3,2,1,0:T(8,128)(2,1)} %bitcast.142, f32[16,256]{1,0:T(8,128)S(1)} %mul.207, f32[1024]{0:T(1024)S(1)} %add_rsqrt_fusion.1, bf16[16384,256]{1,0:T(8,128)(2,1)} %all-gather.3.cloned.1.call-done), kind=kOutput, calls=%fused_computation.50 | convolution fusion | flops 553713664 | bytes 9064448 | tf_op jit(solution)/shard_map/srk,skn->rn/dot_general | solution.py:147
  117.3 1.7 collective-permute-start
  119.1 8.4 %fusion.32 = f32[1024,2,64,2]{0,2,3,1:T(8,128)S(1)} fusion(bf16[2,64,2,256,16]{3,4,2,1,0:T(8,128)(2,1)S(1)} %bitcast.127, f32[16,256]{1,0:T(8,128)S(1)} %mul.207, f32[1024]{0:T(1024)S(1)} %add_rsqrt_fusion.1, bf16[16384,256]{1,0:T(8,128)(2,1)} %all-gather.3.cloned.1.call-done), kind=kOutput, calls=%fused_computation.43 | convolution fusion | flops 2164260864 | bytes 11554816 | tf_op jit(solution)/shard_map/srk,skn->rn/dot_general | solution.py:147
  127.4 0.2 subtract_convert_fusion
  127.7 0.3 copy.59
  127.9 0.3 copy.63
  128.4 0.8 fusion.135
  129.1 3.2 fusion.147
  132.3 4.7 %fusion.138 = (f32[2,512]{1,0:T(2,128)S(1)}, f32[2,512,1024]{1,2,0:T(8,128)}) fusion(pred[512,1024]{0,1:T(8,128)(4,1)S(1)} %fusion.23, bf16[512,2,128]{0,1,2:T(2,128)(2,1)S(1)} %bitcast.134, bf16[1024,64]{0,1:T(8,128)(2,1)} %get-tuple-element.57, bf16[1024,64]{0,1:T(8,128)(2,1)} %get-tuple-element.42), kind=kOutput, calls=%fused_computation.166 | convolution fusion | flops 273155072 | bytes 5246976 | tf_op jit(solution)/shard_map/sub | solution.py:56
  137.0 2.1 convolution_convert_fusion.4
  139.1 0.8 copy-done.11
  139.8 0.5 fusion.43
  140.3 5.6 %convolution_convert_fusion.3 = bf16[1024,4096]{1,0:T(8,128)(2,1)} fusion(bf16[256,4096]{1,0:T(8,128)(2,1)S(1)} %copy-done, bf16[512,256]{0,1:T(8,128)(2,1)S(1)} %bitcast.132, bf16[512,256]{0,1:T(8,128)(2,1)S(1)} %bitcast.131), kind=kOutput, calls=%fused_computation.20 | convolution fusion | flops 2152726528 | bytes 11010048 | tf_op jit(solution)/shard_map/dot_general | solution.py:189
  146.0 7.9 %copy.78 = bf16[16,128,8,256]{3,2,0,1:T(8,128)(2,1)} copy(bf16[16,128,8,256]{3,2,1,0:T(8,128)(2,1)} %bitcast.124) | data formatting | bytes 16777216 | tf_op jit(solution)/shard_map/reshape | solution.py:137
  153.9 132.9 %all-reduce.3.cloned.1.call-done = bf16[1024,4096]{1,0:T(8,128)(2,1)} async-done(((bf16[1024,4096]{1,0:T(8,128)(2,1)}), bf16[1024,4096]{1,0:T(8,128)(2,1)}) %all-reduce.3.cloned.1.call-update) | async-done | bytes 8388624 | tf_op jit(solution)/shard_map/psum | solution.py:190
  286.8 7.9 %fusion.5 = (f32[1024]{0:T(1024)S(1)}, bf16[1024,4096]{1,0:T(8,128)(2,1)S(1)}) fusion(bf16[1024,4096]{1,0:T(8,128)(2,1)} %all-reduce.3.cloned.1.call-done, bf16[1024,4096]{1,0:T(8,128)(2,1)} %bitcast.125), kind=kLoop, calls=%fused_computation.9 | loop fusion | flops 29359104 | bytes 25169920 | tf_op jit(solution)/shard_map/reduce_sum | solution.py:27
  294.7 3.2 copy-done.3
  297.9 11.3 %fusion.13 = f32[1024,768]{1,0:T(8,128)} fusion(bf16[4096,768]{1,0:T(8,128)(2,1)} %param.28, bf16[1024,4096]{1,0:T(8,128)(2,1)S(1)} %get-tuple-element.32, f32[4096]{0:T(1024)S(1)} %copy-done.10, f32[1024]{0:T(1024)S(1)} %add_rsqrt_fusion), kind=kOutput, calls=%fused_computation.26 | convolution fusion | flops 6459228160 | bytes 17846272 | tf_op jit(solution)/shard_map/dot_general | solution.py:195
  309.2 26.4 %convolution_convert_fusion.2 = bf16[1024,4096]{1,0:T(8,128)(2,1)} fusion(bf16[768,4096]{1,0:T(8,128)(2,1)} %param.29, f32[1024,768]{1,0:T(8,128)} %fusion.13, bf16[4096,768]{1,0:T(8,128)(2,1)} %param.27, bf16[1024,4096]{1,0:T(8,128)(2,1)} %copy-done.3, f32[4096]{0:T(1024)S(1)} %copy-done.10, f32[1024]{0:T(1024)S(1)} %add_rsqrt_fusion), kind=kOutput, calls=%fused_computation.19 | convolution fusion | flops 12910592000 | bytes 32526336 | tf_op jit(solution)/shard_map/dot_general | solution.py:198
  335.6 84.1 %reduce-scatter.2.cloned.1.call-done = bf16[64,4096]{1,0:T(8,128)(2,1)} async-done(((bf16[1024,4096]{1,0:T(8,128)(2,1)}), bf16[64,4096]{1,0:T(8,128)(2,1)}) %reduce-scatter.2.cloned.1.call-update) | async-done | bytes 524304 | tf_op jit(solution)/shard_map/reduce_scatter | solution.py:197
  419.7 2.1 fusion.54
  (49 shorter events, 1.0 us)
Async XLA Ops:
  6.5 133.8 %copy-start = (bf16[256,4096]{1,0:T(8,128)(2,1)S(1)}, bf16[256,4096]{1,0:T(8,128)(2,1)}, u32[]{:S(2)}) copy-start(bf16[256,4096]{1,0:T(8,128)(2,1)} %param.25) | copy-start | bytes 6291460
  6.5 29.3 %copy-start.8 = (s32[1,1024]{1,0:T(1,128)S(1)}, s32[1,1024]{1,0:T(1,128)}, u32[]{:S(2)}) copy-start(s32[1,1024]{1,0:T(1,128)} %param.20) | copy-start | bytes 12292
  6.5 23.6 %copy-start.9 = (f32[4096]{0:T(1024)S(1)}, f32[4096]{0:T(1024)}, u32[]{:S(2)}) copy-start(f32[4096]{0:T(1024)} %param.21) | copy-start | bytes 49156
  6.5 23.7 %copy-start.5 = (bf16[4096,64]{0,1:T(8,128)(2,1)S(1)}, bf16[4096,64]{0,1:T(8,128)(2,1)}, u32[]{:S(2)}) copy-start(bf16[4096,64]{0,1:T(8,128)(2,1)} %param.23) | copy-start | bytes 1572868
  13.7 13.0 %all-to-all-start = ((bf16[8,2,8320]{2,1,0:T(2,128)(2,1)}), bf16[8,2,8320]{2,1,0:T(2,128)(2,1)S(1)}, u32[]{:S(2)}, u32[]{:S(2)}) async-start(bf16[8,2,8320]{2,1,0:T(2,128)(2,1)} %all_to_all.8), calls=%async_computation | async-start | bytes 532480 | tf_op jit(solution)/shard_map/all_to_all | solution.py:113
  19.1 81.3 %all-gather.3.cloned.1.call-start = ((), (), s32[]{:S(2)}) async-start(), calls=%async_computation.4 | async-start | bytes 8912896 | tf_op jit(solution)/shard_map/all_gather | solution.py:134
  30.1 256.7 %all-reduce.3.cloned.1.call-start = ((), (), s32[]{:S(2)}) async-start(), calls=%async_computation.2 | async-start | bytes 16777216 | tf_op jit(solution)/shard_map/psum | solution.py:190
  100.4 5.8 %copy-start.2 = (bf16[16384,256]{1,0:T(8,128)(2,1)S(1)}, bf16[16384,256]{1,0:T(8,128)(2,1)}, u32[]{:S(2)}) copy-start(bf16[16384,256]{1,0:T(8,128)(2,1)} %all-gather.3.cloned.1.call-done) | copy-start | bytes 25165828
  111.0 8.1 %copy-start.4 = (bf16[16,256,256]{1,0,2:T(8,128)(2,1)S(1)}, bf16[16,256,256]{1,0,2:T(8,128)(2,1)}, u32[]{:S(2)}) copy-start(bf16[16,256,256]{1,0,2:T(8,128)(2,1)} %copy.75) | copy-start | bytes 6291460
  117.3 10.9 %collective-permute-start = (bf16[1024,128]{0,1:T(8,128)(2,1)S(1)}, bf16[1024,128]{0,1:T(8,128)(2,1)S(1)}, u32[]{:S(2)}, u32[]{:S(2)}) collective-permute-start(bf16[1024,128]{0,1:T(8,128)(2,1)S(1)} %pad_maximum_fusion.3), channel_id=1, source_target_pairs={{0,1},{1,0},{2,3},{3,2},{4,5},{5,4},{6,7},{7,6},{8,9},{9,8},{10,11... | collective-permute-start | bytes 786440 | tf_op jit(solution)/shard_map/ppermute | solution.py:22
  127.4 1.7 copy-start.6
  132.3 4.7 %copy-start.7 = (bf16[1024,64]{0,1:T(8,128)(2,1)S(1)}, bf16[1024,64]{0,1:T(8,128)(2,1)}, u32[]{:S(2)}) copy-start(bf16[1024,64]{0,1:T(8,128)(2,1)} %get-tuple-element.58) | copy-start | bytes 393220
  137.0 2.8 copy-start.11
  145.9 273.7 %reduce-scatter.2.cloned.1.call-start = ((), (), s32[]{:S(2)}) async-start(), calls=%async_computation.3 | async-start | bytes 8912896 | tf_op jit(solution)/shard_map/reduce_scatter | solution.py:197
  153.9 144.0 %copy-start.10 = (f32[4096]{0:T(1024)S(1)}, f32[4096]{0:T(1024)}, u32[]{:S(2)}) copy-start(f32[4096]{0:T(1024)} %param.26) | copy-start | bytes 49156
  294.7 3.2 copy-start.3
  309.2 112.6 %copy-start.1 = (bf16[256,4096]{1,0:T(8,128)(2,1)S(1)}, bf16[256,4096]{1,0:T(8,128)(2,1)}, u32[]{:S(2)}) copy-start(bf16[256,4096]{1,0:T(8,128)(2,1)} %param.25) | copy-start | bytes 6291460
Sparse Core Ops, SparseCore 0:
  30.2 70.1 all-gather.2
  146.1 140.7 all-reduce.2
  335.8 83.8 reduce-scatter.1

commit v6 on v5

--- a/solution.py
+++ b/solution.py
@@ -29,18 +29,16 @@
 
 
 def rotate_pairs(values, positions, first_pair):
-    pair_count = values.shape[-1] // 2
+    width = values.shape[-1]
+    pair_count = width // 2
     exponent = 2.0 * (first_pair + jnp.arange(pair_count, dtype=jnp.int32)).astype(jnp.float32) / HD
     frequency = rope_base ** (-exponent)
     angles = positions.astype(jnp.float32)[:, None] * frequency[None, :]
-    cosine = jnp.cos(angles)[:, None, :]
-    sine_part = jnp.sin(angles)[:, None, :]
-    paired = values.reshape(values.shape[0], values.shape[1], pair_count, 2)
-    even_part = paired[..., 0]
-    odd_part = paired[..., 1]
-    new_even = even_part * cosine - odd_part * sine_part
-    new_odd = even_part * sine_part + odd_part * cosine
-    return jnp.stack([new_even, new_odd], axis=-1).reshape(values.shape)
+    even_lane = jnp.arange(width, dtype=jnp.int32) % 2 == 0
+    cosine = jnp.repeat(jnp.cos(angles), 2, axis=-1)[:, None, :]
+    signed_sine = (jnp.repeat(jnp.sin(angles), 2, axis=-1) * jnp.where(even_lane, -1.0, 1.0))[:, None, :]
+    swapped = jnp.where(even_lane, jnp.roll(values, -1, axis=-1), jnp.roll(values, 1, axis=-1))
+    return values * cosine + swapped * signed_sine
 
 
 def attend_block(query_block, query_segments, query_index, keys_full, values_full, segment_ids):

time: 429 us -> 426 us (level)
  matrix products: 75.6 us -> 67.4 us
    dot_general x3, matrix products: 18.7 us -> 10.3 us  [project(): jnp.einsum('srk,skn->rn', normed, weight.reshape(ts_count, part_width, we...]
    all_gather x1, waiting for transfers between devices: 62.1 us -> 56.7 us  [shards(): stacked = lax.all_gather(own_part, 'ts', axis=0, tiled=False)]
    ppermute x1, waiting for transfers between devices: 0.01 us -> 5.18 us  [partner_2(): return lax.ppermute(block, axis, route)]
  transfers between devices with their start and end apart: 5 -> 5, of which waited for: 4 -> 5; matrix products, arithmetic and copies ran while one was open for 6% -> 6% of each run, Pallas kernels for 0% -> 0%
where the time goes in v6:
time: 426 us; the launch traced here: 425 us
  waiting for transfers between devices  285 us (67%)
  matrix products  67.4 us (16%)
  other arithmetic  29.1 us (7%)
  local copies, waits for them, and re-layouts  23.4 us (5%)
  between operations  13.5 us (3%)
  starting transfers between devices  7.07 us (2%)
    psum x1, waiting for transfers between devices, shards(): lax.psum(partial_rows.astype(jnp.bfloat16), 'ts').astype(jnp.float32)  133 us
    reduce_scatter x1, waiting for transfers between devices, shards(): lax.psum_scatter(jnp.dot(hidden, w_down, preferred_element_type=jnp.float...  84 us
    all_gather x1, waiting for transfers between devices, shards(): stacked = lax.all_gather(own_part, 'ts', axis=0, tiled=False)  56.7 us
    dot_general x1, matrix products, shards(): jnp.dot(hidden, w_down, preferred_element_type=jnp.float32)  26.4 us
    dot_general x1, matrix products, shards(): up_proj = jnp.dot(normed_mlp, w_up, preferred_element_type=jnp.float32)  11.3 us
    dot_general x3, matrix products, project(): jnp.einsum('srk,skn->rn', normed, weight.reshape(ts_count, part_width, we...  10.3 us
  transfers between devices with their start and end apart: 5, of which 5 were waited for; matrix products, arithmetic and copies ran while one was open for 6% of the time, Pallas kernels for 0%

profile of v6, /device:TPU:0, one launch (start us, length us, event | category | flops | bytes accessed | tf_op | source)
XLA Modules:
  0.0 425.0 jit_solution(9180079926864898200)
XLA Ops:
  6.5 0.7 compare_reduce_fusion.1
  7.3 0.6 compare_reduce_fusion
  7.9 0.7 and_select_fusion.4
  8.7 0.7 multiply_add_fusion.1
  9.4 2.0 fusion.108
  11.5 1.1 copy.74
  12.7 0.2 convolution_convert_fusion
  12.9 0.8 all_to_all.8
  13.7 5.4 %all-to-all-start = ((bf16[8,2,8320]{2,1,0:T(2,128)(2,1)}), bf16[8,2,8320]{2,1,0:T(2,128)(2,1)S(1)}, u32[]{:S(2)}, u32[]{:S(2)}) async-start(bf16[8,2,8320]{2,1,0:T(2,128)(2,1)} %all_to_all.8), calls=%async_computation | async-start | bytes 532480 | tf_op jit(solution)/shard_map/all_to_all | solution.py:111
  19.1 0.8 convert_reduce_fusion
  19.9 0.8 select_reduce_fusion
  20.7 0.7 iota_subtract_fusion
  21.4 5.2 %all-to-all-done = bf16[8,2,8320]{2,1,0:T(2,128)(2,1)S(1)} async-done(((bf16[8,2,8320]{2,1,0:T(2,128)(2,1)}), bf16[8,2,8320]{2,1,0:T(2,128)(2,1)S(1)}, u32[]{:S(2)}, u32[]{:S(2)}) %all-to-all-start) | async-done | bytes 266272 | tf_op jit(solution)/shard_map/all_to_all | solution.py:111
  27.0 0.3 convolution_convert_fusion.1
  27.4 2.7 fusion.38
  30.2 4.7 %copy.68 = bf16[16,256,256]{1,0,2:T(8,128)(2,1)} copy(bf16[16,256,256]{2,1,0:T(8,128)(2,1)} %bitcast.129) | data formatting | bytes 4194304 | tf_op jit(solution)/shard_map/reshape | solution.py:148
  35.0 0.9 fusion.50
  35.9 1.3 fusion.21
  37.2 0.5 multiply_sine_fusion.1
  37.8 0.9 reshape.331
  38.8 0.9 broadcast_in_dim_reshape.4
  39.6 1.0 multiply_cosine_fusion
  40.8 0.4 mul.191
  41.4 1.2 reshape.334
  42.6 1.1 broadcast_multiply_fusion
  43.7 56.7 %all-gather.3.cloned.1.call-done = bf16[16384,256]{1,0:T(8,128)(2,1)} async-done(((bf16[1024,256]{1,0:T(8,128)(2,1)}), bf16[16384,256]{1,0:T(8,128)(2,1)}) %all-gather.3.cloned.1.call-update) | async-done | bytes 8388624 | tf_op jit(solution)/shard_map/all_gather | solution.py:132
  100.4 5.2 %fusion.2 = f32[1024]{0:T(1024)S(1)} fusion(bf16[16,1024,256]{2,1,0:T(8,128)(2,1)} %bitcast.124), kind=kLoop, calls=%fused_computation.6 | loop fusion | flops 12581888 | bytes 8392704 | tf_op jit(solution)/shard_map/reduce_sum | solution.py:138
  105.6 0.5 copy-done.2
  106.2 4.0 fusion.55
  110.3 3.3 fusion.30
  114.0 3.0 fusion.42
  117.1 1.6 collective-permute-start
  118.6 1.4 fusion.45
  120.0 5.2 %collective-permute-done = bf16[1024,128]{0,1:T(8,128)(2,1)S(1)} collective-permute-done((bf16[1024,128]{0,1:T(8,128)(2,1)S(1)}, bf16[1024,128]{0,1:T(8,128)(2,1)S(1)}, u32[]{:S(2)}, u32[]{:S(2)}) %collective-permute-start) | collective-permute-done | bytes 262176 | tf_op jit(solution)/shard_map/ppermute | solution.py:22
  125.4 3.3 fusion.145
  128.6 4.7 %fusion.136 = (f32[2,512]{1,0:T(2,128)S(1)}, f32[2,512,1024]{1,2,0:T(8,128)}) fusion(pred[512,1024]{0,1:T(8,128)(4,1)} %fusion.21, bf16[1024,2,128]{0,2,1:T(8,128)(2,1)S(1)} %copy-done.7, bf16[1024,64]{0,1:T(8,128)(2,1)S(1)} %get-tuple-element.61, bf16[1024,64]{0,1:T(8,128)(2,1)S(1)} %get-tuple-element.40), kind=kOutput, calls=%fused_computation.172 | convolution fusion | flops 273155072 | bytes 5246976 | tf_op jit(solution)/shard_map/sub | solution.py:54
  133.4 2.1 convolution_convert_fusion.4
  135.4 0.8 copy-done.13
  136.2 0.5 fusion.41
  136.7 5.6 %convolution_convert_fusion.3 = bf16[1024,4096]{1,0:T(8,128)(2,1)} fusion(bf16[256,4096]{1,0:T(8,128)(2,1)S(1)} %copy-done, bf16[512,256]{0,1:T(8,128)(2,1)S(1)} %bitcast.133, bf16[512,256]{0,1:T(8,128)(2,1)S(1)} %bitcast.132), kind=kOutput, calls=%fused_computation.18 | convolution fusion | flops 2152726528 | bytes 11010048 | tf_op jit(solution)/shard_map/dot_general | solution.py:187
  142.3 7.8 %copy.73 = bf16[16,128,8,256]{3,2,0,1:T(8,128)(2,1)} copy(bf16[16,128,8,256]{3,2,1,0:T(8,128)(2,1)} %bitcast.125) | data formatting | bytes 16777216 | tf_op jit(solution)/shard_map/reshape | solution.py:135
  150.1 133.4 %all-reduce.3.cloned.1.call-done = bf16[1024,4096]{1,0:T(8,128)(2,1)} async-done(((bf16[1024,4096]{1,0:T(8,128)(2,1)}), bf16[1024,4096]{1,0:T(8,128)(2,1)}) %all-reduce.3.cloned.1.call-update) | async-done | bytes 8388624 | tf_op jit(solution)/shard_map/psum | solution.py:188
  283.5 7.9 %fusion.5 = (f32[1024]{0:T(1024)S(1)}, bf16[1024,4096]{1,0:T(8,128)(2,1)S(1)}) fusion(bf16[1024,4096]{1,0:T(8,128)(2,1)} %all-reduce.3.cloned.1.call-done, bf16[1024,4096]{1,0:T(8,128)(2,1)} %bitcast.126), kind=kLoop, calls=%fused_computation.9 | loop fusion | flops 29359104 | bytes 25169920 | tf_op jit(solution)/shard_map/reduce_sum | solution.py:27
  291.3 3.2 copy-done.3
  294.6 11.3 %fusion.11 = f32[1024,768]{1,0:T(8,128)} fusion(bf16[4096,768]{1,0:T(8,128)(2,1)} %param.28, bf16[1024,4096]{1,0:T(8,128)(2,1)S(1)} %get-tuple-element.32, f32[4096]{0:T(1024)S(1)} %copy-done.12, f32[1024]{0:T(1024)S(1)} %add_rsqrt_fusion), kind=kOutput, calls=%fused_computation.24 | convolution fusion | flops 6459228160 | bytes 17846272 | tf_op jit(solution)/shard_map/dot_general | solution.py:193
  305.9 26.4 %convolution_convert_fusion.2 = bf16[1024,4096]{1,0:T(8,128)(2,1)} fusion(bf16[768,4096]{1,0:T(8,128)(2,1)} %param.29, f32[1024,768]{1,0:T(8,128)} %fusion.11, bf16[4096,768]{1,0:T(8,128)(2,1)} %param.27, bf16[1024,4096]{1,0:T(8,128)(2,1)} %copy-done.3, f32[4096]{0:T(1024)S(1)} %copy-done.12, f32[1024]{0:T(1024)S(1)} %add_rsqrt_fusion), kind=kOutput, calls=%fused_computation.17 | convolution fusion | flops 12910592000 | bytes 32526336 | tf_op jit(solution)/shard_map/dot_general | solution.py:196
  332.3 84.0 %reduce-scatter.2.cloned.1.call-done = bf16[64,4096]{1,0:T(8,128)(2,1)} async-done(((bf16[1024,4096]{1,0:T(8,128)(2,1)}), bf16[64,4096]{1,0:T(8,128)(2,1)}) %reduce-scatter.2.cloned.1.call-update) | async-done | bytes 524304 | tf_op jit(solution)/shard_map/reduce_scatter | solution.py:195
  416.3 2.1 fusion.52
  (64 shorter events, 2.1 us)
Async XLA Ops:
  6.5 130.1 %copy-start = (bf16[256,4096]{1,0:T(8,128)(2,1)S(1)}, bf16[256,4096]{1,0:T(8,128)(2,1)}, u32[]{:S(2)}) copy-start(bf16[256,4096]{1,0:T(8,128)(2,1)} %param.25) | copy-start | bytes 6291460
  6.5 28.4 %copy-start.9 = (s32[1,1024]{1,0:T(1,128)S(1)}, s32[1,1024]{1,0:T(1,128)}, u32[]{:S(2)}) copy-start(s32[1,1024]{1,0:T(1,128)} %param.20) | copy-start | bytes 12292
  6.5 23.6 %copy-start.10 = (f32[4096]{0:T(1024)S(1)}, f32[4096]{0:T(1024)}, u32[]{:S(2)}) copy-start(f32[4096]{0:T(1024)} %param.21) | copy-start | bytes 49156
  13.7 13.0 %all-to-all-start = ((bf16[8,2,8320]{2,1,0:T(2,128)(2,1)}), bf16[8,2,8320]{2,1,0:T(2,128)(2,1)S(1)}, u32[]{:S(2)}, u32[]{:S(2)}) async-start(bf16[8,2,8320]{2,1,0:T(2,128)(2,1)} %all_to_all.8), calls=%async_computation | async-start | bytes 532480 | tf_op jit(solution)/shard_map/all_to_all | solution.py:111
  19.1 81.3 %all-gather.3.cloned.1.call-start = ((), (), s32[]{:S(2)}) async-start(), calls=%async_computation.4 | async-start | bytes 8912896 | tf_op jit(solution)/shard_map/all_gather | solution.py:132
  30.1 253.3 %all-reduce.3.cloned.1.call-start = ((), (), s32[]{:S(2)}) async-start(), calls=%async_computation.2 | async-start | bytes 16777216 | tf_op jit(solution)/shard_map/psum | solution.py:188
  100.4 5.8 %copy-start.2 = (bf16[16384,256]{1,0:T(8,128)(2,1)S(1)}, bf16[16384,256]{1,0:T(8,128)(2,1)}, u32[]{:S(2)}) copy-start(bf16[16384,256]{1,0:T(8,128)(2,1)} %all-gather.3.cloned.1.call-done) | copy-start | bytes 25165828
  106.2 4.1 copy-start.4
  110.3 3.6 copy-start.5
  110.3 3.6 copy-start.6
  110.3 3.7 copy-start.11
  117.0 8.3 %copy-start.8 = (pred[512,512]{0,1:T(8,128)(4,1)S(1)}, pred[512,512]{0,1:T(8,128)(4,1)}, u32[]{:S(2)}) copy-start(pred[512,512]{0,1:T(8,128)(4,1)} %fusion.50) | copy-start | bytes 786436
  117.1 8.1 %collective-permute-start = (bf16[1024,128]{0,1:T(8,128)(2,1)S(1)}, bf16[1024,128]{0,1:T(8,128)(2,1)S(1)}, u32[]{:S(2)}, u32[]{:S(2)}) collective-permute-start(bf16[1024,128]{0,1:T(8,128)(2,1)S(1)} %pad_maximum_fusion.2), channel_id=1, source_target_pairs={{0,1},{1,0},{2,3},{3,2},{4,5},{5,4},{6,7},{7,6},{8,9},{9,8},{10,11... | collective-permute-start | bytes 786440 | tf_op jit(solution)/shard_map/ppermute | solution.py:22
  120.0 8.6 %copy-start.7 = (bf16[1024,2,128]{0,2,1:T(8,128)(2,1)S(1)}, bf16[1024,2,128]{0,2,1:T(8,128)(2,1)}, u32[]{:S(2)}) copy-start(bf16[1024,2,128]{0,2,1:T(8,128)(2,1)} %fusion.45) | copy-start | bytes 1572868
  133.4 2.8 copy-start.13
  142.3 274.0 %reduce-scatter.2.cloned.1.call-start = ((), (), s32[]{:S(2)}) async-start(), calls=%async_computation.3 | async-start | bytes 8912896 | tf_op jit(solution)/shard_map/reduce_scatter | solution.py:195
  150.1 144.5 %copy-start.12 = (f32[4096]{0:T(1024)S(1)}, f32[4096]{0:T(1024)}, u32[]{:S(2)}) copy-start(f32[4096]{0:T(1024)} %param.26) | copy-start | bytes 49156
  291.3 3.2 copy-start.3
  305.9 112.6 %copy-start.1 = (bf16[256,4096]{1,0:T(8,128)(2,1)S(1)}, bf16[256,4096]{1,0:T(8,128)(2,1)}, u32[]{:S(2)}) copy-start(bf16[256,4096]{1,0:T(8,128)(2,1)} %param.25) | copy-start | bytes 6291460
Sparse Core Ops, SparseCore 0:
  30.2 70.1 all-gather.2
  142.4 140.9 all-reduce.2
  332.4 83.8 reduce-scatter.1

commit v7 on v6

--- a/solution.py
+++ b/solution.py
@@ -149,9 +149,6 @@
             preferred_element_type=jnp.float32,
         )
 
-    heads_here = w_query.shape[1] // HD
-    queries = project(w_query).reshape(seq_len, heads_here, HD)
-    queries = rotate_pairs(queries, positions, 0).astype(jnp.bfloat16)
     kv_cols = w_key.shape[1]
     upper_half = ts_index % 2 == 1
     key_half = project(w_key).reshape(
@@ -162,6 +159,10 @@
     value_half = project(w_value).astype(jnp.bfloat16)
     own_pair = jnp.concatenate([key_half, value_half], axis=1)
     partner = partner_2(own_pair, "ts", 0)
+    query_weight = lax.optimization_barrier((own_pair, w_query))[1]
+    heads_here = w_query.shape[1] // HD
+    queries = project(query_weight).reshape(seq_len, heads_here, HD)
+    queries = rotate_pairs(queries, positions, 0).astype(jnp.bfloat16)
     lower_half = jnp.where(upper_half, partner, own_pair)
     higher = jnp.where(upper_half, own_pair, partner)
     keys_full = jnp.concatenate([lower_half[:, :kv_cols], higher[:, :kv_cols]], axis=1)

time: 426 us -> 430 us (level)
    ppermute x1, waiting for transfers between devices: 5.18 us -> 0.01 us  [partner_2(): return lax.ppermute(block, axis, route)]
    all_gather x1, waiting for transfers between devices: 56.7 us -> 61.2 us  [shards(): stacked = lax.all_gather(own_part, 'ts', axis=0, tiled=False)]
  transfers between devices with their start and end apart: 5 -> 5, of which waited for: 5 -> 4; matrix products, arithmetic and copies ran while one was open for 6% -> 7% of each run, Pallas kernels for 0% -> 0%
where the time goes in v7:
time: 430 us; the launch traced here: 429 us
  waiting for transfers between devices  284 us (66%)
  matrix products  70.7 us (16%)
  other arithmetic  30.8 us (7%)
  local copies, waits for them, and re-layouts  23.6 us (5%)
  between operations  13.5 us (3%)
  starting transfers between devices  6.99 us (2%)
    psum x1, waiting for transfers between devices, shards(): lax.psum(partial_rows.astype(jnp.bfloat16), 'ts').astype(jnp.float32)  133 us
    reduce_scatter x1, waiting for transfers between devices, shards(): lax.psum_scatter(jnp.dot(hidden, w_down, preferred_element_type=jnp.float...  84.2 us
    all_gather x1, waiting for transfers between devices, shards(): stacked = lax.all_gather(own_part, 'ts', axis=0, tiled=False)  61.2 us
    dot_general x1, matrix products, shards(): jnp.dot(hidden, w_down, preferred_element_type=jnp.float32)  26.4 us
    dot_general x3, matrix products, project(): jnp.einsum('srk,skn->rn', normed, weight.reshape(ts_count, part_width, we...  13.6 us
    dot_general x1, matrix products, shards(): up_proj = jnp.dot(normed_mlp, w_up, preferred_element_type=jnp.float32)  11.3 us
  transfers between devices with their start and end apart: 5, of which 4 were waited for; matrix products, arithmetic and copies ran while one was open for 7% of the time, Pallas kernels for 0%

profile of v7, /device:TPU:0, one launch (start us, length us, event | category | flops | bytes accessed | tf_op | source)
XLA Modules:
  0.0 429.2 jit_solution(2186495948332170838)
XLA Ops:
  6.5 0.7 compare_reduce_fusion.1
  7.3 0.6 compare_reduce_fusion
  7.9 0.7 and_select_fusion.4
  8.7 0.7 multiply_add_fusion.1
  9.4 2.0 fusion.108
  11.5 1.1 copy.74
  12.9 0.8 all_to_all.8
  13.7 5.4 %all-to-all-start = ((bf16[8,2,8320]{2,1,0:T(2,128)(2,1)}), bf16[8,2,8320]{2,1,0:T(2,128)(2,1)S(1)}, u32[]{:S(2)}, u32[]{:S(2)}) async-start(bf16[8,2,8320]{2,1,0:T(2,128)(2,1)} %all_to_all.8), calls=%async_computation | async-start | bytes 532480 | tf_op jit(solution)/shard_map/all_to_all | solution.py:111
  19.1 0.8 convert_reduce_fusion
  19.9 0.8 select_reduce_fusion
  20.7 0.7 iota_subtract_fusion
  21.4 5.2 %all-to-all-done = bf16[8,2,8320]{2,1,0:T(2,128)(2,1)S(1)} async-done(((bf16[8,2,8320]{2,1,0:T(2,128)(2,1)}), bf16[8,2,8320]{2,1,0:T(2,128)(2,1)S(1)}, u32[]{:S(2)}, u32[]{:S(2)}) %all-to-all-start) | async-done | bytes 266272 | tf_op jit(solution)/shard_map/all_to_all | solution.py:111
  27.0 0.3 convolution_convert_fusion.1
  27.4 2.7 fusion.38
  30.3 0.9 fusion.50
  31.2 1.3 fusion.21
  32.5 0.5 multiply_sine_fusion.1
  33.1 0.9 reshape.331
  34.1 0.9 broadcast_in_dim_reshape.4
  35.0 1.0 multiply_cosine_fusion
  36.2 0.4 mul.191
  36.7 1.2 reshape.334
  38.0 1.2 broadcast_multiply_fusion
  39.1 61.2 %all-gather.3.cloned.1.call-done = bf16[16384,256]{1,0:T(8,128)(2,1)} async-done(((bf16[1024,256]{1,0:T(8,128)(2,1)}), bf16[16384,256]{1,0:T(8,128)(2,1)}) %all-gather.3.cloned.1.call-update) | async-done | bytes 8388624 | tf_op jit(solution)/shard_map/all_gather | solution.py:132
  100.4 5.2 %fusion.2 = f32[1024]{0:T(1024)S(1)} fusion(bf16[16,1024,256]{2,1,0:T(8,128)(2,1)} %bitcast.124), kind=kLoop, calls=%fused_computation.6 | loop fusion | flops 12581888 | bytes 8392704 | tf_op jit(solution)/shard_map/reduce_sum | solution.py:138
  105.6 0.5 copy-done.2
  106.2 3.9 fusion.55
  110.3 2.8 fusion.42
  113.2 0.7 pad_maximum_fusion.2
  113.9 1.5 collective-permute-start
  115.4 4.7 %copy.68 = bf16[16,256,256]{1,0,2:T(8,128)(2,1)} copy(bf16[16,256,256]{2,1,0:T(8,128)(2,1)} %bitcast.129) | data formatting | bytes 4194304 | tf_op jit(solution)/shard_map/reshape | solution.py:148
  120.1 6.8 %fusion.30 = f32[1024,2,128]{0,2,1:T(8,128)S(1)} fusion(bf16[2,128,256,16]{2,3,1,0:T(8,128)(2,1)} %bitcast.130, f32[16,256]{1,0:T(8,128)S(1)} %mul.177, f32[1024]{0:T(1024)S(1)} %add_rsqrt_fusion.1, bf16[16384,256]{1,0:T(8,128)(2,1)} %all-gather.3.cloned.1.call-done), kind=kOutput, calls=%fused_computation.41 | convolution fusion | flops 2164260864 | bytes 11554816 | tf_op jit(solution)/shard_map/srk,skn->rn/dot_general | solution.py:145
  127.1 1.4 fusion.45
  128.5 1.1 broadcast_select_fusion.1
  129.7 3.3 fusion.145
  133.0 4.7 %fusion.136 = (f32[2,512]{1,0:T(2,128)S(1)}, f32[2,512,1024]{1,2,0:T(8,128)}) fusion(pred[512,1024]{0,1:T(8,128)(4,1)} %fusion.21, bf16[1024,2,128]{0,2,1:T(8,128)(2,1)S(1)} %copy-done.6, bf16[1024,64]{0,1:T(8,128)(2,1)S(1)} %get-tuple-element.63, bf16[1024,64]{0,1:T(8,128)(2,1)S(1)} %get-tuple-element.42), kind=kOutput, calls=%fused_computation.172 | convolution fusion | flops 273155072 | bytes 5246976 | tf_op jit(solution)/shard_map/sub | solution.py:54
  137.8 2.1 convolution_convert_fusion.4
  139.8 0.8 copy-done.11
  140.6 0.5 fusion.41
  141.1 5.6 %convolution_convert_fusion.3 = bf16[1024,4096]{1,0:T(8,128)(2,1)} fusion(bf16[256,4096]{1,0:T(8,128)(2,1)S(1)} %copy-done, bf16[512,256]{0,1:T(8,128)(2,1)S(1)} %bitcast.133, bf16[512,256]{0,1:T(8,128)(2,1)S(1)} %bitcast.132), kind=kOutput, calls=%fused_computation.18 | convolution fusion | flops 2152726528 | bytes 11010048 | tf_op jit(solution)/shard_map/dot_general | solution.py:188
  146.8 7.9 %copy.73 = bf16[16,128,8,256]{3,2,0,1:T(8,128)(2,1)} copy(bf16[16,128,8,256]{3,2,1,0:T(8,128)(2,1)} %bitcast.125) | data formatting | bytes 16777216 | tf_op jit(solution)/shard_map/reshape | solution.py:135
  154.7 132.8 %all-reduce.3.cloned.1.call-done = bf16[1024,4096]{1,0:T(8,128)(2,1)} async-done(((bf16[1024,4096]{1,0:T(8,128)(2,1)}), bf16[1024,4096]{1,0:T(8,128)(2,1)}) %all-reduce.3.cloned.1.call-update) | async-done | bytes 8388624 | tf_op jit(solution)/shard_map/psum | solution.py:189
  287.5 7.9 %fusion.5 = (f32[1024]{0:T(1024)S(1)}, bf16[1024,4096]{1,0:T(8,128)(2,1)S(1)}) fusion(bf16[1024,4096]{1,0:T(8,128)(2,1)} %all-reduce.3.cloned.1.call-done, bf16[1024,4096]{1,0:T(8,128)(2,1)} %bitcast.126), kind=kLoop, calls=%fused_computation.9 | loop fusion | flops 29359104 | bytes 25169920 | tf_op jit(solution)/shard_map/reduce_sum | solution.py:27
  295.4 3.2 copy-done.3
  298.6 11.3 %fusion.11 = f32[1024,768]{1,0:T(8,128)} fusion(bf16[4096,768]{1,0:T(8,128)(2,1)} %param.28, bf16[1024,4096]{1,0:T(8,128)(2,1)S(1)} %get-tuple-element.34, f32[4096]{0:T(1024)S(1)} %copy-done.10, f32[1024]{0:T(1024)S(1)} %add_rsqrt_fusion), kind=kOutput, calls=%fused_computation.24 | convolution fusion | flops 6459228160 | bytes 17846272 | tf_op jit(solution)/shard_map/dot_general | solution.py:194
  309.9 26.4 %convolution_convert_fusion.2 = bf16[1024,4096]{1,0:T(8,128)(2,1)} fusion(bf16[768,4096]{1,0:T(8,128)(2,1)} %param.29, f32[1024,768]{1,0:T(8,128)} %fusion.11, bf16[4096,768]{1,0:T(8,128)(2,1)} %param.27, bf16[1024,4096]{1,0:T(8,128)(2,1)} %copy-done.3, f32[4096]{0:T(1024)S(1)} %copy-done.10, f32[1024]{0:T(1024)S(1)} %add_rsqrt_fusion), kind=kOutput, calls=%fused_computation.17 | convolution fusion | flops 12910592000 | bytes 32526336 | tf_op jit(solution)/shard_map/dot_general | solution.py:197
  336.4 84.2 %reduce-scatter.2.cloned.1.call-done = bf16[64,4096]{1,0:T(8,128)(2,1)} async-done(((bf16[1024,4096]{1,0:T(8,128)(2,1)}), bf16[64,4096]{1,0:T(8,128)(2,1)}) %reduce-scatter.2.cloned.1.call-update) | async-done | bytes 524304 | tf_op jit(solution)/shard_map/reduce_scatter | solution.py:196
  420.6 2.1 fusion.52
  (60 shorter events, 2.2 us)
Async XLA Ops:
  6.5 134.5 %copy-start = (bf16[256,4096]{1,0:T(8,128)(2,1)S(1)}, bf16[256,4096]{1,0:T(8,128)(2,1)}, u32[]{:S(2)}) copy-start(bf16[256,4096]{1,0:T(8,128)(2,1)} %param.25) | copy-start | bytes 6291460
  6.5 23.7 %copy-start.7 = (s32[1,1024]{1,0:T(1,128)S(1)}, s32[1,1024]{1,0:T(1,128)}, u32[]{:S(2)}) copy-start(s32[1,1024]{1,0:T(1,128)} %param.20) | copy-start | bytes 12292
  6.5 23.6 %copy-start.8 = (f32[4096]{0:T(1024)S(1)}, f32[4096]{0:T(1024)}, u32[]{:S(2)}) copy-start(f32[4096]{0:T(1024)} %param.21) | copy-start | bytes 49156
  13.7 13.0 %all-to-all-start = ((bf16[8,2,8320]{2,1,0:T(2,128)(2,1)}), bf16[8,2,8320]{2,1,0:T(2,128)(2,1)S(1)}, u32[]{:S(2)}, u32[]{:S(2)}) async-start(bf16[8,2,8320]{2,1,0:T(2,128)(2,1)} %all_to_all.8), calls=%async_computation | async-start | bytes 532480 | tf_op jit(solution)/shard_map/all_to_all | solution.py:111
  19.1 81.3 %all-gather.3.cloned.1.call-start = ((), (), s32[]{:S(2)}) async-start(), calls=%async_computation.4 | async-start | bytes 8912896 | tf_op jit(solution)/shard_map/all_gather | solution.py:132
  30.1 257.4 %all-reduce.3.cloned.1.call-start = ((), (), s32[]{:S(2)}) async-start(), calls=%async_computation.2 | async-start | bytes 16777216 | tf_op jit(solution)/shard_map/psum | solution.py:189
  100.4 5.8 %copy-start.2 = (bf16[16384,256]{1,0:T(8,128)(2,1)S(1)}, bf16[16384,256]{1,0:T(8,128)(2,1)}, u32[]{:S(2)}) copy-start(bf16[16384,256]{1,0:T(8,128)(2,1)} %all-gather.3.cloned.1.call-done) | copy-start | bytes 25165828
  106.2 4.0 copy-start.4
  106.2 4.0 copy-start.5
  106.2 4.2 copy-start.9
  113.9 14.6 %collective-permute-start = (bf16[1024,128]{0,1:T(8,128)(2,1)}, bf16[1024,128]{0,1:T(8,128)(2,1)}, u32[]{:S(2)}, u32[]{:S(2)}) collective-permute-start(bf16[1024,128]{0,1:T(8,128)(2,1)} %pad_maximum_fusion.2), channel_id=1, source_target_pairs={{0,1},{1,0},{2,3},{3,2},{4,5},{5,4},{6,7},{7,6},{8,9},{9,8},{10,11... | collective-permute-start | bytes 786440 | tf_op jit(solution)/shard_map/ppermute | solution.py:22
  128.5 4.5 %copy-start.6 = (bf16[1024,2,128]{0,2,1:T(8,128)(2,1)S(1)}, bf16[1024,2,128]{0,2,1:T(8,128)(2,1)}, u32[]{:S(2)}) copy-start(bf16[1024,2,128]{0,2,1:T(8,128)(2,1)} %fusion.45) | copy-start | bytes 1572868
  137.8 2.8 copy-start.11
  146.7 273.8 %reduce-scatter.2.cloned.1.call-start = ((), (), s32[]{:S(2)}) async-start(), calls=%async_computation.3 | async-start | bytes 8912896 | tf_op jit(solution)/shard_map/reduce_scatter | solution.py:196
  154.7 143.9 %copy-start.10 = (f32[4096]{0:T(1024)S(1)}, f32[4096]{0:T(1024)}, u32[]{:S(2)}) copy-start(f32[4096]{0:T(1024)} %param.26) | copy-start | bytes 49156
  295.4 3.2 copy-start.3
  309.9 112.7 %copy-start.1 = (bf16[256,4096]{1,0:T(8,128)(2,1)S(1)}, bf16[256,4096]{1,0:T(8,128)(2,1)}, u32[]{:S(2)}) copy-start(bf16[256,4096]{1,0:T(8,128)(2,1)} %param.25) | copy-start | bytes 6291460
Sparse Core Ops, SparseCore 0:
  30.2 70.1 all-gather.2
  146.8 140.6 all-reduce.2
  336.5 84.0 reduce-scatter.1

commit v8 on v7

--- a/solution.py
+++ b/solution.py
@@ -141,10 +141,10 @@
         widened * inverse_rms[None, :, None] * attn_gain.reshape(ts_count, 1, part_width)
     ).astype(jnp.bfloat16)
 
-    def project(weight):
+    def project(weight, rows=normed):
         return jnp.einsum(
             "srk,skn->rn",
-            normed,
+            rows,
             weight.reshape(ts_count, part_width, weight.shape[1]),
             preferred_element_type=jnp.float32,
         )
@@ -159,9 +159,9 @@
     value_half = project(w_value).astype(jnp.bfloat16)
     own_pair = jnp.concatenate([key_half, value_half], axis=1)
     partner = partner_2(own_pair, "ts", 0)
-    query_weight = lax.optimization_barrier((own_pair, w_query))[1]
+    query_rows = lax.optimization_barrier((own_pair, normed))[1]
     heads_here = w_query.shape[1] // HD
-    queries = project(query_weight).reshape(seq_len, heads_here, HD)
+    queries = project(w_query, query_rows).reshape(seq_len, heads_here, HD)
     queries = rotate_pairs(queries, positions, 0).astype(jnp.bfloat16)
     lower_half = jnp.where(upper_half, partner, own_pair)
     higher = jnp.where(upper_half, own_pair, partner)

time: 430 us -> 433 us (level)
  other arithmetic: 30.8 us -> 37.9 us
    convert_element_type x0 -> x1, other arithmetic: none -> 8.96 us  [shards(): normed = (widened * inverse_rms[None, :, None] * attn_gain.reshape(ts_cou...]
    all_gather x1, waiting for transfers between devices: 61.2 us -> 56.7 us  [shards(): stacked = lax.all_gather(own_part, 'ts', axis=0, tiled=False)]
  transfers between devices with their start and end apart: 5 -> 5, of which waited for: 4 -> 5; matrix products, arithmetic and copies ran while one was open for 7% -> 6% of each run, Pallas kernels for 0% -> 0%
where the time goes in v8:
time: 433 us; the launch traced here: 432 us
  waiting for transfers between devices  282 us (65%)
  matrix products  68.5 us (16%)
  other arithmetic  37.9 us (9%)
  local copies, waits for them, and re-layouts  22.9 us (5%)
  between operations  13.5 us (3%)
  starting transfers between devices  7.25 us (2%)
    psum x1, waiting for transfers between devices, shards(): lax.psum(partial_rows.astype(jnp.bfloat16), 'ts').astype(jnp.float32)  133 us
    reduce_scatter x1, waiting for transfers between devices, shards(): lax.psum_scatter(jnp.dot(hidden, w_down, preferred_element_type=jnp.float...  84.2 us
    all_gather x1, waiting for transfers between devices, shards(): stacked = lax.all_gather(own_part, 'ts', axis=0, tiled=False)  56.7 us
    dot_general x1, matrix products, shards(): jnp.dot(hidden, w_down, preferred_element_type=jnp.float32)  26.4 us
    dot_general x3, matrix products, project(): jnp.einsum('srk,skn->rn', rows, weight.reshape(ts_count, part_width, weig...  11.5 us
    dot_general x1, matrix products, shards(): up_proj = jnp.dot(normed_mlp, w_up, preferred_element_type=jnp.float32)  11.3 us
    convert_element_type x1, other arithmetic, shards(): normed = (widened * inverse_rms[None, :, None] * attn_gain.reshape(ts_cou...  8.96 us
  transfers between devices with their start and end apart: 5, of which 5 were waited for; matrix products, arithmetic and copies ran while one was open for 6% of the time, Pallas kernels for 0%

profile of v8, /device:TPU:0, one launch (start us, length us, event | category | flops | bytes accessed | tf_op | source)
XLA Modules:
  0.0 431.8 jit_solution(12173163024638641891)
XLA Ops:
  6.5 0.7 compare_reduce_fusion.1
  7.3 0.6 compare_reduce_fusion
  7.9 0.7 and_select_fusion.4
  8.7 0.7 multiply_add_fusion.1
  9.4 2.0 fusion.108
  11.5 1.1 copy.74
  12.7 0.2 convolution_convert_fusion
  12.9 0.8 all_to_all.8
  13.7 5.4 %all-to-all-start = ((bf16[8,2,8320]{2,1,0:T(2,128)(2,1)}), bf16[8,2,8320]{2,1,0:T(2,128)(2,1)S(1)}, u32[]{:S(2)}, u32[]{:S(2)}) async-start(bf16[8,2,8320]{2,1,0:T(2,128)(2,1)} %all_to_all.8), calls=%async_computation | async-start | bytes 532480 | tf_op jit(solution)/shard_map/all_to_all | solution.py:111
  19.1 0.8 convert_reduce_fusion
  19.9 0.8 select_reduce_fusion
  20.7 0.7 iota_subtract_fusion
  21.4 5.2 %all-to-all-done = bf16[8,2,8320]{2,1,0:T(2,128)(2,1)S(1)} async-done(((bf16[8,2,8320]{2,1,0:T(2,128)(2,1)}), bf16[8,2,8320]{2,1,0:T(2,128)(2,1)S(1)}, u32[]{:S(2)}, u32[]{:S(2)}) %all-to-all-start) | async-done | bytes 266272 | tf_op jit(solution)/shard_map/all_to_all | solution.py:111
  27.0 0.3 convolution_convert_fusion.1
  27.4 2.7 fusion.38
  30.2 4.6 %copy.68 = bf16[16,256,256]{1,0,2:T(8,128)(2,1)} copy(bf16[16,256,256]{2,1,0:T(8,128)(2,1)} %bitcast.126) | data formatting | bytes 4194304 | tf_op jit(solution)/shard_map/reshape | solution.py:148
  34.9 0.9 fusion.50
  35.8 1.3 fusion.21
  37.1 0.5 multiply_sine_fusion.1
  37.7 0.9 reshape.331
  38.7 0.9 broadcast_in_dim_reshape.4
  39.6 1.0 multiply_cosine_fusion
  40.7 0.4 mul.191
  41.3 1.2 reshape.334
  42.5 1.1 broadcast_multiply_fusion
  43.7 56.7 %all-gather.3.cloned.1.call-done = bf16[16384,256]{1,0:T(8,128)(2,1)} async-done(((bf16[1024,256]{1,0:T(8,128)(2,1)}), bf16[16384,256]{1,0:T(8,128)(2,1)}) %all-gather.3.cloned.1.call-update) | async-done | bytes 8388624 | tf_op jit(solution)/shard_map/all_gather | solution.py:132
  100.4 5.1 %fusion.2 = f32[1024]{0:T(1024)S(1)} fusion(bf16[16,1024,256]{2,1,0:T(8,128)(2,1)} %bitcast.121), kind=kLoop, calls=%fused_computation.6 | loop fusion | flops 12581888 | bytes 8392704 | tf_op jit(solution)/shard_map/reduce_sum | solution.py:138
  105.5 9.0 %fusion.4 = bf16[16,1024,256]{2,1,0:T(8,128)(2,1)} fusion(f32[16,256]{1,0:T(8,128)S(1)} %mul.177, f32[1024]{0:T(1024)S(1)} %add_rsqrt_fusion.1, bf16[16384,256]{1,0:T(8,128)(2,1)} %all-gather.3.cloned.1.call-done), kind=kLoop, calls=%fused_computation.8 | loop fusion | flops 16777216 | bytes 16797696 | tf_op jit(solution)/shard_map/convert_element_type | solution.py:142
  114.5 6.2 %fusion.55 = f32[1024,64,1]{0,1,2:T(8,128)S(1)} fusion(bf16[16,1024,256]{2,1,0:T(8,128)(2,1)} %fusion.4, bf16[8,16,8,256]{3,2,1,0:T(8,128)(2,1)S(1)} %bitcast.129), kind=kOutput, calls=%fused_computation.63 | convolution fusion | flops 536870912 | bytes 9175040 | tf_op jit(solution)/shard_map/srk,skn->rn/dot_general | solution.py:145
  120.7 2.6 fusion.42
  123.5 1.7 collective-permute-start
  125.2 2.7 fusion.30
  128.2 1.4 fusion.45
  129.6 2.2 collective-permute-done
  132.0 3.3 fusion.142
  135.3 4.7 %fusion.133 = (f32[2,512]{1,0:T(2,128)S(1)}, f32[2,512,1024]{1,2,0:T(8,128)}) fusion(pred[512,1024]{0,1:T(8,128)(4,1)} %fusion.21, bf16[1024,2,128]{0,2,1:T(8,128)(2,1)S(1)} %copy-done.9, bf16[1024,64]{0,1:T(8,128)(2,1)S(1)} %get-tuple-element.63, bf16[1024,64]{0,1:T(8,128)(2,1)S(1)} %get-tuple-element.42), kind=kOutput, calls=%fused_computation.172 | convolution fusion | flops 273155072 | bytes 5246976 | tf_op jit(solution)/shard_map/sub | solution.py:54
  140.0 2.1 convolution_convert_fusion.4
  142.1 0.8 copy-done.14
  142.8 0.5 fusion.41
  143.3 5.6 %convolution_convert_fusion.3 = bf16[1024,4096]{1,0:T(8,128)(2,1)} fusion(bf16[256,4096]{1,0:T(8,128)(2,1)S(1)} %copy-done, bf16[512,256]{0,1:T(8,128)(2,1)S(1)} %bitcast.132, bf16[512,256]{0,1:T(8,128)(2,1)S(1)} %bitcast.131), kind=kOutput, calls=%fused_computation.18 | convolution fusion | flops 2152726528 | bytes 11010048 | tf_op jit(solution)/shard_map/dot_general | solution.py:188
  149.0 7.8 %copy.73 = bf16[16,128,8,256]{3,2,0,1:T(8,128)(2,1)} copy(bf16[16,128,8,256]{3,2,1,0:T(8,128)(2,1)} %bitcast.122) | data formatting | bytes 16777216 | tf_op jit(solution)/shard_map/reshape | solution.py:135
  156.7 133.3 %all-reduce.3.cloned.1.call-done = bf16[1024,4096]{1,0:T(8,128)(2,1)} async-done(((bf16[1024,4096]{1,0:T(8,128)(2,1)}), bf16[1024,4096]{1,0:T(8,128)(2,1)}) %all-reduce.3.cloned.1.call-update) | async-done | bytes 8388624 | tf_op jit(solution)/shard_map/psum | solution.py:189
  290.1 7.9 %fusion.5 = (f32[1024]{0:T(1024)S(1)}, bf16[1024,4096]{1,0:T(8,128)(2,1)S(1)}) fusion(bf16[1024,4096]{1,0:T(8,128)(2,1)} %all-reduce.3.cloned.1.call-done, bf16[1024,4096]{1,0:T(8,128)(2,1)} %bitcast.123), kind=kLoop, calls=%fused_computation.9 | loop fusion | flops 29359104 | bytes 25169920 | tf_op jit(solution)/shard_map/reduce_sum | solution.py:27
  298.0 3.2 copy-done.3
  301.2 11.3 %fusion.11 = f32[1024,768]{1,0:T(8,128)} fusion(bf16[4096,768]{1,0:T(8,128)(2,1)} %param.28, bf16[1024,4096]{1,0:T(8,128)(2,1)S(1)} %get-tuple-element.34, f32[4096]{0:T(1024)S(1)} %copy-done.13, f32[1024]{0:T(1024)S(1)} %add_rsqrt_fusion), kind=kOutput, calls=%fused_computation.24 | convolution fusion | flops 6459228160 | bytes 17846272 | tf_op jit(solution)/shard_map/dot_general | solution.py:194
  312.5 26.4 %convolution_convert_fusion.2 = bf16[1024,4096]{1,0:T(8,128)(2,1)} fusion(bf16[768,4096]{1,0:T(8,128)(2,1)} %param.29, f32[1024,768]{1,0:T(8,128)} %fusion.11, bf16[4096,768]{1,0:T(8,128)(2,1)} %param.27, bf16[1024,4096]{1,0:T(8,128)(2,1)} %copy-done.3, f32[4096]{0:T(1024)S(1)} %copy-done.13, f32[1024]{0:T(1024)S(1)} %add_rsqrt_fusion), kind=kOutput, calls=%fused_computation.17 | convolution fusion | flops 12910592000 | bytes 32526336 | tf_op jit(solution)/shard_map/dot_general | solution.py:197
  338.9 84.2 %reduce-scatter.2.cloned.1.call-done = bf16[64,4096]{1,0:T(8,128)(2,1)} async-done(((bf16[1024,4096]{1,0:T(8,128)(2,1)}), bf16[64,4096]{1,0:T(8,128)(2,1)}) %reduce-scatter.2.cloned.1.call-update) | async-done | bytes 524304 | tf_op jit(solution)/shard_map/reduce_scatter | solution.py:196
  423.2 2.1 fusion.52
  (67 shorter events, 2.1 us)
Async XLA Ops:
  6.5 136.8 %copy-start = (bf16[256,4096]{1,0:T(8,128)(2,1)S(1)}, bf16[256,4096]{1,0:T(8,128)(2,1)}, u32[]{:S(2)}) copy-start(bf16[256,4096]{1,0:T(8,128)(2,1)} %param.25) | copy-start | bytes 6291460
  6.5 28.3 %copy-start.11 = (s32[1,1024]{1,0:T(1,128)S(1)}, s32[1,1024]{1,0:T(1,128)}, u32[]{:S(2)}) copy-start(s32[1,1024]{1,0:T(1,128)} %param.20) | copy-start | bytes 12292
  6.5 23.6 %copy-start.12 = (f32[4096]{0:T(1024)S(1)}, f32[4096]{0:T(1024)}, u32[]{:S(2)}) copy-start(f32[4096]{0:T(1024)} %param.21) | copy-start | bytes 49156
  13.7 13.0 %all-to-all-start = ((bf16[8,2,8320]{2,1,0:T(2,128)(2,1)}), bf16[8,2,8320]{2,1,0:T(2,128)(2,1)S(1)}, u32[]{:S(2)}, u32[]{:S(2)}) async-start(bf16[8,2,8320]{2,1,0:T(2,128)(2,1)} %all_to_all.8), calls=%async_computation | async-start | bytes 532480 | tf_op jit(solution)/shard_map/all_to_all | solution.py:111
  19.1 81.3 %all-gather.3.cloned.1.call-start = ((), (), s32[]{:S(2)}) async-start(), calls=%async_computation.4 | async-start | bytes 8912896 | tf_op jit(solution)/shard_map/all_gather | solution.py:132
  30.1 260.0 %all-reduce.3.cloned.1.call-start = ((), (), s32[]{:S(2)}) async-start(), calls=%async_computation.2 | async-start | bytes 16777216 | tf_op jit(solution)/shard_map/psum | solution.py:189
  105.5 9.0 %copy-start.7 = (bf16[4096,64]{0,1:T(8,128)(2,1)S(1)}, bf16[4096,64]{0,1:T(8,128)(2,1)}, u32[]{:S(2)}) copy-start(bf16[4096,64]{0,1:T(8,128)(2,1)} %param.23) | copy-start | bytes 1572868
  114.4 6.2 %copy-start.2 = (bf16[16,1024,256]{2,1,0:T(8,128)(2,1)S(1)}, bf16[16,1024,256]{2,1,0:T(8,128)(2,1)}, u32[]{:S(2)}) copy-start(bf16[16,1024,256]{2,1,0:T(8,128)(2,1)} %fusion.4) | copy-start | bytes 25165828
  114.4 6.3 %copy-start.8 = (bf16[4096,64]{0,1:T(8,128)(2,1)S(1)}, bf16[4096,64]{0,1:T(8,128)(2,1)}, u32[]{:S(2)}) copy-start(bf16[4096,64]{0,1:T(8,128)(2,1)} %param.24) | copy-start | bytes 1572868
  120.6 2.7 copy-start.5
  120.6 2.7 copy-start.6
  120.7 4.6 %copy-start.4 = (bf16[16,256,256]{1,0,2:T(8,128)(2,1)S(1)}, bf16[16,256,256]{1,0,2:T(8,128)(2,1)}, u32[]{:S(2)}) copy-start(bf16[16,256,256]{1,0,2:T(8,128)(2,1)} %copy.68) | copy-start | bytes 6291460
  123.5 8.3 %collective-permute-start = (bf16[1024,128]{0,1:T(8,128)(2,1)S(1)}, bf16[1024,128]{0,1:T(8,128)(2,1)S(1)}, u32[]{:S(2)}, u32[]{:S(2)}) collective-permute-start(bf16[1024,128]{0,1:T(8,128)(2,1)S(1)} %pad_maximum_fusion.2), channel_id=1, source_target_pairs={{0,1},{1,0},{2,3},{3,2},{4,5},{5,4},{6,7},{7,6},{8,9},{9,8},{10,11... | collective-permute-start | bytes 786440 | tf_op jit(solution)/shard_map/ppermute | solution.py:22
  128.0 4.0 copy-start.10
  129.6 5.6 %copy-start.9 = (bf16[1024,2,128]{0,2,1:T(8,128)(2,1)S(1)}, bf16[1024,2,128]{0,2,1:T(8,128)(2,1)}, u32[]{:S(2)}) copy-start(bf16[1024,2,128]{0,2,1:T(8,128)(2,1)} %fusion.45) | copy-start | bytes 1572868
  140.0 2.8 copy-start.14
  148.9 274.2 %reduce-scatter.2.cloned.1.call-start = ((), (), s32[]{:S(2)}) async-start(), calls=%async_computation.3 | async-start | bytes 8912896 | tf_op jit(solution)/shard_map/reduce_scatter | solution.py:196
  156.7 144.4 %copy-start.13 = (f32[4096]{0:T(1024)S(1)}, f32[4096]{0:T(1024)}, u32[]{:S(2)}) copy-start(f32[4096]{0:T(1024)} %param.26) | copy-start | bytes 49156
  298.0 3.2 copy-start.3
  312.5 112.8 %copy-start.1 = (bf16[256,4096]{1,0:T(8,128)(2,1)S(1)}, bf16[256,4096]{1,0:T(8,128)(2,1)}, u32[]{:S(2)}) copy-start(bf16[256,4096]{1,0:T(8,128)(2,1)} %param.25) | copy-start | bytes 6291460
Sparse Core Ops, SparseCore 0:
  30.2 70.1 all-gather.2
  149.1 140.9 all-reduce.2
  339.0 84.0 reduce-scatter.1

commit v9 on v6

--- a/solution.py
+++ b/solution.py
@@ -151,7 +151,6 @@
 
     heads_here = w_query.shape[1] // HD
     queries = project(w_query).reshape(seq_len, heads_here, HD)
-    queries = rotate_pairs(queries, positions, 0).astype(jnp.bfloat16)
     kv_cols = w_key.shape[1]
     upper_half = ts_index % 2 == 1
     key_half = project(w_key).reshape(
@@ -162,6 +161,8 @@
     value_half = project(w_value).astype(jnp.bfloat16)
     own_pair = jnp.concatenate([key_half, value_half], axis=1)
     partner = partner_2(own_pair, "ts", 0)
+    queries = lax.optimization_barrier((own_pair, queries))[1]
+    queries = rotate_pairs(queries, positions, 0).astype(jnp.bfloat16)
     lower_half = jnp.where(upper_half, partner, own_pair)
     higher = jnp.where(upper_half, own_pair, partner)
     keys_full = jnp.concatenate([lower_half[:, :kv_cols], higher[:, :kv_cols]], axis=1)

time: 426 us -> 423 us (level)
    ppermute x1, waiting for transfers between devices: 5.18 us -> 0.82 us  [partner_2(): return lax.ppermute(block, axis, route)]
  transfers between devices with their start and end apart: 5 -> 5, of which waited for: 5 -> 5; matrix products, arithmetic and copies ran while one was open for 6% -> 7% of each run, Pallas kernels for 0% -> 0%
where the time goes in v9:
time: 423 us; the launch traced here: 422 us
  waiting for transfers between devices  281 us (66%)
  matrix products  66.9 us (16%)
  other arithmetic  28 us (7%)
  local copies, waits for them, and re-layouts  25.3 us (6%)
  between operations  13.5 us (3%)
  starting transfers between devices  7.24 us (2%)
    psum x1, waiting for transfers between devices, shards(): lax.psum(partial_rows.astype(jnp.bfloat16), 'ts').astype(jnp.float32)  133 us
    reduce_scatter x1, waiting for transfers between devices, shards(): lax.psum_scatter(jnp.dot(hidden, w_down, preferred_element_type=jnp.float...  84.1 us
    all_gather x1, waiting for transfers between devices, shards(): stacked = lax.all_gather(own_part, 'ts', axis=0, tiled=False)  57.4 us
    dot_general x1, matrix products, shards(): jnp.dot(hidden, w_down, preferred_element_type=jnp.float32)  26.4 us
    dot_general x1, matrix products, shards(): up_proj = jnp.dot(normed_mlp, w_up, preferred_element_type=jnp.float32)  11.3 us
    dot_general x3, matrix products, project(): jnp.einsum('srk,skn->rn', normed, weight.reshape(ts_count, part_width, we...  9.95 us
  transfers between devices with their start and end apart: 5, of which 5 were waited for; matrix products, arithmetic and copies ran while one was open for 7% of the time, Pallas kernels for 0%

profile of v9, /device:TPU:0, one launch (start us, length us, event | category | flops | bytes accessed | tf_op | source)
XLA Modules:
  0.0 421.9 jit_solution(227193484083050166)
XLA Ops:
  6.5 0.7 compare_reduce_fusion.1
  7.2 0.6 compare_reduce_fusion
  7.8 0.7 and_select_fusion.4
  8.7 0.7 multiply_add_fusion.1
  9.4 1.9 fusion.108
  11.4 1.1 copy.70
  12.8 0.8 all_to_all.8
  13.6 5.4 %all-to-all-start = ((bf16[8,2,8320]{2,1,0:T(2,128)(2,1)}), bf16[8,2,8320]{2,1,0:T(2,128)(2,1)S(1)}, u32[]{:S(2)}, u32[]{:S(2)}) async-start(bf16[8,2,8320]{2,1,0:T(2,128)(2,1)} %all_to_all.8), calls=%async_computation | async-start | bytes 532480 | tf_op jit(solution)/shard_map/all_to_all | solution.py:111
  19.0 0.8 convert_reduce_fusion
  19.8 0.8 select_reduce_fusion
  20.6 0.7 iota_subtract_fusion
  21.3 5.2 %all-to-all-done = bf16[8,2,8320]{2,1,0:T(2,128)(2,1)S(1)} async-done(((bf16[8,2,8320]{2,1,0:T(2,128)(2,1)}), bf16[8,2,8320]{2,1,0:T(2,128)(2,1)S(1)}, u32[]{:S(2)}, u32[]{:S(2)}) %all-to-all-start) | async-done | bytes 266272 | tf_op jit(solution)/shard_map/all_to_all | solution.py:111
  27.3 2.7 fusion.38
  30.1 4.7 %copy.65 = bf16[16,256,256]{1,0,2:T(8,128)(2,1)} copy(bf16[16,256,256]{2,1,0:T(8,128)(2,1)} %bitcast.128) | data formatting | bytes 4194304 | tf_op jit(solution)/shard_map/reshape | solution.py:148
  34.9 0.9 fusion.50
  35.8 1.3 fusion.21
  37.0 0.5 multiply_sine_fusion.1
  37.7 0.9 reshape.331
  38.6 0.9 broadcast_in_dim_reshape.4
  39.5 1.0 multiply_cosine_fusion
  40.7 0.4 mul.191
  41.0 1.0 copy.53
  42.2 0.4 reshape.334
  42.9 57.4 %all-gather.3.cloned.1.call-done = bf16[16384,256]{1,0:T(8,128)(2,1)} async-done(((bf16[1024,256]{1,0:T(8,128)(2,1)}), bf16[16384,256]{1,0:T(8,128)(2,1)}) %all-gather.3.cloned.1.call-update) | async-done | bytes 8388624 | tf_op jit(solution)/shard_map/all_gather | solution.py:132
  100.3 5.2 %fusion.2 = f32[1024]{0:T(1024)S(1)} fusion(bf16[16,1024,256]{2,1,0:T(8,128)(2,1)} %bitcast.123), kind=kLoop, calls=%fused_computation.6 | loop fusion | flops 12581888 | bytes 8392704 | tf_op jit(solution)/shard_map/reduce_sum | solution.py:138
  105.5 0.5 copy-done.2
  106.1 3.9 fusion.55
  110.3 2.8 fusion.42
  113.1 1.7 collective-permute-start
  114.9 3.2 fusion.30
  118.7 0.3 copy-done.5
  119.1 1.5 fusion.45
  120.6 0.8 collective-permute-done
  121.6 0.8 fusion.133
  122.3 3.3 fusion.145
  125.6 4.7 %fusion.136 = (f32[2,512]{1,0:T(2,128)S(1)}, f32[2,512,1024]{1,2,0:T(8,128)}) fusion(pred[512,1024]{0,1:T(8,128)(4,1)S(1)} %copy-done.8, bf16[1024,2,128]{2,0,1:T(8,128)(2,1)S(1)} %copy-done.9, bf16[1024,64]{0,1:T(8,128)(2,1)} %get-tuple-element.63, bf16[1024,64]{0,1:T(8,128)(2,1)} %get-tuple-element.42), kind=kOutput, calls=%fused_computation.172 | convolution fusion | flops 273155072 | bytes 5246976 | tf_op jit(solution)/shard_map/sub | solution.py:54
  130.3 2.1 convolution_convert_fusion.4
  132.4 0.7 copy-done.16
  133.2 0.5 fusion.41
  133.7 5.6 %convolution_convert_fusion.3 = bf16[1024,4096]{1,0:T(8,128)(2,1)} fusion(bf16[256,4096]{1,0:T(8,128)(2,1)S(1)} %copy-done, bf16[512,256]{0,1:T(8,128)(2,1)S(1)} %bitcast.132, bf16[512,256]{0,1:T(8,128)(2,1)S(1)} %bitcast.131), kind=kOutput, calls=%fused_computation.18 | convolution fusion | flops 2152726528 | bytes 11010048 | tf_op jit(solution)/shard_map/dot_general | solution.py:188
  139.3 7.8 %copy.69 = bf16[16,128,8,256]{3,2,0,1:T(8,128)(2,1)} copy(bf16[16,128,8,256]{3,2,1,0:T(8,128)(2,1)} %bitcast.124) | data formatting | bytes 16777216 | tf_op jit(solution)/shard_map/reshape | solution.py:135
  147.1 133.3 %all-reduce.3.cloned.1.call-done = bf16[1024,4096]{1,0:T(8,128)(2,1)} async-done(((bf16[1024,4096]{1,0:T(8,128)(2,1)}), bf16[1024,4096]{1,0:T(8,128)(2,1)}) %all-reduce.3.cloned.1.call-update) | async-done | bytes 8388624 | tf_op jit(solution)/shard_map/psum | solution.py:189
  280.4 7.8 %fusion.5 = (f32[1024]{0:T(1024)S(1)}, bf16[1024,4096]{1,0:T(8,128)(2,1)S(1)}) fusion(bf16[1024,4096]{1,0:T(8,128)(2,1)} %all-reduce.3.cloned.1.call-done, bf16[1024,4096]{1,0:T(8,128)(2,1)} %bitcast.125), kind=kLoop, calls=%fused_computation.9 | loop fusion | flops 29359104 | bytes 25169920 | tf_op jit(solution)/shard_map/reduce_sum | solution.py:27
  288.2 3.2 copy-done.3
  291.4 11.3 %fusion.11 = f32[1024,768]{1,0:T(8,128)} fusion(bf16[4096,768]{1,0:T(8,128)(2,1)} %param.28, bf16[1024,4096]{1,0:T(8,128)(2,1)S(1)} %get-tuple-element.34, f32[4096]{0:T(1024)S(1)} %copy-done.15, f32[1024]{0:T(1024)S(1)} %add_rsqrt_fusion), kind=kOutput, calls=%fused_computation.24 | convolution fusion | flops 6459228160 | bytes 17846272 | tf_op jit(solution)/shard_map/dot_general | solution.py:194
  302.7 26.4 %convolution_convert_fusion.2 = bf16[1024,4096]{1,0:T(8,128)(2,1)} fusion(bf16[768,4096]{1,0:T(8,128)(2,1)} %param.29, f32[1024,768]{1,0:T(8,128)} %fusion.11, bf16[4096,768]{1,0:T(8,128)(2,1)} %param.27, bf16[1024,4096]{1,0:T(8,128)(2,1)} %copy-done.3, f32[4096]{0:T(1024)S(1)} %copy-done.15, f32[1024]{0:T(1024)S(1)} %add_rsqrt_fusion), kind=kOutput, calls=%fused_computation.17 | convolution fusion | flops 12910592000 | bytes 32526336 | tf_op jit(solution)/shard_map/dot_general | solution.py:197
  329.1 84.1 %reduce-scatter.2.cloned.1.call-done = bf16[64,4096]{1,0:T(8,128)(2,1)} async-done(((bf16[1024,4096]{1,0:T(8,128)(2,1)}), bf16[64,4096]{1,0:T(8,128)(2,1)}) %reduce-scatter.2.cloned.1.call-update) | async-done | bytes 524304 | tf_op jit(solution)/shard_map/reduce_scatter | solution.py:196
  413.3 2.1 fusion.52
  (72 shorter events, 3.3 us)
Async XLA Ops:
  6.5 127.1 %copy-start = (bf16[256,4096]{1,0:T(8,128)(2,1)S(1)}, bf16[256,4096]{1,0:T(8,128)(2,1)}, u32[]{:S(2)}) copy-start(bf16[256,4096]{1,0:T(8,128)(2,1)} %param.25) | copy-start | bytes 6291460
  6.5 28.3 %copy-start.12 = (s32[1,1024]{1,0:T(1,128)S(1)}, s32[1,1024]{1,0:T(1,128)}, u32[]{:S(2)}) copy-start(s32[1,1024]{1,0:T(1,128)} %param.20) | copy-start | bytes 12292
  6.5 23.5 %copy-start.13 = (f32[4096]{0:T(1024)S(1)}, f32[4096]{0:T(1024)}, u32[]{:S(2)}) copy-start(f32[4096]{0:T(1024)} %param.21) | copy-start | bytes 49156
  13.6 13.0 %all-to-all-start = ((bf16[8,2,8320]{2,1,0:T(2,128)(2,1)}), bf16[8,2,8320]{2,1,0:T(2,128)(2,1)S(1)}, u32[]{:S(2)}, u32[]{:S(2)}) async-start(bf16[8,2,8320]{2,1,0:T(2,128)(2,1)} %all_to_all.8), calls=%async_computation | async-start | bytes 532480 | tf_op jit(solution)/shard_map/all_to_all | solution.py:111
  19.0 81.3 %all-gather.3.cloned.1.call-start = ((), (), s32[]{:S(2)}) async-start(), calls=%async_computation.4 | async-start | bytes 8912896 | tf_op jit(solution)/shard_map/all_gather | solution.py:132
  30.0 250.4 %all-reduce.3.cloned.1.call-start = ((), (), s32[]{:S(2)}) async-start(), calls=%async_computation.2 | async-start | bytes 16777216 | tf_op jit(solution)/shard_map/psum | solution.py:189
  100.3 5.8 %copy-start.2 = (bf16[16384,256]{1,0:T(8,128)(2,1)S(1)}, bf16[16384,256]{1,0:T(8,128)(2,1)}, u32[]{:S(2)}) copy-start(bf16[16384,256]{1,0:T(8,128)(2,1)} %all-gather.3.cloned.1.call-done) | copy-start | bytes 25165828
  106.1 4.0 copy-start.6
  106.1 4.0 copy-start.7
  106.1 4.2 copy-start.14
  110.3 4.6 %copy-start.4 = (bf16[16,256,256]{1,0,2:T(8,128)(2,1)S(1)}, bf16[16,256,256]{1,0,2:T(8,128)(2,1)}, u32[]{:S(2)}) copy-start(bf16[16,256,256]{1,0,2:T(8,128)(2,1)} %copy.65) | copy-start | bytes 6291460
  113.1 8.3 %collective-permute-start = (bf16[1024,128]{0,1:T(8,128)(2,1)S(1)}, bf16[1024,128]{0,1:T(8,128)(2,1)S(1)}, u32[]{:S(2)}, u32[]{:S(2)}) collective-permute-start(bf16[1024,128]{0,1:T(8,128)(2,1)S(1)} %pad_maximum_fusion.2), channel_id=1, source_target_pairs={{0,1},{1,0},{2,3},{3,2},{4,5},{5,4},{6,7},{7,6},{8,9},{9,8},{10,11... | collective-permute-start | bytes 786440 | tf_op jit(solution)/shard_map/ppermute | solution.py:22
  118.0 1.0 copy-start.5
  118.4 4.0 copy-start.10
  119.1 6.6 %copy-start.8 = (pred[512,1024]{0,1:T(8,128)(4,1)S(1)}, pred[512,1024]{0,1:T(8,128)(4,1)}, u32[]{:S(2)}) copy-start(pred[512,1024]{0,1:T(8,128)(4,1)} %fusion.21) | copy-start | bytes 1572868
  120.6 5.0 %copy-start.9 = (bf16[1024,2,128]{2,0,1:T(8,128)(2,1)S(1)}, bf16[1024,2,128]{2,0,1:T(8,128)(2,1)}, u32[]{:S(2)}) copy-start(bf16[1024,2,128]{2,0,1:T(8,128)(2,1)} %fusion.45) | copy-start | bytes 1572868
  125.6 4.7 %copy-start.11 = (bf16[1024,64]{0,1:T(8,128)(2,1)S(1)}, bf16[1024,64]{0,1:T(8,128)(2,1)}, u32[]{:S(2)}) copy-start(bf16[1024,64]{0,1:T(8,128)(2,1)} %get-tuple-element.64) | copy-start | bytes 393220
  130.3 2.8 copy-start.16
  139.3 274.0 %reduce-scatter.2.cloned.1.call-start = ((), (), s32[]{:S(2)}) async-start(), calls=%async_computation.3 | async-start | bytes 8912896 | tf_op jit(solution)/shard_map/reduce_scatter | solution.py:196
  147.1 144.4 %copy-start.15 = (f32[4096]{0:T(1024)S(1)}, f32[4096]{0:T(1024)}, u32[]{:S(2)}) copy-start(f32[4096]{0:T(1024)} %param.26) | copy-start | bytes 49156
  288.2 3.2 copy-start.3
  302.7 112.7 %copy-start.1 = (bf16[256,4096]{1,0:T(8,128)(2,1)S(1)}, bf16[256,4096]{1,0:T(8,128)(2,1)}, u32[]{:S(2)}) copy-start(bf16[256,4096]{1,0:T(8,128)(2,1)} %param.25) | copy-start | bytes 6291460
Sparse Core Ops, SparseCore 0:
  30.1 70.1 all-gather.2
  139.4 140.9 all-reduce.2
  329.2 83.9 reduce-scatter.1

commit v10 on v9

--- a/solution.py
+++ b/solution.py
@@ -108,7 +108,15 @@
     outgoing = jnp.dot(
         sending.astype(jnp.bfloat16), payload, preferred_element_type=jnp.float32
     ).astype(jnp.bfloat16)
-    arrived_all = lax.all_to_all(outgoing, "dp", 0, 0, tiled=True)
+    dp_count = lax.axis_size("dp")
+    pieces = [lax.dynamic_slice_in_dim(outgoing, group_index * per_destination, per_destination, 0)]
+    for step in range(1, dp_count):
+        block = lax.dynamic_slice_in_dim(
+            outgoing, (group_index + step) % dp_count * per_destination, per_destination, 0
+        )
+        route = [(low, (low + step) % dp_count) for low in range(dp_count)]
+        pieces.append(lax.ppermute(block, "dp", route))
+    arrived_all = jnp.concatenate(pieces, axis=0)
     arrived = arrived_all[:, : bridge_len * part_width]
     arrived_slots = (
         arrived_all[:, -128].astype(jnp.int32) * 128 + arrived_all[:, -127].astype(jnp.int32)

time: 423 us -> 431 us (1.019)
    ppermute x0 -> x7, starting transfers between devices: none -> 9.03 us  [shards(): pieces.append(lax.ppermute(block, 'dp', route))]
    all_to_all x1 -> x0, starting transfers between devices: 5.4 us -> none  [shards(): arrived_all = lax.all_to_all(outgoing, 'dp', 0, 0, tiled=True)]
    all_to_all x1 -> x0, waiting for transfers between devices: 5.23 us -> none  [shards(): arrived_all = lax.all_to_all(outgoing, 'dp', 0, 0, tiled=True)]
  transfers between devices with their start and end apart: 5 -> 11, of which waited for: 5 -> 6; matrix products, arithmetic and copies ran while one was open for 7% -> 7% of each run, Pallas kernels for 0% -> 0%
where the time goes in v10:
time: 431 us; the launch traced here: 427 us
  waiting for transfers between devices  280 us (65%)
  matrix products  66.9 us (16%)
  other arithmetic  28.1 us (7%)
  local copies, waits for them, and re-layouts  26.2 us (6%)
  between operations  14 us (3%)
  starting transfers between devices  11.1 us (3%)
    psum x1, waiting for transfers between devices, shards(): lax.psum(partial_rows.astype(jnp.bfloat16), 'ts').astype(jnp.float32)  133 us
    reduce_scatter x1, waiting for transfers between devices, shards(): lax.psum_scatter(jnp.dot(hidden, w_down, preferred_element_type=jnp.float...  84.1 us
    all_gather x1, waiting for transfers between devices, shards(): stacked = lax.all_gather(own_part, 'ts', axis=0, tiled=False)  58.5 us
    dot_general x1, matrix products, shards(): jnp.dot(hidden, w_down, preferred_element_type=jnp.float32)  26.4 us
    dot_general x1, matrix products, shards(): up_proj = jnp.dot(normed_mlp, w_up, preferred_element_type=jnp.float32)  11.3 us
    dot_general x3, matrix products, project(): jnp.einsum('srk,skn->rn', normed, weight.reshape(ts_count, part_width, we...  9.95 us
    ppermute x7, starting transfers between devices, shards(): pieces.append(lax.ppermute(block, 'dp', route))  9.03 us
  transfers between devices with their start and end apart: 11, of which 6 were waited for; matrix products, arithmetic and copies ran while one was open for 7% of the time, Pallas kernels for 0%

profile of v10, /device:TPU:0, one launch (start us, length us, event | category | flops | bytes accessed | tf_op | source)
XLA Modules:
  0.0 426.8 jit_solution(634958916180569106)
XLA Ops:
  6.5 0.6 compare_reduce_fusion.1
  7.2 0.6 compare_reduce_fusion
  7.8 0.7 and_select_fusion.4
  8.7 0.7 multiply_add_fusion.1
  9.3 1.9 fusion.108
  11.3 1.1 copy.57
  13.0 3.6 collective-permute-start.6
  16.6 0.6 collective-permute-start.5
  17.2 3.3 collective-permute-start.3
  20.5 0.8 convert_reduce_fusion
  21.3 0.8 select_reduce_fusion
  22.1 0.7 iota_subtract_fusion
  22.9 1.4 collective-permute-start
  24.3 1.1 collective-permute-done.2
  25.5 2.6 collective-permute-done.1
  28.1 1.6 concatenate.49
  30.3 2.7 fusion.38
  33.3 4.6 %copy.52 = bf16[16,256,256]{1,0,2:T(8,128)(2,1)} copy(bf16[16,256,256]{2,1,0:T(8,128)(2,1)} %bitcast.128) | data formatting | bytes 4194304 | tf_op jit(solution)/shard_map/reshape | solution.py:156
  38.0 0.9 fusion.50
  38.9 1.3 fusion.21
  40.2 0.5 multiply_sine_fusion.1
  40.8 0.9 reshape.329
  41.8 0.9 broadcast_in_dim_reshape.4
  42.6 1.0 multiply_cosine_fusion
  44.2 1.0 copy.40
  46.1 58.5 %all-gather.3.cloned.1.call-done = bf16[16384,256]{1,0:T(8,128)(2,1)} async-done(((bf16[1024,256]{1,0:T(8,128)(2,1)}), bf16[16384,256]{1,0:T(8,128)(2,1)}) %all-gather.3.cloned.1.call-update) | async-done | bytes 8388624 | tf_op jit(solution)/shard_map/all_gather | solution.py:140
  104.5 5.2 %fusion.2 = f32[1024]{0:T(1024)S(1)} fusion(bf16[16,1024,256]{2,1,0:T(8,128)(2,1)} %bitcast.123), kind=kLoop, calls=%fused_computation.6 | loop fusion | flops 12581888 | bytes 8392704 | tf_op jit(solution)/shard_map/reduce_sum | solution.py:146
  109.8 0.5 copy-done.2
  110.3 3.9 fusion.55
  114.5 2.8 fusion.42
  117.4 1.8 collective-permute-start.7
  119.1 3.2 fusion.30
  123.4 1.5 fusion.45
  124.9 0.8 collective-permute-done.7
  125.8 0.8 fusion.133
  126.6 3.3 fusion.145
  129.9 4.7 %fusion.136 = (f32[2,512]{1,0:T(2,128)S(1)}, f32[2,512,1024]{1,2,0:T(8,128)}) fusion(pred[512,1024]{0,1:T(8,128)(4,1)S(1)} %copy-done.8, bf16[1024,2,128]{2,0,1:T(8,128)(2,1)S(1)} %copy-done.9, bf16[1024,64]{0,1:T(8,128)(2,1)} %get-tuple-element.71, bf16[1024,64]{0,1:T(8,128)(2,1)} %get-tuple-element.50), kind=kOutput, calls=%fused_computation.180 | convolution fusion | flops 273155072 | bytes 5246976 | tf_op jit(solution)/shard_map/sub | solution.py:54
  134.6 2.1 convolution_convert_fusion.4
  136.7 0.8 copy-done.16
  137.9 5.6 %convolution_convert_fusion.3 = bf16[1024,4096]{1,0:T(8,128)(2,1)} fusion(bf16[256,4096]{1,0:T(8,128)(2,1)S(1)} %copy-done, bf16[512,256]{0,1:T(8,128)(2,1)S(1)} %bitcast.132, bf16[512,256]{0,1:T(8,128)(2,1)S(1)} %bitcast.131), kind=kOutput, calls=%fused_computation.18 | convolution fusion | flops 2152726528 | bytes 11010048 | tf_op jit(solution)/shard_map/dot_general | solution.py:196
  143.6 7.8 %copy.56 = bf16[16,128,8,256]{3,2,0,1:T(8,128)(2,1)} copy(bf16[16,128,8,256]{3,2,1,0:T(8,128)(2,1)} %bitcast.124) | data formatting | bytes 16777216 | tf_op jit(solution)/shard_map/reshape | solution.py:143
  151.4 133.3 %all-reduce.3.cloned.1.call-done = bf16[1024,4096]{1,0:T(8,128)(2,1)} async-done(((bf16[1024,4096]{1,0:T(8,128)(2,1)}), bf16[1024,4096]{1,0:T(8,128)(2,1)}) %all-reduce.3.cloned.1.call-update) | async-done | bytes 8388624 | tf_op jit(solution)/shard_map/psum | solution.py:197
  284.7 8.1 %fusion.5 = (f32[1024]{0:T(1024)S(1)}, bf16[1024,4096]{1,0:T(8,128)(2,1)S(1)}) fusion(bf16[1024,4096]{1,0:T(8,128)(2,1)} %all-reduce.3.cloned.1.call-done, bf16[1024,4096]{1,0:T(8,128)(2,1)} %bitcast.125), kind=kLoop, calls=%fused_computation.9 | loop fusion | flops 29359104 | bytes 25169920 | tf_op jit(solution)/shard_map/reduce_sum | solution.py:27
  292.8 3.2 copy-done.3
  296.0 11.3 %fusion.11 = f32[1024,768]{1,0:T(8,128)} fusion(bf16[4096,768]{1,0:T(8,128)(2,1)} %param.28, bf16[1024,4096]{1,0:T(8,128)(2,1)S(1)} %get-tuple-element.34, f32[4096]{0:T(1024)S(1)} %copy-done.15, f32[1024]{0:T(1024)S(1)} %add_rsqrt_fusion), kind=kOutput, calls=%fused_computation.24 | convolution fusion | flops 6459228160 | bytes 17846272 | tf_op jit(solution)/shard_map/dot_general | solution.py:202
  307.3 26.4 %convolution_convert_fusion.2 = bf16[1024,4096]{1,0:T(8,128)(2,1)} fusion(bf16[768,4096]{1,0:T(8,128)(2,1)} %param.29, f32[1024,768]{1,0:T(8,128)} %fusion.11, bf16[4096,768]{1,0:T(8,128)(2,1)} %param.27, bf16[1024,4096]{1,0:T(8,128)(2,1)} %copy-done.3, f32[4096]{0:T(1024)S(1)} %copy-done.15, f32[1024]{0:T(1024)S(1)} %add_rsqrt_fusion), kind=kOutput, calls=%fused_computation.17 | convolution fusion | flops 12910592000 | bytes 32526336 | tf_op jit(solution)/shard_map/dot_general | solution.py:205
  333.7 84.1 %reduce-scatter.2.cloned.1.call-done = bf16[64,4096]{1,0:T(8,128)(2,1)} async-done(((bf16[1024,4096]{1,0:T(8,128)(2,1)}), bf16[64,4096]{1,0:T(8,128)(2,1)}) %reduce-scatter.2.cloned.1.call-update) | async-done | bytes 524304 | tf_op jit(solution)/shard_map/reduce_scatter | solution.py:204
  417.7 2.1 fusion.52
  (84 shorter events, 5.3 us)
Async XLA Ops:
  6.5 131.4 %copy-start = (bf16[256,4096]{1,0:T(8,128)(2,1)S(1)}, bf16[256,4096]{1,0:T(8,128)(2,1)}, u32[]{:S(2)}) copy-start(bf16[256,4096]{1,0:T(8,128)(2,1)} %param.25) | copy-start | bytes 6291460
  6.5 31.5 %copy-start.12 = (s32[1,1024]{1,0:T(1,128)S(1)}, s32[1,1024]{1,0:T(1,128)}, u32[]{:S(2)}) copy-start(s32[1,1024]{1,0:T(1,128)} %param.20) | copy-start | bytes 12292
  6.5 26.7 %copy-start.13 = (f32[4096]{0:T(1024)S(1)}, f32[4096]{0:T(1024)}, u32[]{:S(2)}) copy-start(f32[4096]{0:T(1024)} %param.21) | copy-start | bytes 49156
  6.5 98.0 %all-gather.3.cloned.1.call-start = ((), (), s32[]{:S(2)}) async-start(), calls=%async_computation.3 | async-start | bytes 8912896 | tf_op jit(solution)/shard_map/all_gather | solution.py:140
  13.0 9.8 %collective-permute-start.6 = (bf16[2,8320]{1,0:T(2,128)(2,1)S(1)}, bf16[2,8320]{1,0:T(2,128)(2,1)S(1)}, u32[]{:S(2)}, u32[]{:S(2)}) collective-permute-start(bf16[2,8320]{1,0:T(2,128)(2,1)S(1)} %get-tuple-element.41), channel_id=1, source_target_pairs={{0,112},{16,0},{32,16},{48,32},{64,48},{80,64},{96,80},{112,96},{1... | collective-permute-start | bytes 99848 | tf_op jit(solution)/shard_map/ppermute | solution.py:118
  16.6 6.3 %collective-permute-start.5 = (bf16[2,8320]{1,0:T(2,128)(2,1)S(1)}, bf16[2,8320]{1,0:T(2,128)(2,1)S(1)}, u32[]{:S(2)}, u32[]{:S(2)}) collective-permute-start(bf16[2,8320]{1,0:T(2,128)(2,1)S(1)} %get-tuple-element.42), channel_id=1, source_target_pairs={{0,96},{16,112},{32,0},{48,16},{64,32},{80,48},{96,64},{112,80},{1... | collective-permute-start | bytes 99848 | tf_op jit(solution)/shard_map/ppermute | solution.py:118
  17.2 7.1 %collective-permute-start.4 = (bf16[2,8320]{1,0:T(2,128)(2,1)S(1)}, bf16[2,8320]{1,0:T(2,128)(2,1)S(1)}, u32[]{:S(2)}, u32[]{:S(2)}) collective-permute-start(bf16[2,8320]{1,0:T(2,128)(2,1)S(1)} %get-tuple-element.43), channel_id=1, source_target_pairs={{0,80},{16,96},{32,112},{48,0},{64,16},{80,32},{96,48},{112,64},{1... | collective-permute-start | bytes 99848 | tf_op jit(solution)/shard_map/ppermute | solution.py:118
  17.2 7.1 %collective-permute-start.3 = (bf16[2,8320]{1,0:T(2,128)(2,1)S(1)}, bf16[2,8320]{1,0:T(2,128)(2,1)S(1)}, u32[]{:S(2)}, u32[]{:S(2)}) collective-permute-start(bf16[2,8320]{1,0:T(2,128)(2,1)S(1)} %get-tuple-element.44), channel_id=1, source_target_pairs={{0,64},{16,80},{32,96},{48,112},{64,0},{80,16},{96,32},{112,48},{1... | collective-permute-start | bytes 99848 | tf_op jit(solution)/shard_map/ppermute | solution.py:118
  20.5 5.0 %collective-permute-start.2 = (bf16[2,8320]{1,0:T(2,128)(2,1)S(1)}, bf16[2,8320]{1,0:T(2,128)(2,1)S(1)}, u32[]{:S(2)}, u32[]{:S(2)}) collective-permute-start(bf16[2,8320]{1,0:T(2,128)(2,1)S(1)} %get-tuple-element.45), channel_id=1, source_target_pairs={{0,48},{16,64},{32,80},{48,96},{64,112},{80,0},{96,16},{112,32},{1... | collective-permute-start | bytes 99848 | tf_op jit(solution)/shard_map/ppermute | solution.py:118
  22.8 5.3 %collective-permute-start.1 = (bf16[2,8320]{1,0:T(2,128)(2,1)S(1)}, bf16[2,8320]{1,0:T(2,128)(2,1)S(1)}, u32[]{:S(2)}, u32[]{:S(2)}) collective-permute-start(bf16[2,8320]{1,0:T(2,128)(2,1)S(1)} %get-tuple-element.46), channel_id=1, source_target_pairs={{0,32},{16,48},{32,64},{48,80},{64,96},{80,112},{96,0},{112,16},{1... | collective-permute-start | bytes 99848 | tf_op jit(solution)/shard_map/ppermute | solution.py:118
  22.9 5.2 %collective-permute-start = (bf16[2,8320]{1,0:T(2,128)(2,1)S(1)}, bf16[2,8320]{1,0:T(2,128)(2,1)S(1)}, u32[]{:S(2)}, u32[]{:S(2)}) collective-permute-start(bf16[2,8320]{1,0:T(2,128)(2,1)S(1)} %get-tuple-element.47), channel_id=1, source_target_pairs={{0,16},{16,32},{32,48},{48,64},{64,80},{80,96},{96,112},{112,0},{1... | collective-permute-start | bytes 99848 | tf_op jit(solution)/shard_map/ppermute | solution.py:118
  33.0 251.7 %all-reduce.3.cloned.1.call-start = ((), (), s32[]{:S(2)}) async-start(), calls=%async_computation.1 | async-start | bytes 16777216 | tf_op jit(solution)/shard_map/psum | solution.py:197
  104.5 5.8 %copy-start.2 = (bf16[16384,256]{1,0:T(8,128)(2,1)S(1)}, bf16[16384,256]{1,0:T(8,128)(2,1)}, u32[]{:S(2)}) copy-start(bf16[16384,256]{1,0:T(8,128)(2,1)} %all-gather.3.cloned.1.call-done) | copy-start | bytes 25165828
  110.3 4.0 copy-start.6
  110.3 4.0 copy-start.7
  110.3 4.2 copy-start.14
  114.5 4.6 %copy-start.4 = (bf16[16,256,256]{1,0,2:T(8,128)(2,1)S(1)}, bf16[16,256,256]{1,0,2:T(8,128)(2,1)}, u32[]{:S(2)}) copy-start(bf16[16,256,256]{1,0,2:T(8,128)(2,1)} %copy.52) | copy-start | bytes 6291460
  117.4 8.3 %collective-permute-start.7 = (bf16[1024,128]{0,1:T(8,128)(2,1)S(1)}, bf16[1024,128]{0,1:T(8,128)(2,1)S(1)}, u32[]{:S(2)}, u32[]{:S(2)}) collective-permute-start(bf16[1024,128]{0,1:T(8,128)(2,1)S(1)} %pad_maximum_fusion.2), channel_id=1, source_target_pairs={{0,1},{1,0},{2,3},{3,2},{4,5},{5,4},{6,7},{7,6},{8,9},{9,8},{10,11... | collective-permute-start | bytes 786440 | tf_op jit(solution)/shard_map/ppermute | solution.py:22
  122.3 1.0 copy-start.5
  122.7 3.9 copy-start.10
  123.4 6.5 %copy-start.8 = (pred[512,1024]{0,1:T(8,128)(4,1)S(1)}, pred[512,1024]{0,1:T(8,128)(4,1)}, u32[]{:S(2)}) copy-start(pred[512,1024]{0,1:T(8,128)(4,1)} %fusion.21) | copy-start | bytes 1572868
  124.9 5.0 %copy-start.9 = (bf16[1024,2,128]{2,0,1:T(8,128)(2,1)S(1)}, bf16[1024,2,128]{2,0,1:T(8,128)(2,1)}, u32[]{:S(2)}) copy-start(bf16[1024,2,128]{2,0,1:T(8,128)(2,1)} %fusion.45) | copy-start | bytes 1572868
  129.9 4.7 %copy-start.11 = (bf16[1024,64]{0,1:T(8,128)(2,1)S(1)}, bf16[1024,64]{0,1:T(8,128)(2,1)}, u32[]{:S(2)}) copy-start(bf16[1024,64]{0,1:T(8,128)(2,1)} %get-tuple-element.72) | copy-start | bytes 393220
  134.6 2.8 copy-start.16
  143.5 274.2 %reduce-scatter.2.cloned.1.call-start = ((), (), s32[]{:S(2)}) async-start(), calls=%async_computation.2 | async-start | bytes 8912896 | tf_op jit(solution)/shard_map/reduce_scatter | solution.py:204
  151.4 144.6 %copy-start.15 = (f32[4096]{0:T(1024)S(1)}, f32[4096]{0:T(1024)}, u32[]{:S(2)}) copy-start(f32[4096]{0:T(1024)} %param.26) | copy-start | bytes 49156
  292.7 3.2 copy-start.3
  307.3 112.6 %copy-start.1 = (bf16[256,4096]{1,0:T(8,128)(2,1)S(1)}, bf16[256,4096]{1,0:T(8,128)(2,1)}, u32[]{:S(2)}) copy-start(bf16[256,4096]{1,0:T(8,128)(2,1)} %param.25) | copy-start | bytes 6291460
Sparse Core Ops, SparseCore 0:
  33.1 71.3 all-gather.2
  143.7 140.9 all-reduce.2
  333.8 83.8 reduce-scatter.1
